TPU v7x, 512 devices: a whole 4x8x8 slice. The times are simulated.
512 devices in a mesh: clus: 256 (over z, y, x), samp: 2 (over core).
Axes of the slice: x: 4, y: 8, z: 8, core: 2. Of those that a mesh axis runs over, the one named last changes fastest.
Arguments:
- samples: float32 [262144, 256], P('clus', 'samp'), may hold values from -8 to 8
- sketch: float32 [256, 128], P('samp'), may hold values from -0.375 to 0.375
- leaf_slot: int32 [256, 4], P('clus'), may hold values from 0 to 3, each once within a row
Outputs:
- leaf_basis: float32 [262144, 128], P('clus')
- local_transfer: float32 [768, 256, 128], P('clus')
- top_transfer: float32 [256, 256, 128], P('clus')
- root_factor: float32 [128, 128], replicated
Inputs may be any that keep to these rules, and one draw needn't show every extreme that they name: Each row of leaf_slot names every number from 0 to 3 once.
All inputs are finite; a program needn't handle non-finite values.
Results may differ from a plain program's by a relative error of at most 0.0003.
Values sent between devices are 32-bit elements; how exact they have to be, the bound alone decides.
No kernel may reach another device: no remote copies, remote signals or barrier semaphores. Data moves between devices by JAX's collectives and lax.ppermute only.
A program may use at most 64 MiB of HBM per device.

v0:
```python
import jax
import jax.numpy as jnp
from jax import lax
from jax.sharding import PartitionSpec as P

NS_STEPS = 5


highest = lax.Precision.HIGHEST


def from_partner(block, axis, apart):
    count = lax.axis_size(axis)
    route = []
    for low in range(count):
        high = low | 1 << apart
        if high != low and high < count:
            route += [(low, high), (high, low)]
    return lax.ppermute(block, axis, route)


def factor(stacked):
    gram_matrix = jnp.einsum("mrk,mrl->mkl", stacked, stacked, precision=highest)
    width = gram_matrix.shape[1]
    identity = jnp.eye(width, dtype=jnp.float32)
    scale = jnp.einsum("mkk->m", gram_matrix)[:, None, None] + 1e-06
    start_root = gram_matrix / scale
    start_inverse = jnp.broadcast_to(identity, gram_matrix.shape)

    def newton_step(index, carry):
        root, inverse = carry
        middle = 1.5 * identity - 0.5 * jnp.einsum("mkl,mlj->mkj", inverse, root, precision=highest)
        return (
            jnp.einsum("mkl,mlj->mkj", root, middle, precision=highest),
            jnp.einsum("mkl,mlj->mkj", middle, inverse, precision=highest),
        )

    root, inverse = lax.fori_loop(0, NS_STEPS, newton_step, (start_root, start_inverse))
    scale_root = jnp.sqrt(scale)
    orthonormal = jnp.einsum("mrk,mkl->mrl", stacked, inverse, precision=highest) / scale_root
    return (orthonormal, root * scale_root)


def body(samples, sketch, leaf_slot):
    columns = sketch.shape[1]
    leaf_count = leaf_slot.shape[1]
    partial_value = jnp.dot(samples, sketch, precision=highest).reshape(leaf_count, -1, columns)
    sketched = lax.psum(partial_value, "samp")
    leaf_basis, triangle = factor(sketched)
    factors = triangle[leaf_slot[0]]
    local_list = []
    while factors.shape[0] > 1:
        stacked = factors.reshape(-1, 2 * columns, columns)
        transfer, factors = factor(stacked)
        local_list.append(transfer)
    local_transfer = jnp.concatenate(local_list, axis=0)
    position = lax.axis_index("clus")
    tree_depth = lax.axis_size("clus").bit_length() - 1
    top_out = jnp.zeros((1, 2 * columns, columns), jnp.float32)
    for level_bit in range(tree_depth):
        partner = from_partner(factors, "clus", level_bit)
        upper_half = position >> level_bit & 1 == 1
        stacked = jnp.where(
            upper_half,
            jnp.concatenate([partner, factors], axis=1),
            jnp.concatenate([factors, partner], axis=1),
        )
        transfer, factors = factor(stacked)
        owned = position % (2 << level_bit) == 1 << level_bit
        top_out = jnp.where(owned, transfer, top_out)
    return (leaf_basis.reshape(-1, columns), local_transfer, top_out, factors[0])


def solution(mesh):
    return jax.shard_map(
        body,
        mesh=mesh,
        in_specs=(P("clus", "samp"), P("samp", None), P("clus", None)),
        out_specs=(P("clus", None), P("clus", None, None), P("clus", None, None), P()),
        check_vma=False,
    )
```

profile of v0, /device:TPU:32, one launch (start us, length us, event | category | flops | bytes accessed | tf_op | source)
XLA Modules:
  0.0 200.3 jit_solution(17816542363103940892)
XLA Ops:
  8.2 2.2 %fusion.137 = f32[1024,128]{1,0:T(8,128)} fusion(f32[1024,128]{1,0:T(8,128)S(1)} %copy-done, f32[128,128]{1,0:T(8,128)} %param.26), kind=kOutput, calls=%fused_computation.230 | convolution fusion | flops 201326592 | bytes 1114112 | tf_op jit(solution)/shard_map/dot_general | solution.py:47
  11.8 39.1 %all-reduce.2.cloned.1.call-done = f32[4,256,128]{2,1,0:T(8,128)} async-done(((f32[4,256,128]{2,1,0:T(8,128)}), f32[4,256,128]{2,1,0:T(8,128)}) %all-reduce.2.cloned.1.call-update) | async-done | bytes 524304 | tf_op jit(solution)/shard_map/psum | solution.py:48
  50.9 2.3 %select_reduce_fusion = (f32[4]{0:T(128)S(1)}, f32[4,128,128]{2,1,0:T(8,128)S(1)}) fusion(pred[128,128]{1,0:T(8,128)(4,1)S(1)} %iota_compare_fusion.13, f32[4,256,128]{2,1,0:T(8,128)} %all-reduce.2.cloned.1.call-done), kind=kOutput, calls=%fused_computation.126 | convolution fusion | flops 201457664 | bytes 802832 | tf_op jit(solution)/shard_map/mrk,mrl->mkl/dot_general | solution.py:23
  53.5 8.8 %while.143 = (s32[]{:T(128)}, f32[4,128,128]{1,2,0:T(8,128)S(1)}, f32[4,128,128]{2,1,0:T(8,128)S(1)}, s32[]{:T(128)}) while((s32[]{:T(128)}, f32[4,128,128]{1,2,0:T(8,128)S(1)}, f32[4,128,128]{2,1,0:T(8,128)S(1)}, s32[]{:T(128)}) %tuple.231), condition=%wide.region_3.0_spmd.clone, body=%wide.region_2.0_spmd.clone.sunk | while | flops 302153728 | bytes 3538997 | solution.py:38
  64.1 5.6 %while.144 = (s32[]{:T(128)}, f32[2,128,128]{1,2,0:T(8,128)S(1)}, f32[2,128,128]{2,1,0:T(8,128)S(1)}, s32[]{:T(128)}) while((s32[]{:T(128)}, f32[2,128,128]{1,2,0:T(8,128)S(1)}, f32[2,128,128]{2,1,0:T(8,128)S(1)}, s32[]{:T(128)}) %tuple.234), condition=%wide.region_6.0_spmd.clone, body=%wide.region_5.0_spmd.clone.sunk | while | flops 151093248 | bytes 1835061 | solution.py:38
  69.9 1.0 select_reduce_fusion.10
  72.5 4.1 %while.145 = (s32[]{:T(128)}, f32[1,128,128]{1,2,0:T(8,128)S(1)}, f32[1,128,128]{2,1,0:T(8,128)S(1)}, s32[]{:T(128)}) while((s32[]{:T(128)}, f32[1,128,128]{1,2,0:T(8,128)S(1)}, f32[1,128,128]{2,1,0:T(8,128)S(1)}, s32[]{:T(128)}) %tuple.267), condition=%wide.region_9.0_spmd.clone, body=%wide.region_8.0_spmd.clone.sunk | while | flops 75563008 | bytes 852021 | solution.py:38
  76.9 3.4 %collective-permute-start = (f32[1,128,128]{1,2,0:T(8,128)S(1)}, f32[1,128,128]{1,2,0:T(8,128)S(1)}, u32[]{:S(2)}, u32[]{:S(2)}) collective-permute-start(f32[1,128,128]{1,2,0:T(8,128)S(1)} %broadcast_multiply_fusion.9), channel_id=1, source_target_pairs={{0,2},{2,0},{4,6},{6,4},{8,10},{10,8},{12,14},{14,12},{16,18},{18,... | collective-permute-start | bytes 196616 | tf_op jit(solution)/shard_map/ppermute | solution.py:19
  80.6 1.4 convolution_divide_fusion
  85.6 4.1 %while.146 = (s32[]{:T(128)}, f32[1,128,128]{1,2,0:T(8,128)S(1)}, f32[1,128,128]{2,1,0:T(8,128)S(1)}, s32[]{:T(128)}) while((s32[]{:T(128)}, f32[1,128,128]{1,2,0:T(8,128)S(1)}, f32[1,128,128]{2,1,0:T(8,128)S(1)}, s32[]{:T(128)}) %tuple.268), condition=%wide.region_12.13_spmd.clone, body=%wide.region_11.12_spmd.clone.sunk | while | flops 75563008 | bytes 852021 | solution.py:38
  89.6 4.9 %collective-permute-start.1 = (f32[1,128,128]{1,2,0:T(8,128)S(1)}, f32[1,128,128]{1,2,0:T(8,128)S(1)}, u32[]{:S(2)}, u32[]{:S(2)}) collective-permute-start(f32[1,128,128]{1,2,0:T(8,128)S(1)} %broadcast_multiply_fusion.8), channel_id=1, source_target_pairs={{0,4},{4,0},{2,6},{6,2},{8,12},{12,8},{10,14},{14,10},{16,20},{20,... | collective-permute-start | bytes 196616 | tf_op jit(solution)/shard_map/ppermute | solution.py:19
  95.0 2.4 %collective-permute-done.1 = f32[1,128,128]{1,2,0:T(8,128)S(1)} collective-permute-done((f32[1,128,128]{1,2,0:T(8,128)S(1)}, f32[1,128,128]{1,2,0:T(8,128)S(1)}, u32[]{:S(2)}, u32[]{:S(2)}) %collective-permute-start.1) | collective-permute-done | bytes 65568 | tf_op jit(solution)/shard_map/ppermute | solution.py:19
  99.7 4.1 %while.147 = (s32[]{:T(128)}, f32[1,128,128]{1,2,0:T(8,128)S(1)}, f32[1,128,128]{2,1,0:T(8,128)S(1)}, s32[]{:T(128)}) while((s32[]{:T(128)}, f32[1,128,128]{1,2,0:T(8,128)S(1)}, f32[1,128,128]{2,1,0:T(8,128)S(1)}, s32[]{:T(128)}) %tuple.269), condition=%wide.region_15.16_spmd.clone, body=%wide.region_14.15_spmd.clone.sunk | while | flops 75563008 | bytes 852021 | solution.py:38
  103.8 2.5 %collective-permute-start.2 = (f32[1,128,128]{1,2,0:T(8,128)S(1)}, f32[1,128,128]{1,2,0:T(8,128)S(1)}, u32[]{:S(2)}, u32[]{:S(2)}) collective-permute-start(f32[1,128,128]{1,2,0:T(8,128)S(1)} %broadcast_multiply_fusion.7), channel_id=1, source_target_pairs={{0,8},{8,0},{2,10},{10,2},{4,12},{12,4},{6,14},{14,6},{16,24},{24,... | collective-permute-start | bytes 196616 | tf_op jit(solution)/shard_map/ppermute | solution.py:19
  106.7 3.2 %collective-permute-done.2 = f32[1,128,128]{1,2,0:T(8,128)S(1)} collective-permute-done((f32[1,128,128]{1,2,0:T(8,128)S(1)}, f32[1,128,128]{1,2,0:T(8,128)S(1)}, u32[]{:S(2)}, u32[]{:S(2)}) %collective-permute-start.2) | collective-permute-done | bytes 65568 | tf_op jit(solution)/shard_map/ppermute | solution.py:19
  112.4 4.1 %while.148 = (s32[]{:T(128)}, f32[1,128,128]{1,2,0:T(8,128)S(1)}, f32[1,128,128]{2,1,0:T(8,128)S(1)}, s32[]{:T(128)}) while((s32[]{:T(128)}, f32[1,128,128]{1,2,0:T(8,128)S(1)}, f32[1,128,128]{2,1,0:T(8,128)S(1)}, s32[]{:T(128)}) %tuple.270), condition=%wide.region_18.19_spmd.clone, body=%wide.region_17.18_spmd.clone.sunk | while | flops 75563008 | bytes 852021 | solution.py:38
  116.5 2.5 %collective-permute-start.3 = (f32[1,128,128]{1,2,0:T(8,128)S(1)}, f32[1,128,128]{1,2,0:T(8,128)S(1)}, u32[]{:S(2)}, u32[]{:S(2)}) collective-permute-start(f32[1,128,128]{1,2,0:T(8,128)S(1)} %broadcast_multiply_fusion.6), channel_id=1, source_target_pairs={{0,16},{16,0},{2,18},{18,2},{4,20},{20,4},{6,22},{22,6},{8,24},{24... | collective-permute-start | bytes 196616 | tf_op jit(solution)/shard_map/ppermute | solution.py:19
  119.4 4.8 %collective-permute-done.3 = f32[1,128,128]{1,2,0:T(8,128)S(1)} collective-permute-done((f32[1,128,128]{1,2,0:T(8,128)S(1)}, f32[1,128,128]{1,2,0:T(8,128)S(1)}, u32[]{:S(2)}, u32[]{:S(2)}) %collective-permute-start.3) | collective-permute-done | bytes 65568 | tf_op jit(solution)/shard_map/ppermute | solution.py:19
  126.7 4.1 %while.149 = (s32[]{:T(128)}, f32[1,128,128]{1,2,0:T(8,128)S(1)}, f32[1,128,128]{2,1,0:T(8,128)S(1)}, s32[]{:T(128)}) while((s32[]{:T(128)}, f32[1,128,128]{1,2,0:T(8,128)S(1)}, f32[1,128,128]{2,1,0:T(8,128)S(1)}, s32[]{:T(128)}) %tuple.271), condition=%wide.region_21.22_spmd.clone, body=%wide.region_20.21_spmd.clone.sunk | while | flops 75563008 | bytes 852021 | solution.py:38
  130.8 3.5 %collective-permute-start.4 = (f32[1,128,128]{1,2,0:T(8,128)S(1)}, f32[1,128,128]{1,2,0:T(8,128)S(1)}, u32[]{:S(2)}, u32[]{:S(2)}) collective-permute-start(f32[1,128,128]{1,2,0:T(8,128)S(1)} %broadcast_multiply_fusion.5), channel_id=1, source_target_pairs={{0,32},{32,0},{2,34},{34,2},{4,36},{36,4},{6,38},{38,6},{8,40},{40... | collective-permute-start | bytes 196616 | tf_op jit(solution)/shard_map/ppermute | solution.py:19
  134.7 6.2 %collective-permute-done.4 = f32[1,128,128]{1,2,0:T(8,128)S(1)} collective-permute-done((f32[1,128,128]{1,2,0:T(8,128)S(1)}, f32[1,128,128]{1,2,0:T(8,128)S(1)}, u32[]{:S(2)}, u32[]{:S(2)}) %collective-permute-start.4) | collective-permute-done | bytes 65568 | tf_op jit(solution)/shard_map/ppermute | solution.py:19
  143.3 4.1 %while.150 = (s32[]{:T(128)}, f32[1,128,128]{1,2,0:T(8,128)S(1)}, f32[1,128,128]{2,1,0:T(8,128)S(1)}, s32[]{:T(128)}) while((s32[]{:T(128)}, f32[1,128,128]{1,2,0:T(8,128)S(1)}, f32[1,128,128]{2,1,0:T(8,128)S(1)}, s32[]{:T(128)}) %tuple.272), condition=%wide.region_24.25_spmd.clone, body=%wide.region_23.24_spmd.clone.sunk | while | flops 75563008 | bytes 852021 | solution.py:38
  147.4 4.0 %collective-permute-start.5 = (f32[1,128,128]{1,2,0:T(8,128)S(1)}, f32[1,128,128]{1,2,0:T(8,128)S(1)}, u32[]{:S(2)}, u32[]{:S(2)}) collective-permute-start(f32[1,128,128]{1,2,0:T(8,128)S(1)} %broadcast_multiply_fusion.4), channel_id=1, source_target_pairs={{0,64},{64,0},{2,66},{66,2},{4,68},{68,4},{6,70},{70,6},{8,72},{72... | collective-permute-start | bytes 196616 | tf_op jit(solution)/shard_map/ppermute | solution.py:19
  151.8 1.8 collective-permute-done.5
  156.1 4.1 %while.151 = (s32[]{:T(128)}, f32[1,128,128]{1,2,0:T(8,128)S(1)}, f32[1,128,128]{2,1,0:T(8,128)S(1)}, s32[]{:T(128)}) while((s32[]{:T(128)}, f32[1,128,128]{1,2,0:T(8,128)S(1)}, f32[1,128,128]{2,1,0:T(8,128)S(1)}, s32[]{:T(128)}) %tuple.273), condition=%wide.region_27.28_spmd.clone, body=%wide.region_26.27_spmd.clone.sunk | while | flops 75563008 | bytes 852021 | solution.py:38
  160.2 5.0 %collective-permute-start.6 = (f32[1,128,128]{1,2,0:T(8,128)S(1)}, f32[1,128,128]{1,2,0:T(8,128)S(1)}, u32[]{:S(2)}, u32[]{:S(2)}) collective-permute-start(f32[1,128,128]{1,2,0:T(8,128)S(1)} %broadcast_multiply_fusion.3), channel_id=1, source_target_pairs={{0,128},{128,0},{2,130},{130,2},{4,132},{132,4},{6,134},{134,6},{8... | collective-permute-start | bytes 196616 | tf_op jit(solution)/shard_map/ppermute | solution.py:19
  165.6 1.8 collective-permute-done.6
  169.8 4.1 %while.152 = (s32[]{:T(128)}, f32[1,128,128]{1,2,0:T(8,128)S(1)}, f32[1,128,128]{2,1,0:T(8,128)S(1)}, s32[]{:T(128)}) while((s32[]{:T(128)}, f32[1,128,128]{1,2,0:T(8,128)S(1)}, f32[1,128,128]{2,1,0:T(8,128)S(1)}, s32[]{:T(128)}) %tuple.274), condition=%wide.region_30.31_spmd.clone, body=%wide.region_29.30_spmd.clone.sunk | while | flops 75563008 | bytes 852021 | solution.py:38
  173.9 8.9 %collective-permute-start.7 = (f32[1,128,128]{1,2,0:T(8,128)S(1)}, f32[1,128,128]{1,2,0:T(8,128)S(1)}, u32[]{:S(2)}, u32[]{:S(2)}) collective-permute-start(f32[1,128,128]{1,2,0:T(8,128)S(1)} %broadcast_multiply_fusion.2), channel_id=1, source_target_pairs={{0,256},{256,0},{2,258},{258,2},{4,260},{260,4},{6,262},{262,6},{8... | collective-permute-start | bytes 196616 | tf_op jit(solution)/shard_map/ppermute | solution.py:19
  183.2 1.9 collective-permute-done.7
  187.6 4.1 %while.153 = (s32[]{:T(128)}, f32[1,128,128]{1,2,0:T(8,128)S(1)}, f32[1,128,128]{2,1,0:T(8,128)S(1)}, s32[]{:T(128)}) while((s32[]{:T(128)}, f32[1,128,128]{1,2,0:T(8,128)S(1)}, f32[1,128,128]{2,1,0:T(8,128)S(1)}, s32[]{:T(128)}) %tuple.266), condition=%wide.region_33.34_spmd.clone, body=%wide.region_32.33_spmd.clone.sunk | while | flops 75563008 | bytes 852021 | solution.py:38
  192.4 1.0 fusion.73
  (387 shorter events, 72.9 us)
Async XLA Ops:
  7.2 1.0 copy-start
  7.2 43.8 %all-reduce.2.cloned.1.call-start = ((), (), s32[]{:S(2)}) async-start(), calls=%async_computation | async-start | bytes 1048576 | tf_op jit(solution)/shard_map/psum | solution.py:48
  10.5 0.6 copy-start.1
  11.1 0.7 copy-start.12
  71.6 0.8 copy-start.3
  76.6 4.0 %copy-start.11 = (f32[4,256,128]{2,1,0:T(8,128)S(1)}, f32[4,256,128]{2,1,0:T(8,128)}, u32[]{:S(2)}) copy-start(f32[4,256,128]{2,1,0:T(8,128)} %all-reduce.2.cloned.1.call-done) | copy-start | bytes 1572868
  76.9 6.2 %collective-permute-start = (f32[1,128,128]{1,2,0:T(8,128)S(1)}, f32[1,128,128]{1,2,0:T(8,128)S(1)}, u32[]{:S(2)}, u32[]{:S(2)}) collective-permute-start(f32[1,128,128]{1,2,0:T(8,128)S(1)} %broadcast_multiply_fusion.9), channel_id=1, source_target_pairs={{0,2},{2,0},{4,6},{6,4},{8,10},{10,8},{12,14},{14,12},{16,18},{18,... | collective-permute-start | bytes 196616 | tf_op jit(solution)/shard_map/ppermute | solution.py:19
  84.7 0.8 copy-start.4
  89.6 7.7 %collective-permute-start.1 = (f32[1,128,128]{1,2,0:T(8,128)S(1)}, f32[1,128,128]{1,2,0:T(8,128)S(1)}, u32[]{:S(2)}, u32[]{:S(2)}) collective-permute-start(f32[1,128,128]{1,2,0:T(8,128)S(1)} %broadcast_multiply_fusion.8), channel_id=1, source_target_pairs={{0,4},{4,0},{2,6},{6,2},{8,12},{12,8},{10,14},{14,10},{16,20},{20,... | collective-permute-start | bytes 196616 | tf_op jit(solution)/shard_map/ppermute | solution.py:19
  98.9 0.8 copy-start.5
  103.8 6.2 %collective-permute-start.2 = (f32[1,128,128]{1,2,0:T(8,128)S(1)}, f32[1,128,128]{1,2,0:T(8,128)S(1)}, u32[]{:S(2)}, u32[]{:S(2)}) collective-permute-start(f32[1,128,128]{1,2,0:T(8,128)S(1)} %broadcast_multiply_fusion.7), channel_id=1, source_target_pairs={{0,8},{8,0},{2,10},{10,2},{4,12},{12,4},{6,14},{14,6},{16,24},{24,... | collective-permute-start | bytes 196616 | tf_op jit(solution)/shard_map/ppermute | solution.py:19
  111.6 0.8 copy-start.6
  116.5 7.8 %collective-permute-start.3 = (f32[1,128,128]{1,2,0:T(8,128)S(1)}, f32[1,128,128]{1,2,0:T(8,128)S(1)}, u32[]{:S(2)}, u32[]{:S(2)}) collective-permute-start(f32[1,128,128]{1,2,0:T(8,128)S(1)} %broadcast_multiply_fusion.6), channel_id=1, source_target_pairs={{0,16},{16,0},{2,18},{18,2},{4,20},{20,4},{6,22},{22,6},{8,24},{24... | collective-permute-start | bytes 196616 | tf_op jit(solution)/shard_map/ppermute | solution.py:19
  125.9 0.8 copy-start.7
  130.8 10.1 %collective-permute-start.4 = (f32[1,128,128]{1,2,0:T(8,128)S(1)}, f32[1,128,128]{1,2,0:T(8,128)S(1)}, u32[]{:S(2)}, u32[]{:S(2)}) collective-permute-start(f32[1,128,128]{1,2,0:T(8,128)S(1)} %broadcast_multiply_fusion.5), channel_id=1, source_target_pairs={{0,32},{32,0},{2,34},{34,2},{4,36},{36,4},{6,38},{38,6},{8,40},{40... | collective-permute-start | bytes 196616 | tf_op jit(solution)/shard_map/ppermute | solution.py:19
  142.5 0.8 copy-start.8
  147.4 6.2 %collective-permute-start.5 = (f32[1,128,128]{1,2,0:T(8,128)S(1)}, f32[1,128,128]{1,2,0:T(8,128)S(1)}, u32[]{:S(2)}, u32[]{:S(2)}) collective-permute-start(f32[1,128,128]{1,2,0:T(8,128)S(1)} %broadcast_multiply_fusion.4), channel_id=1, source_target_pairs={{0,64},{64,0},{2,66},{66,2},{4,68},{68,4},{6,70},{70,6},{8,72},{72... | collective-permute-start | bytes 196616 | tf_op jit(solution)/shard_map/ppermute | solution.py:19
  155.2 0.8 copy-start.9
  160.2 7.2 %collective-permute-start.6 = (f32[1,128,128]{1,2,0:T(8,128)S(1)}, f32[1,128,128]{1,2,0:T(8,128)S(1)}, u32[]{:S(2)}, u32[]{:S(2)}) collective-permute-start(f32[1,128,128]{1,2,0:T(8,128)S(1)} %broadcast_multiply_fusion.3), channel_id=1, source_target_pairs={{0,128},{128,0},{2,130},{130,2},{4,132},{132,4},{6,134},{134,6},{8... | collective-permute-start | bytes 196616 | tf_op jit(solution)/shard_map/ppermute | solution.py:19
  169.0 0.8 copy-start.10
  173.9 11.2 %collective-permute-start.7 = (f32[1,128,128]{1,2,0:T(8,128)S(1)}, f32[1,128,128]{1,2,0:T(8,128)S(1)}, u32[]{:S(2)}, u32[]{:S(2)}) collective-permute-start(f32[1,128,128]{1,2,0:T(8,128)S(1)} %broadcast_multiply_fusion.2), channel_id=1, source_target_pairs={{0,256},{256,0},{2,258},{258,2},{4,260},{260,4},{6,262},{262,6},{8... | collective-permute-start | bytes 196616 | tf_op jit(solution)/shard_map/ppermute | solution.py:19
  186.7 0.8 copy-start.2
Sparse Core Ops, SparseCore 0:
  11.5 39.4 all-reduce.1
where the time goes:
time: 201 us; the launch traced here: 200 us
  matrix products  66.6 us (33%)
  waiting for transfers between devices  61.6 us (31%)
  starting transfers between devices  34.7 us (17%)
  between operations  21 us (10%)
  local copies, waits for them, and re-layouts  11.7 us (6%)
  loops' own time  2.47 us (1%)
  other arithmetic  2.16 us (1%)
    psum x1, waiting for transfers between devices, body(): sketched = lax.psum(partial_value, 'samp')  39.1 us
    ppermute x8, starting transfers between devices, from_partner(): return lax.ppermute(block, axis, route)  34.7 us
    ppermute x8, waiting for transfers between devices, from_partner(): return lax.ppermute(block, axis, route)  22.5 us
    dot_general x55, matrix products, newton_step(): jnp.einsum('mkl,mlj->mkj', root, middle, precision=highest)  17.8 us
    dot_general x55, matrix products, newton_step(): jnp.einsum('mkl,mlj->mkj', inverse, root, precision=highest)  17.3 us
    dot_general x55, matrix products, newton_step(): jnp.einsum('mkl,mlj->mkj', middle, inverse, precision=highest)  12.4 us
    dot_general x11, matrix products, factor(): jnp.einsum('mrk,mrl->mkl', stacked, stacked, precision=highest)  11 us
    unnamed x37, local copies, waits for them, and re-layouts  9.91 us
  transfers between devices with their start and end apart: 9, of which 9 were waited for; matrix products, arithmetic and copies ran while one was open for 3% of the time, Pallas kernels for 0%

commit v1 on v0

--- a/solution.py
+++ b/solution.py
@@ -4,18 +4,15 @@
 from jax.sharding import PartitionSpec as P
 
 NS_STEPS = 5
+ROUND_BITS = 2
 
 
 highest = lax.Precision.HIGHEST
 
 
-def from_partner(block, axis, apart):
+def from_xor(block, axis, mask):
     count = lax.axis_size(axis)
-    route = []
-    for low in range(count):
-        high = low | 1 << apart
-        if high != low and high < count:
-            route += [(low, high), (high, low)]
+    route = [(low, low ^ mask) for low in range(count) if low ^ mask < count]
     return lax.ppermute(block, axis, route)
 
 
@@ -45,7 +42,7 @@
     columns = sketch.shape[1]
     leaf_count = leaf_slot.shape[1]
     partial_value = jnp.dot(samples, sketch, precision=highest).reshape(leaf_count, -1, columns)
-    sketched = lax.psum(partial_value, "samp")
+    sketched = partial_value + from_xor(partial_value, "samp", 1)
     leaf_basis, triangle = factor(sketched)
     factors = triangle[leaf_slot[0]]
     local_list = []
@@ -57,17 +54,24 @@
     position = lax.axis_index("clus")
     tree_depth = lax.axis_size("clus").bit_length() - 1
     top_out = jnp.zeros((1, 2 * columns, columns), jnp.float32)
-    for level_bit in range(tree_depth):
-        partner = from_partner(factors, "clus", level_bit)
-        upper_half = position >> level_bit & 1 == 1
-        stacked = jnp.where(
-            upper_half,
-            jnp.concatenate([partner, factors], axis=1),
-            jnp.concatenate([factors, partner], axis=1),
-        )
-        transfer, factors = factor(stacked)
-        owned = position % (2 << level_bit) == 1 << level_bit
-        top_out = jnp.where(owned, transfer, top_out)
+    low_bit = 0
+    while low_bit < tree_depth:
+        width = min(ROUND_BITS, tree_depth - low_bit)
+        members = 1 << width
+        member = (position >> low_bit) & (members - 1)
+        received = [factors] + [from_xor(factors, "clus", j << low_bit) for j in range(1, members)]
+        received = jnp.concatenate(received, axis=0)
+        slots = jnp.arange(members, dtype=jnp.int32) ^ member
+        group = jnp.take(received, slots, axis=0)
+        for level in range(width):
+            stacked = group.reshape(-1, 2 * columns, columns)
+            transfer, group = factor(stacked)
+            level_bit = low_bit + level
+            mine = lax.dynamic_index_in_dim(transfer, member >> (level + 1), 0, keepdims=True)
+            owned = position % (2 << level_bit) == 1 << level_bit
+            top_out = jnp.where(owned, mine, top_out)
+        factors = group
+        low_bit += width
     return (leaf_basis.reshape(-1, columns), local_transfer, top_out, factors[0])
 
 

time: 201 us -> 164 us (0.82)
  the two profiles are of different devices: /device:TPU:32 before, /device:TPU:8 now
where the time goes in v1:
time: 164 us; the launch traced here: 163 us
  matrix products  72 us (44%)
  starting transfers between devices  55.2 us (34%)
  local copies, waits for them, and re-layouts  16.3 us (10%)
  waiting for transfers between devices  7.97 us (5%)
  between operations  5.12 us (3%)
  other arithmetic  3.51 us (2%)
  loops' own time  2.76 us (2%)
    ppermute x13, starting transfers between devices, from_xor(): return lax.ppermute(block, axis, route)  55.2 us
    dot_general x55, matrix products, newton_step(): jnp.einsum('mkl,mlj->mkj', root, middle, precision=highest)  19.8 us
    dot_general x55, matrix products, newton_step(): jnp.einsum('mkl,mlj->mkj', inverse, root, precision=highest)  19.7 us
    dot_general x55, matrix products, newton_step(): jnp.einsum('mkl,mlj->mkj', middle, inverse, precision=highest)  13.7 us
    dot_general x11, matrix products, factor(): jnp.einsum('mrk,mrl->mkl', stacked, stacked, precision=highest)  9.57 us
    unnamed x39, local copies, waits for them, and re-layouts  8.71 us
    ppermute x13, waiting for transfers between devices, from_xor(): return lax.ppermute(block, axis, route)  7.97 us
    dot_general x11, matrix products, factor(): jnp.einsum('mrk,mkl->mrl', stacked, inverse, precision=highest) / scale_root  7.82 us
  transfers between devices with their start and end apart: 13, of which 5 were waited for; matrix products, arithmetic and copies ran while one was open for 5% of the time, Pallas kernels for 0%

profile of v1, /device:TPU:8, one launch (start us, length us, event | category | flops | bytes accessed | tf_op | source)
XLA Modules:
  0.0 162.8 jit_solution(15643967585361404123)
XLA Ops:
  1.7 1.4 fusion.92
  3.1 1.9 %collective-permute-start = (f32[4,256,128]{2,1,0:T(8,128)S(1)}, f32[4,256,128]{2,1,0:T(8,128)S(1)}, u32[]{:S(2)}, u32[]{:S(2)}) collective-permute-start(f32[4,256,128]{2,1,0:T(8,128)S(1)} %bitcast.430), channel_id=1, source_target_pairs={{0,1},{1,0},{2,3},{3,2},{4,5},{5,4},{6,7},{7,6},{8,9},{9,8},{10,11... | collective-permute-start | bytes 1572872 | tf_op jit(solution)/shard_map/ppermute | solution.py:16
  6.9 1.1 select_reduce_fusion
  8.3 8.8 %while.143 = (s32[]{:T(128)}, f32[4,128,128]{1,2,0:T(8,128)S(1)}, f32[4,128,128]{2,1,0:T(8,128)S(1)}, s32[]{:T(128)}) while((s32[]{:T(128)}, f32[4,128,128]{1,2,0:T(8,128)S(1)}, f32[4,128,128]{2,1,0:T(8,128)S(1)}, s32[]{:T(128)}) %tuple.236), condition=%wide.region_2.0_spmd.clone, body=%wide.region_1.0_spmd.clone.sunk | while | flops 302153728 | bytes 3538997 | solution.py:35
  18.9 5.6 %while.144 = (s32[]{:T(128)}, f32[2,128,128]{1,2,0:T(8,128)S(1)}, f32[2,128,128]{2,1,0:T(8,128)S(1)}, s32[]{:T(128)}) while((s32[]{:T(128)}, f32[2,128,128]{1,2,0:T(8,128)S(1)}, f32[2,128,128]{2,1,0:T(8,128)S(1)}, s32[]{:T(128)}) %tuple.239), condition=%wide.region_5.0_spmd.clone, body=%wide.region_4.0_spmd.clone.sunk | while | flops 151093248 | bytes 1835061 | solution.py:35
  27.3 4.1 %while.145 = (s32[]{:T(128)}, f32[1,128,128]{1,2,0:T(8,128)S(1)}, f32[1,128,128]{2,1,0:T(8,128)S(1)}, s32[]{:T(128)}) while((s32[]{:T(128)}, f32[1,128,128]{1,2,0:T(8,128)S(1)}, f32[1,128,128]{2,1,0:T(8,128)S(1)}, s32[]{:T(128)}) %tuple.270), condition=%wide.region_8.0_spmd.clone, body=%wide.region_7.0_spmd.clone.sunk | while | flops 75563008 | bytes 852021 | solution.py:35
  31.4 4.7 %collective-permute-start.3 = (f32[1,128,128]{2,1,0:T(8,128)S(1)}, f32[1,128,128]{2,1,0:T(8,128)S(1)}, u32[]{:S(2)}, u32[]{:S(2)}) collective-permute-start(f32[1,128,128]{2,1,0:T(8,128)S(1)} %broadcast_multiply_fusion.9), channel_id=1, source_target_pairs={{0,6},{2,4},{4,2},{6,0},{8,14},{10,12},{12,10},{14,8},{16,22},{18,... | collective-permute-start | bytes 196616 | tf_op jit(solution)/shard_map/ppermute | solution.py:16
  36.1 2.7 %collective-permute-start.2 = (f32[1,128,128]{2,1,0:T(8,128)S(1)}, f32[1,128,128]{2,1,0:T(8,128)S(1)}, u32[]{:S(2)}, u32[]{:S(2)}) collective-permute-start(f32[1,128,128]{2,1,0:T(8,128)S(1)} %broadcast_multiply_fusion.9), channel_id=1, source_target_pairs={{0,4},{2,6},{4,0},{6,2},{8,12},{10,14},{12,8},{14,10},{16,20},{18,... | collective-permute-start | bytes 196616 | tf_op jit(solution)/shard_map/ppermute | solution.py:16
  38.8 2.4 %collective-permute-start.1 = (f32[1,128,128]{2,1,0:T(8,128)S(1)}, f32[1,128,128]{2,1,0:T(8,128)S(1)}, u32[]{:S(2)}, u32[]{:S(2)}) collective-permute-start(f32[1,128,128]{2,1,0:T(8,128)S(1)} %broadcast_multiply_fusion.9), channel_id=1, source_target_pairs={{0,2},{2,0},{4,6},{6,4},{8,10},{10,8},{12,14},{14,12},{16,18},{18,... | collective-permute-start | bytes 196616 | tf_op jit(solution)/shard_map/ppermute | solution.py:16
  41.3 1.4 convolution_divide_fusion
  46.6 5.6 %while.146 = (s32[]{:T(128)}, f32[2,128,128]{1,2,0:T(8,128)S(1)}, f32[2,128,128]{2,1,0:T(8,128)S(1)}, s32[]{:T(128)}) while((s32[]{:T(128)}, f32[2,128,128]{1,2,0:T(8,128)S(1)}, f32[2,128,128]{2,1,0:T(8,128)S(1)}, s32[]{:T(128)}) %tuple.245), condition=%wide.region_11.13_spmd.clone, body=%wide.region_10.12_spmd.clone.sunk | while | flops 151093248 | bytes 1835061 | solution.py:35
  55.0 4.1 %while.147 = (s32[]{:T(128)}, f32[1,128,128]{1,2,0:T(8,128)S(1)}, f32[1,128,128]{2,1,0:T(8,128)S(1)}, s32[]{:T(128)}) while((s32[]{:T(128)}, f32[1,128,128]{1,2,0:T(8,128)S(1)}, f32[1,128,128]{2,1,0:T(8,128)S(1)}, s32[]{:T(128)}) %tuple.271), condition=%wide.region_14.16_spmd.clone, body=%wide.region_13.15_spmd.clone.sunk | while | flops 75563008 | bytes 852021 | solution.py:35
  59.7 3.5 %collective-permute-start.6 = (f32[1,128,128]{2,1,0:T(8,128)S(1)}, f32[1,128,128]{2,1,0:T(8,128)S(1)}, u32[]{:S(2)}, u32[]{:S(2)}) collective-permute-start(f32[1,128,128]{2,1,0:T(8,128)S(1)} %broadcast_multiply_fusion.8), channel_id=1, source_target_pairs={{0,24},{2,26},{4,28},{6,30},{8,16},{10,18},{12,20},{14,22},{16,8},... | collective-permute-start | bytes 196616 | tf_op jit(solution)/shard_map/ppermute | solution.py:16
  63.2 7.6 %collective-permute-start.5 = (f32[1,128,128]{2,1,0:T(8,128)S(1)}, f32[1,128,128]{2,1,0:T(8,128)S(1)}, u32[]{:S(2)}, u32[]{:S(2)}) collective-permute-start(f32[1,128,128]{2,1,0:T(8,128)S(1)} %broadcast_multiply_fusion.8), channel_id=1, source_target_pairs={{0,16},{2,18},{4,20},{6,22},{8,24},{10,26},{12,28},{14,30},{16,0},... | collective-permute-start | bytes 196616 | tf_op jit(solution)/shard_map/ppermute | solution.py:16
  70.8 2.1 %collective-permute-start.4 = (f32[1,128,128]{2,1,0:T(8,128)S(1)}, f32[1,128,128]{2,1,0:T(8,128)S(1)}, u32[]{:S(2)}, u32[]{:S(2)}) collective-permute-start(f32[1,128,128]{2,1,0:T(8,128)S(1)} %broadcast_multiply_fusion.8), channel_id=1, source_target_pairs={{0,8},{2,10},{4,12},{6,14},{8,0},{10,2},{12,4},{14,6},{16,24},{18,... | collective-permute-start | bytes 196616 | tf_op jit(solution)/shard_map/ppermute | solution.py:16
  73.9 3.0 %collective-permute-done.4 = f32[1,128,128]{2,1,0:T(8,128)S(1)} collective-permute-done((f32[1,128,128]{2,1,0:T(8,128)S(1)}, f32[1,128,128]{2,1,0:T(8,128)S(1)}, u32[]{:S(2)}, u32[]{:S(2)}) %collective-permute-start.4) | collective-permute-done | bytes 65568 | tf_op jit(solution)/shard_map/ppermute | solution.py:16
  78.6 5.6 %while.148 = (s32[]{:T(128)}, f32[2,128,128]{1,2,0:T(8,128)S(1)}, f32[2,128,128]{2,1,0:T(8,128)S(1)}, s32[]{:T(128)}) while((s32[]{:T(128)}, f32[2,128,128]{1,2,0:T(8,128)S(1)}, f32[2,128,128]{2,1,0:T(8,128)S(1)}, s32[]{:T(128)}) %tuple.251), condition=%wide.region_17.19_spmd.clone, body=%wide.region_16.18_spmd.clone.sunk | while | flops 151093248 | bytes 1835061 | solution.py:35
  84.4 1.1 select_reduce_fusion.8
  87.0 4.1 %while.149 = (s32[]{:T(128)}, f32[1,128,128]{1,2,0:T(8,128)S(1)}, f32[1,128,128]{2,1,0:T(8,128)S(1)}, s32[]{:T(128)}) while((s32[]{:T(128)}, f32[1,128,128]{1,2,0:T(8,128)S(1)}, f32[1,128,128]{2,1,0:T(8,128)S(1)}, s32[]{:T(128)}) %tuple.272), condition=%wide.region_20.22_spmd.clone, body=%wide.region_19.21_spmd.clone.sunk | while | flops 75563008 | bytes 852021 | solution.py:35
  91.7 5.0 %collective-permute-start.9 = (f32[1,128,128]{2,1,0:T(8,128)S(1)}, f32[1,128,128]{2,1,0:T(8,128)S(1)}, u32[]{:S(2)}, u32[]{:S(2)}) collective-permute-start(f32[1,128,128]{2,1,0:T(8,128)S(1)} %broadcast_multiply_fusion.7), channel_id=1, source_target_pairs={{0,96},{2,98},{4,100},{6,102},{8,104},{10,106},{12,108},{14,110},{... | collective-permute-start | bytes 196616 | tf_op jit(solution)/shard_map/ppermute | solution.py:16
  96.7 1.9 %collective-permute-start.8 = (f32[1,128,128]{2,1,0:T(8,128)S(1)}, f32[1,128,128]{2,1,0:T(8,128)S(1)}, u32[]{:S(2)}, u32[]{:S(2)}) collective-permute-start(f32[1,128,128]{2,1,0:T(8,128)S(1)} %broadcast_multiply_fusion.7), channel_id=1, source_target_pairs={{0,64},{2,66},{4,68},{6,70},{8,72},{10,74},{12,76},{14,78},{16,80}... | collective-permute-start | bytes 196616 | tf_op jit(solution)/shard_map/ppermute | solution.py:16
  98.7 6.2 %collective-permute-start.7 = (f32[1,128,128]{2,1,0:T(8,128)S(1)}, f32[1,128,128]{2,1,0:T(8,128)S(1)}, u32[]{:S(2)}, u32[]{:S(2)}) collective-permute-start(f32[1,128,128]{2,1,0:T(8,128)S(1)} %broadcast_multiply_fusion.7), channel_id=1, source_target_pairs={{0,32},{2,34},{4,36},{6,38},{8,40},{10,42},{12,44},{14,46},{16,48}... | collective-permute-start | bytes 196616 | tf_op jit(solution)/shard_map/ppermute | solution.py:16
  105.9 1.6 fusion.70
  107.5 1.4 collective-permute-done.7
  110.5 5.6 %while.150 = (s32[]{:T(128)}, f32[2,128,128]{1,2,0:T(8,128)S(1)}, f32[2,128,128]{2,1,0:T(8,128)S(1)}, s32[]{:T(128)}) while((s32[]{:T(128)}, f32[2,128,128]{1,2,0:T(8,128)S(1)}, f32[2,128,128]{2,1,0:T(8,128)S(1)}, s32[]{:T(128)}) %tuple.257), condition=%wide.region_23.25_spmd.clone, body=%wide.region_22.24_spmd.clone.sunk | while | flops 151093248 | bytes 1835061 | solution.py:35
  118.9 4.1 %while.151 = (s32[]{:T(128)}, f32[1,128,128]{1,2,0:T(8,128)S(1)}, f32[1,128,128]{2,1,0:T(8,128)S(1)}, s32[]{:T(128)}) while((s32[]{:T(128)}, f32[1,128,128]{1,2,0:T(8,128)S(1)}, f32[1,128,128]{2,1,0:T(8,128)S(1)}, s32[]{:T(128)}) %tuple.273), condition=%wide.region_26.28_spmd.clone, body=%wide.region_25.27_spmd.clone.sunk | while | flops 75563008 | bytes 852021 | solution.py:35
  123.6 10.9 %collective-permute-start.12 = (f32[1,128,128]{2,1,0:T(8,128)S(1)}, f32[1,128,128]{2,1,0:T(8,128)S(1)}, u32[]{:S(2)}, u32[]{:S(2)}) collective-permute-start(f32[1,128,128]{2,1,0:T(8,128)S(1)} %broadcast_multiply_fusion.6), channel_id=1, source_target_pairs={{0,384},{2,386},{4,388},{6,390},{8,392},{10,394},{12,396},{14,398}... | collective-permute-start | bytes 196616 | tf_op jit(solution)/shard_map/ppermute | solution.py:16
  134.5 1.9 %collective-permute-start.11 = (f32[1,128,128]{2,1,0:T(8,128)S(1)}, f32[1,128,128]{2,1,0:T(8,128)S(1)}, u32[]{:S(2)}, u32[]{:S(2)}) collective-permute-start(f32[1,128,128]{2,1,0:T(8,128)S(1)} %broadcast_multiply_fusion.6), channel_id=1, source_target_pairs={{0,256},{2,258},{4,260},{6,262},{8,264},{10,266},{12,268},{14,270}... | collective-permute-start | bytes 196616 | tf_op jit(solution)/shard_map/ppermute | solution.py:16
  136.4 4.3 %collective-permute-start.10 = (f32[1,128,128]{2,1,0:T(8,128)S(1)}, f32[1,128,128]{2,1,0:T(8,128)S(1)}, u32[]{:S(2)}, u32[]{:S(2)}) collective-permute-start(f32[1,128,128]{2,1,0:T(8,128)S(1)} %broadcast_multiply_fusion.6), channel_id=1, source_target_pairs={{0,128},{2,130},{4,132},{6,134},{8,136},{10,138},{12,140},{14,142}... | collective-permute-start | bytes 196616 | tf_op jit(solution)/shard_map/ppermute | solution.py:16
  142.7 2.2 %collective-permute-done.11 = f32[1,128,128]{2,1,0:T(8,128)S(1)} collective-permute-done((f32[1,128,128]{2,1,0:T(8,128)S(1)}, f32[1,128,128]{2,1,0:T(8,128)S(1)}, u32[]{:S(2)}, u32[]{:S(2)}) %collective-permute-start.11) | collective-permute-done | bytes 65568 | tf_op jit(solution)/shard_map/ppermute | solution.py:16
  146.6 5.6 %while.152 = (s32[]{:T(128)}, f32[2,128,128]{1,2,0:T(8,128)S(1)}, f32[2,128,128]{2,1,0:T(8,128)S(1)}, s32[]{:T(128)}) while((s32[]{:T(128)}, f32[2,128,128]{1,2,0:T(8,128)S(1)}, f32[2,128,128]{2,1,0:T(8,128)S(1)}, s32[]{:T(128)}) %tuple.263), condition=%wide.region_29.31_spmd.clone, body=%wide.region_28.30_spmd.clone.sunk | while | flops 151093248 | bytes 1835061 | solution.py:35
  156.0 4.1 %while.153 = (s32[]{:T(128)}, f32[1,128,128]{1,2,0:T(8,128)S(1)}, f32[1,128,128]{2,1,0:T(8,128)S(1)}, s32[]{:T(128)}) while((s32[]{:T(128)}, f32[1,128,128]{1,2,0:T(8,128)S(1)}, f32[1,128,128]{2,1,0:T(8,128)S(1)}, s32[]{:T(128)}) %tuple.269), condition=%wide.region_32.34_spmd.clone, body=%wide.region_31.33_spmd.clone.sunk | while | flops 75563008 | bytes 852021 | solution.py:35
  (453 shorter events, 86.6 us)
Async XLA Ops:
  0.6 1.0 copy-start
  3.1 3.8 %collective-permute-start = (f32[4,256,128]{2,1,0:T(8,128)S(1)}, f32[4,256,128]{2,1,0:T(8,128)S(1)}, u32[]{:S(2)}, u32[]{:S(2)}) collective-permute-start(f32[4,256,128]{2,1,0:T(8,128)S(1)} %bitcast.430), channel_id=1, source_target_pairs={{0,1},{1,0},{2,3},{3,2},{4,5},{5,4},{6,7},{7,6},{8,9},{9,8},{10,11... | collective-permute-start | bytes 1572872 | tf_op jit(solution)/shard_map/ppermute | solution.py:16
  5.0 0.6 copy-start.1
  5.7 0.7 copy-start.13
  26.4 0.8 copy-start.9
  31.4 12.7 %collective-permute-start.3 = (f32[1,128,128]{2,1,0:T(8,128)S(1)}, f32[1,128,128]{2,1,0:T(8,128)S(1)}, u32[]{:S(2)}, u32[]{:S(2)}) collective-permute-start(f32[1,128,128]{2,1,0:T(8,128)S(1)} %broadcast_multiply_fusion.9), channel_id=1, source_target_pairs={{0,6},{2,4},{4,2},{6,0},{8,14},{10,12},{12,10},{14,8},{16,22},{18,... | collective-permute-start | bytes 196616 | tf_op jit(solution)/shard_map/ppermute | solution.py:16
  36.1 8.0 %collective-permute-start.2 = (f32[1,128,128]{2,1,0:T(8,128)S(1)}, f32[1,128,128]{2,1,0:T(8,128)S(1)}, u32[]{:S(2)}, u32[]{:S(2)}) collective-permute-start(f32[1,128,128]{2,1,0:T(8,128)S(1)} %broadcast_multiply_fusion.9), channel_id=1, source_target_pairs={{0,4},{2,6},{4,0},{6,2},{8,12},{10,14},{12,8},{14,10},{16,20},{18,... | collective-permute-start | bytes 196616 | tf_op jit(solution)/shard_map/ppermute | solution.py:16
  38.8 6.2 %collective-permute-start.1 = (f32[1,128,128]{2,1,0:T(8,128)S(1)}, f32[1,128,128]{2,1,0:T(8,128)S(1)}, u32[]{:S(2)}, u32[]{:S(2)}) collective-permute-start(f32[1,128,128]{2,1,0:T(8,128)S(1)} %broadcast_multiply_fusion.9), channel_id=1, source_target_pairs={{0,2},{2,0},{4,6},{6,4},{8,10},{10,8},{12,14},{14,12},{16,18},{18,... | collective-permute-start | bytes 196616 | tf_op jit(solution)/shard_map/ppermute | solution.py:16
  54.1 0.8 copy-start.10
  59.1 0.6 copy-start.3
  59.7 14.2 %collective-permute-start.6 = (f32[1,128,128]{2,1,0:T(8,128)S(1)}, f32[1,128,128]{2,1,0:T(8,128)S(1)}, u32[]{:S(2)}, u32[]{:S(2)}) collective-permute-start(f32[1,128,128]{2,1,0:T(8,128)S(1)} %broadcast_multiply_fusion.8), channel_id=1, source_target_pairs={{0,24},{2,26},{4,28},{6,30},{8,16},{10,18},{12,20},{14,22},{16,8},... | collective-permute-start | bytes 196616 | tf_op jit(solution)/shard_map/ppermute | solution.py:16
  63.2 10.8 %collective-permute-start.5 = (f32[1,128,128]{2,1,0:T(8,128)S(1)}, f32[1,128,128]{2,1,0:T(8,128)S(1)}, u32[]{:S(2)}, u32[]{:S(2)}) collective-permute-start(f32[1,128,128]{2,1,0:T(8,128)S(1)} %broadcast_multiply_fusion.8), channel_id=1, source_target_pairs={{0,16},{2,18},{4,20},{6,22},{8,24},{10,26},{12,28},{14,30},{16,0},... | collective-permute-start | bytes 196616 | tf_op jit(solution)/shard_map/ppermute | solution.py:16
  70.8 6.2 %collective-permute-start.4 = (f32[1,128,128]{2,1,0:T(8,128)S(1)}, f32[1,128,128]{2,1,0:T(8,128)S(1)}, u32[]{:S(2)}, u32[]{:S(2)}) collective-permute-start(f32[1,128,128]{2,1,0:T(8,128)S(1)} %broadcast_multiply_fusion.8), channel_id=1, source_target_pairs={{0,8},{2,10},{4,12},{6,14},{8,0},{10,2},{12,4},{14,6},{16,24},{18,... | collective-permute-start | bytes 196616 | tf_op jit(solution)/shard_map/ppermute | solution.py:16
  86.1 0.8 copy-start.11
  91.1 0.6 copy-start.5
  91.7 15.8 %collective-permute-start.9 = (f32[1,128,128]{2,1,0:T(8,128)S(1)}, f32[1,128,128]{2,1,0:T(8,128)S(1)}, u32[]{:S(2)}, u32[]{:S(2)}) collective-permute-start(f32[1,128,128]{2,1,0:T(8,128)S(1)} %broadcast_multiply_fusion.7), channel_id=1, source_target_pairs={{0,96},{2,98},{4,100},{6,102},{8,104},{10,106},{12,108},{14,110},{... | collective-permute-start | bytes 196616 | tf_op jit(solution)/shard_map/ppermute | solution.py:16
  96.7 10.7 %collective-permute-start.8 = (f32[1,128,128]{2,1,0:T(8,128)S(1)}, f32[1,128,128]{2,1,0:T(8,128)S(1)}, u32[]{:S(2)}, u32[]{:S(2)}) collective-permute-start(f32[1,128,128]{2,1,0:T(8,128)S(1)} %broadcast_multiply_fusion.7), channel_id=1, source_target_pairs={{0,64},{2,66},{4,68},{6,70},{8,72},{10,74},{12,76},{14,78},{16,80}... | collective-permute-start | bytes 196616 | tf_op jit(solution)/shard_map/ppermute | solution.py:16
  98.7 10.3 %collective-permute-start.7 = (f32[1,128,128]{2,1,0:T(8,128)S(1)}, f32[1,128,128]{2,1,0:T(8,128)S(1)}, u32[]{:S(2)}, u32[]{:S(2)}) collective-permute-start(f32[1,128,128]{2,1,0:T(8,128)S(1)} %broadcast_multiply_fusion.7), channel_id=1, source_target_pairs={{0,32},{2,34},{4,36},{6,38},{8,40},{10,42},{12,44},{14,46},{16,48}... | collective-permute-start | bytes 196616 | tf_op jit(solution)/shard_map/ppermute | solution.py:16
  104.8 1.1 copy-start.4
  118.0 0.8 copy-start.12
  123.0 0.6 copy-start.7
  123.6 19.1 %collective-permute-start.12 = (f32[1,128,128]{2,1,0:T(8,128)S(1)}, f32[1,128,128]{2,1,0:T(8,128)S(1)}, u32[]{:S(2)}, u32[]{:S(2)}) collective-permute-start(f32[1,128,128]{2,1,0:T(8,128)S(1)} %broadcast_multiply_fusion.6), channel_id=1, source_target_pairs={{0,384},{2,386},{4,388},{6,390},{8,392},{10,394},{12,396},{14,398}... | collective-permute-start | bytes 196616 | tf_op jit(solution)/shard_map/ppermute | solution.py:16
  134.5 10.5 %collective-permute-start.11 = (f32[1,128,128]{2,1,0:T(8,128)S(1)}, f32[1,128,128]{2,1,0:T(8,128)S(1)}, u32[]{:S(2)}, u32[]{:S(2)}) collective-permute-start(f32[1,128,128]{2,1,0:T(8,128)S(1)} %broadcast_multiply_fusion.6), channel_id=1, source_target_pairs={{0,256},{2,258},{4,260},{6,262},{8,264},{10,266},{12,268},{14,270}... | collective-permute-start | bytes 196616 | tf_op jit(solution)/shard_map/ppermute | solution.py:16
  136.4 8.5 %collective-permute-start.10 = (f32[1,128,128]{2,1,0:T(8,128)S(1)}, f32[1,128,128]{2,1,0:T(8,128)S(1)}, u32[]{:S(2)}, u32[]{:S(2)}) collective-permute-start(f32[1,128,128]{2,1,0:T(8,128)S(1)} %broadcast_multiply_fusion.6), channel_id=1, source_target_pairs={{0,128},{2,130},{4,132},{6,134},{8,136},{10,138},{12,140},{14,142}... | collective-permute-start | bytes 196616 | tf_op jit(solution)/shard_map/ppermute | solution.py:16
  140.7 1.1 copy-start.6
  155.2 0.8 copy-start.2
  160.2 0.8 copy-start.8

commit v2 on v1

v2 whole, which is shorter than its diff:
```python
import functools

import jax
import jax.numpy as jnp
from jax import lax
from jax.experimental import pallas as pl
from jax.experimental.pallas import tpu as pltpu
from jax.sharding import PartitionSpec as P

NS_STEPS = 5
ROUND_BITS = 2


highest = lax.Precision.HIGHEST


def from_xor(block, axis, mask):
    count = lax.axis_size(axis)
    route = [(low, low ^ mask) for low in range(count) if low ^ mask < count]
    return lax.ppermute(block, axis, route)


def mm(a, b):
    return jnp.dot(a, b, precision=highest, preferred_element_type=jnp.float32)


def gram(a):
    return lax.dot_general(a, a, (((0,), (0,)), ((), ())), precision=highest, preferred_element_type=jnp.float32)


def factor_nodes(nodes):
    width = nodes[0][0].shape[1]
    rows = lax.broadcasted_iota(jnp.int32, (width, width), 0)
    cols = lax.broadcasted_iota(jnp.int32, (width, width), 1)
    diag = rows == cols
    identity = jnp.where(diag, 1.0, 0.0).astype(jnp.float32)
    grams = []
    for parts in nodes:
        g = gram(parts[0])
        for part in parts[1:]:
            g = g + gram(part)
        grams.append(g)
    scales = [jnp.sum(jnp.where(diag, g, 0.0), keepdims=True) + 1e-06 for g in grams]
    roots = [g / c for g, c in zip(grams, scales)]
    inverses = [identity for _ in nodes]
    for _ in range(NS_STEPS):
        middles = [1.5 * identity - 0.5 * mm(w, y) for w, y in zip(inverses, roots)]
        roots, inverses = (
            [mm(y, m) for y, m in zip(roots, middles)],
            [mm(m, w) for m, w in zip(middles, inverses)],
        )
    results = []
    for parts, c, y, w in zip(nodes, scales, roots, inverses):
        s = jnp.sqrt(c)
        results.append(([mm(part, w) / s for part in parts], y * s))
    return results


def pair_levels(factors, levels, store):
    for level in range(levels):
        nodes = [[factors[2 * i], factors[2 * i + 1]] for i in range(len(factors) // 2)]
        results = factor_nodes(nodes)
        for i, (q_parts, _) in enumerate(results):
            store(level, i, q_parts)
        factors = [r for _, r in results]
    return factors


def local_kernel(slot_ref, z_ref, basis_ref, transfer_ref, top_ref):
    leaf_count = z_ref.shape[0]
    width = z_ref.shape[2]
    results = factor_nodes([[z_ref[i]] for i in range(leaf_count)])
    for i, (q_parts, _) in enumerate(results):
        basis_ref[i] = q_parts[0]
    triangles = [r for _, r in results]
    factors = []
    for j in range(leaf_count):
        pick = slot_ref[0, j]
        chosen = triangles[0]
        for i in range(1, leaf_count):
            chosen = jnp.where(pick == i, triangles[i], chosen)
        factors.append(chosen)
    offsets = []
    count = leaf_count
    total = 0
    while count > 1:
        count //= 2
        offsets.append(total)
        total += count

    def store(level, i, q_parts):
        for p, part in enumerate(q_parts):
            transfer_ref[offsets[level] + i, p * width:(p + 1) * width, :] = part

    factors = pair_levels(factors, len(offsets), store)
    top_ref[0] = factors[0]


def round_kernel(group_ref, *out_refs):
    members = group_ref.shape[0]
    width = group_ref.shape[2]
    levels = members.bit_length() - 1
    transfer_refs, top_ref = out_refs[:levels], out_refs[levels]

    def store(level, i, q_parts):
        for p, part in enumerate(q_parts):
            transfer_refs[level][i, p * width:(p + 1) * width, :] = part

    factors = pair_levels([group_ref[i] for i in range(members)], levels, store)
    top_ref[0] = factors[0]


def local_call(leaf_slot, sketched):
    leaf_count, rows, width = sketched.shape
    levels = leaf_count.bit_length() - 1
    vmem = pltpu.MemorySpace.VMEM
    return pl.pallas_call(
        local_kernel,
        out_shape=(
            jax.ShapeDtypeStruct((leaf_count, rows, width), jnp.float32),
            jax.ShapeDtypeStruct((leaf_count - 1, 2 * width, width), jnp.float32),
            jax.ShapeDtypeStruct((1, width, width), jnp.float32),
        ),
        in_specs=[pl.BlockSpec(memory_space=pltpu.MemorySpace.SMEM), pl.BlockSpec(memory_space=vmem)],
        out_specs=tuple(pl.BlockSpec(memory_space=vmem) for _ in range(3)),
    )(leaf_slot, sketched)


def round_call(group):
    members, width, _ = group.shape
    levels = members.bit_length() - 1
    vmem = pltpu.MemorySpace.VMEM
    shapes = [jax.ShapeDtypeStruct((members >> (level + 1), 2 * width, width), jnp.float32) for level in range(levels)]
    shapes.append(jax.ShapeDtypeStruct((1, width, width), jnp.float32))
    return pl.pallas_call(
        round_kernel,
        out_shape=tuple(shapes),
        in_specs=[pl.BlockSpec(memory_space=vmem)],
        out_specs=tuple(pl.BlockSpec(memory_space=vmem) for _ in shapes),
    )(group)


def body(samples, sketch, leaf_slot):
    columns = sketch.shape[1]
    leaf_count = leaf_slot.shape[1]
    partial_value = jnp.dot(samples, sketch, precision=highest).reshape(leaf_count, -1, columns)
    sketched = partial_value + from_xor(partial_value, "samp", 1)
    leaf_basis, local_transfer, factors = local_call(leaf_slot, sketched)
    position = lax.axis_index("clus")
    tree_depth = lax.axis_size("clus").bit_length() - 1
    top_out = jnp.zeros((1, 2 * columns, columns), jnp.float32)
    low_bit = 0
    while low_bit < tree_depth:
        width = min(ROUND_BITS, tree_depth - low_bit)
        members = 1 << width
        member = (position >> low_bit) & (members - 1)
        received = [factors] + [from_xor(factors, "clus", j << low_bit) for j in range(1, members)]
        received = jnp.concatenate(received, axis=0)
        slots = jnp.arange(members, dtype=jnp.int32) ^ member
        group = jnp.take(received, slots, axis=0)
        outs = round_call(group)
        for level in range(width):
            transfer = outs[level]
            level_bit = low_bit + level
            mine = lax.dynamic_index_in_dim(transfer, member >> (level + 1), 0, keepdims=True)
            owned = position % (2 << level_bit) == 1 << level_bit
            top_out = jnp.where(owned, mine, top_out)
        factors = outs[width]
        low_bit += width
    return (leaf_basis.reshape(-1, columns), local_transfer, top_out, factors[0])


def solution(mesh):
    return jax.shard_map(
        body,
        mesh=mesh,
        in_specs=(P("clus", "samp"), P("samp", None), P("clus", None)),
        out_specs=(P("clus", None), P("clus", None, None), P("clus", None, None), P()),
        check_vma=False,
    )
```

time: 164 us -> 134 us (0.82)
  matrix products: 72 us -> 1.4 us
  Pallas kernels: 0 us -> 44.5 us
  local copies, waits for them, and re-layouts: 16.3 us -> 3.33 us
  waiting for transfers between devices: 7.97 us -> 19.3 us
  other arithmetic: 3.51 us -> 9.18 us
  between operations: 5.12 us -> 1.08 us
  loops' own time: 2.76 us -> 0 us
    dot_general x187 -> x0, matrix products: 70.7 us -> none  [the longest x55 19.8 us: newton_step(): jnp.einsum('mkl,mlj->mkj', root, middle, precision=highest)]
    pallas_call x0 -> x5, Pallas kernels: none -> 44.5 us  [the longest x4 31.9 us: round_call(): pl.pallas_call(round_kernel, out_shape=tuple(shapes), in_specs=[pl.BlockS...]
    ppermute x13, waiting for transfers between devices: 7.97 us -> 19.3 us  [from_xor(): return lax.ppermute(block, axis, route)]
    unnamed x39 -> x14, local copies, waits for them, and re-layouts: 8.71 us -> 1.06 us
    concatenate x4, other arithmetic: 0.08 us -> 3.43 us  [body(): received = jnp.concatenate(received, axis=0)]
    select_n x8, other arithmetic: 0.38 us -> 3.2 us  [body(): group = jnp.take(received, slots, axis=0)]
    another operation x11 -> x0, loops' own time: 2.76 us -> none  [factor(): lax.fori_loop(0, NS_STEPS, newton_step, (start_root, start_inverse))]
    dynamic_slice x4 -> x0, local copies, waits for them, and re-layouts: 2.59 us -> none  [body(): lax.dynamic_index_in_dim(transfer, member >> level + 1, 0, keepdims=True)]
  transfers between devices with their start and end apart: 13 -> 13, of which waited for: 5 -> 7; matrix products, arithmetic and copies ran while one was open for 5% -> 0% of each run, Pallas kernels for 0% -> 0%
where the time goes in v2:
time: 134 us; the launch traced here: 133 us
  starting transfers between devices  54.5 us (41%)
  Pallas kernels  44.5 us (33%)
  waiting for transfers between devices  19.3 us (14%)
  other arithmetic  9.18 us (7%)
  local copies, waits for them, and re-layouts  3.33 us (2%)
  matrix products  1.4 us (1%)
    ppermute x13, starting transfers between devices, from_xor(): return lax.ppermute(block, axis, route)  54.5 us
    pallas_call x4, Pallas kernels, round_call(): pl.pallas_call(round_kernel, out_shape=tuple(shapes), in_specs=[pl.BlockS...  31.9 us
    ppermute x13, waiting for transfers between devices, from_xor(): return lax.ppermute(block, axis, route)  19.3 us
    pallas_call x1, Pallas kernels, local_call(): pl.pallas_call(local_kernel, out_shape=(jax.ShapeDtypeStruct((leaf_count,...  12.6 us
    concatenate x4, other arithmetic, body(): received = jnp.concatenate(received, axis=0)  3.43 us
    select_n x8, other arithmetic, body(): group = jnp.take(received, slots, axis=0)  3.2 us
  transfers between devices with their start and end apart: 13, of which 7 were waited for; matrix products, arithmetic and copies ran while one was open for 0% of the time, Pallas kernels for 0%

profile of v2, /device:TPU:8, one launch (start us, length us, event | category | flops | bytes accessed | tf_op | source)
XLA Modules:
  0.0 133.3 jit_solution(14569647802681572051)
XLA Ops:
  0.6 1.0 copy-done
  1.7 1.4 %fusion = f32[1024,128]{1,0:T(8,128)S(1)} fusion(f32[1024,128]{1,0:T(8,128)S(1)} %copy-done, f32[128,128]{1,0:T(8,128)} %param.6), kind=kOutput, calls=%fused_computation.25 | convolution fusion | flops 201326592 | bytes 1114112 | tf_op jit(solution)/shard_map/dot_general | solution.py:146
  3.1 1.9 %collective-permute-start = (f32[4,256,128]{2,1,0:T(8,128)S(1)}, f32[4,256,128]{2,1,0:T(8,128)S(1)}, u32[]{:S(2)}, u32[]{:S(2)}) collective-permute-start(f32[4,256,128]{2,1,0:T(8,128)S(1)} %bitcast.5), channel_id=1, source_target_pairs={{0,1},{1,0},{2,3},{3,2},{4,5},{5,4},{6,7},{7,6},{8,9},{9,8},{10,11... | collective-permute-start | bytes 1572872 | tf_op jit(solution)/shard_map/ppermute | solution.py:20
  5.2 1.7 %collective-permute-done = f32[4,256,128]{2,1,0:T(8,128)S(1)} collective-permute-done((f32[4,256,128]{2,1,0:T(8,128)S(1)}, f32[4,256,128]{2,1,0:T(8,128)S(1)}, u32[]{:S(2)}, u32[]{:S(2)}) %collective-permute-start) | collective-permute-done | bytes 524320 | tf_op jit(solution)/shard_map/ppermute | solution.py:20
  6.9 0.9 add.49.z_ref
  7.8 12.6 %shard_map.66 = (f32[4,256,128]{2,1,0:T(8,128)}, f32[3,256,128]{2,1,0:T(8,128)}, f32[1,128,128]{2,1,0:T(8,128)}) custom-call(s32[1,4]{1,0:T(1,128)} %slot_ref.1, f32[4,256,128]{2,1,0:T(8,128)} %add.49.z_ref), custom_call_target="tpu_custom_call" | custom-call | tf_op jit(solution)/shard_map/pallas_call | solution.py:117
  20.3 4.7 %collective-permute-start.3 = (f32[1,128,128]{2,1,0:T(8,128)}, f32[1,128,128]{2,1,0:T(8,128)S(1)}, u32[]{:S(2)}, u32[]{:S(2)}) collective-permute-start(f32[1,128,128]{2,1,0:T(8,128)} %get-tuple-element.22), channel_id=1, source_target_pairs={{0,6},{2,4},{4,2},{6,0},{8,14},{10,12},{12,10},{14,8},{16,22},{18,... | collective-permute-start | bytes 196616 | tf_op jit(solution)/shard_map/ppermute | solution.py:20
  25.0 2.7 %collective-permute-start.2 = (f32[1,128,128]{2,1,0:T(8,128)}, f32[1,128,128]{2,1,0:T(8,128)S(1)}, u32[]{:S(2)}, u32[]{:S(2)}) collective-permute-start(f32[1,128,128]{2,1,0:T(8,128)} %get-tuple-element.22), channel_id=1, source_target_pairs={{0,4},{2,6},{4,0},{6,2},{8,12},{10,14},{12,8},{14,10},{16,20},{18,... | collective-permute-start | bytes 196616 | tf_op jit(solution)/shard_map/ppermute | solution.py:20
  27.7 2.6 %collective-permute-start.1 = (f32[1,128,128]{2,1,0:T(8,128)}, f32[1,128,128]{2,1,0:T(8,128)S(1)}, u32[]{:S(2)}, u32[]{:S(2)}) collective-permute-start(f32[1,128,128]{2,1,0:T(8,128)} %get-tuple-element.22), channel_id=1, source_target_pairs={{0,2},{2,0},{4,6},{6,4},{8,10},{10,8},{12,14},{14,12},{16,18},{18,... | collective-permute-start | bytes 196616 | tf_op jit(solution)/shard_map/ppermute | solution.py:20
  30.4 2.5 %collective-permute-done.2 = f32[1,128,128]{2,1,0:T(8,128)S(1)} collective-permute-done((f32[1,128,128]{2,1,0:T(8,128)}, f32[1,128,128]{2,1,0:T(8,128)S(1)}, u32[]{:S(2)}, u32[]{:S(2)}) %collective-permute-start.2) | collective-permute-done | bytes 65568 | tf_op jit(solution)/shard_map/ppermute | solution.py:20
  32.9 1.2 collective-permute-done.1
  34.1 0.9 pad_maximum_fusion
  36.3 8.0 %shard_map.67 = (f32[2,256,128]{2,1,0:T(8,128)}, f32[1,256,128]{2,1,0:T(8,128)}, f32[1,128,128]{2,1,0:T(8,128)}) custom-call(f32[4,128,128]{2,1,0:T(8,128)} %broadcast_select_fusion.3.group_ref), custom_call_target="tpu_custom_call" | custom-call | tf_op jit(solution)/shard_map/pallas_call | solution.py:135
  44.3 3.5 %collective-permute-start.6 = (f32[1,128,128]{2,1,0:T(8,128)}, f32[1,128,128]{2,1,0:T(8,128)S(1)}, u32[]{:S(2)}, u32[]{:S(2)}) collective-permute-start(f32[1,128,128]{2,1,0:T(8,128)} %get-tuple-element.23), channel_id=1, source_target_pairs={{0,24},{2,26},{4,28},{6,30},{8,16},{10,18},{12,20},{14,22},{16,8},... | collective-permute-start | bytes 196616 | tf_op jit(solution)/shard_map/ppermute | solution.py:20
  47.8 7.0 %collective-permute-start.5 = (f32[1,128,128]{2,1,0:T(8,128)}, f32[1,128,128]{2,1,0:T(8,128)S(1)}, u32[]{:S(2)}, u32[]{:S(2)}) collective-permute-start(f32[1,128,128]{2,1,0:T(8,128)} %get-tuple-element.23), channel_id=1, source_target_pairs={{0,16},{2,18},{4,20},{6,22},{8,24},{10,26},{12,28},{14,30},{16,0},... | collective-permute-start | bytes 196616 | tf_op jit(solution)/shard_map/ppermute | solution.py:20
  54.8 1.9 %collective-permute-start.4 = (f32[1,128,128]{2,1,0:T(8,128)}, f32[1,128,128]{2,1,0:T(8,128)S(1)}, u32[]{:S(2)}, u32[]{:S(2)}) collective-permute-start(f32[1,128,128]{2,1,0:T(8,128)} %get-tuple-element.23), channel_id=1, source_target_pairs={{0,8},{2,10},{4,12},{6,14},{8,0},{10,2},{12,4},{14,6},{16,24},{18,... | collective-permute-start | bytes 196616 | tf_op jit(solution)/shard_map/ppermute | solution.py:20
  56.8 1.1 collective-permute-done.5
  57.9 3.3 %collective-permute-done.4 = f32[1,128,128]{2,1,0:T(8,128)S(1)} collective-permute-done((f32[1,128,128]{2,1,0:T(8,128)}, f32[1,128,128]{2,1,0:T(8,128)S(1)}, u32[]{:S(2)}, u32[]{:S(2)}) %collective-permute-start.4) | collective-permute-done | bytes 65568 | tf_op jit(solution)/shard_map/ppermute | solution.py:20
  61.2 0.9 pad_maximum_fusion.1
  63.4 8.0 %shard_map.68 = (f32[2,256,128]{2,1,0:T(8,128)}, f32[1,256,128]{2,1,0:T(8,128)}, f32[1,128,128]{2,1,0:T(8,128)}) custom-call(f32[4,128,128]{2,1,0:T(8,128)} %broadcast_select_fusion.2.group_ref), custom_call_target="tpu_custom_call" | custom-call | tf_op jit(solution)/shard_map/pallas_call | solution.py:135
  71.4 5.6 %collective-permute-start.9 = (f32[1,128,128]{2,1,0:T(8,128)}, f32[1,128,128]{2,1,0:T(8,128)S(1)}, u32[]{:S(2)}, u32[]{:S(2)}) collective-permute-start(f32[1,128,128]{2,1,0:T(8,128)} %get-tuple-element.24), channel_id=1, source_target_pairs={{0,96},{2,98},{4,100},{6,102},{8,104},{10,106},{12,108},{14,110},{... | collective-permute-start | bytes 196616 | tf_op jit(solution)/shard_map/ppermute | solution.py:20
  77.0 1.9 %collective-permute-start.8 = (f32[1,128,128]{2,1,0:T(8,128)}, f32[1,128,128]{2,1,0:T(8,128)S(1)}, u32[]{:S(2)}, u32[]{:S(2)}) collective-permute-start(f32[1,128,128]{2,1,0:T(8,128)} %get-tuple-element.24), channel_id=1, source_target_pairs={{0,64},{2,66},{4,68},{6,70},{8,72},{10,74},{12,76},{14,78},{16,80}... | collective-permute-start | bytes 196616 | tf_op jit(solution)/shard_map/ppermute | solution.py:20
  79.0 5.8 %collective-permute-start.7 = (f32[1,128,128]{2,1,0:T(8,128)}, f32[1,128,128]{2,1,0:T(8,128)S(1)}, u32[]{:S(2)}, u32[]{:S(2)}) collective-permute-start(f32[1,128,128]{2,1,0:T(8,128)} %get-tuple-element.24), channel_id=1, source_target_pairs={{0,32},{2,34},{4,36},{6,38},{8,40},{10,42},{12,44},{14,46},{16,48}... | collective-permute-start | bytes 196616 | tf_op jit(solution)/shard_map/ppermute | solution.py:20
  84.8 4.9 %collective-permute-done.7 = f32[1,128,128]{2,1,0:T(8,128)S(1)} collective-permute-done((f32[1,128,128]{2,1,0:T(8,128)}, f32[1,128,128]{2,1,0:T(8,128)S(1)}, u32[]{:S(2)}, u32[]{:S(2)}) %collective-permute-start.7) | collective-permute-done | bytes 65568 | tf_op jit(solution)/shard_map/ppermute | solution.py:20
  91.9 8.0 %shard_map.69 = (f32[2,256,128]{2,1,0:T(8,128)}, f32[1,256,128]{2,1,0:T(8,128)}, f32[1,128,128]{2,1,0:T(8,128)}) custom-call(f32[4,128,128]{2,1,0:T(8,128)} %broadcast_select_fusion.1.group_ref), custom_call_target="tpu_custom_call" | custom-call | tf_op jit(solution)/shard_map/pallas_call | solution.py:135
  99.8 10.7 %collective-permute-start.12 = (f32[1,128,128]{2,1,0:T(8,128)}, f32[1,128,128]{2,1,0:T(8,128)S(1)}, u32[]{:S(2)}, u32[]{:S(2)}) collective-permute-start(f32[1,128,128]{2,1,0:T(8,128)} %get-tuple-element.25), channel_id=1, source_target_pairs={{0,384},{2,386},{4,388},{6,390},{8,392},{10,394},{12,396},{14,398}... | collective-permute-start | bytes 196616 | tf_op jit(solution)/shard_map/ppermute | solution.py:20
  110.5 1.9 %collective-permute-start.11 = (f32[1,128,128]{2,1,0:T(8,128)}, f32[1,128,128]{2,1,0:T(8,128)S(1)}, u32[]{:S(2)}, u32[]{:S(2)}) collective-permute-start(f32[1,128,128]{2,1,0:T(8,128)} %get-tuple-element.25), channel_id=1, source_target_pairs={{0,256},{2,258},{4,260},{6,262},{8,264},{10,266},{12,268},{14,270}... | collective-permute-start | bytes 196616 | tf_op jit(solution)/shard_map/ppermute | solution.py:20
  112.5 4.3 %collective-permute-start.10 = (f32[1,128,128]{2,1,0:T(8,128)}, f32[1,128,128]{2,1,0:T(8,128)S(1)}, u32[]{:S(2)}, u32[]{:S(2)}) collective-permute-start(f32[1,128,128]{2,1,0:T(8,128)} %get-tuple-element.25), channel_id=1, source_target_pairs={{0,128},{2,130},{4,132},{6,134},{8,136},{10,138},{12,140},{14,142}... | collective-permute-start | bytes 196616 | tf_op jit(solution)/shard_map/ppermute | solution.py:20
  116.8 4.6 %collective-permute-done.11 = f32[1,128,128]{2,1,0:T(8,128)S(1)} collective-permute-done((f32[1,128,128]{2,1,0:T(8,128)}, f32[1,128,128]{2,1,0:T(8,128)S(1)}, u32[]{:S(2)}, u32[]{:S(2)}) %collective-permute-start.11) | collective-permute-done | bytes 65568 | tf_op jit(solution)/shard_map/ppermute | solution.py:20
  121.4 0.9 pad_maximum_fusion.3
  123.6 8.0 %shard_map.70 = (f32[2,256,128]{2,1,0:T(8,128)}, f32[1,256,128]{2,1,0:T(8,128)}, f32[1,128,128]{2,1,0:T(8,128)}) custom-call(f32[4,128,128]{2,1,0:T(8,128)} %broadcast_select_fusion.group_ref), custom_call_target="tpu_custom_call" | custom-call | tf_op jit(solution)/shard_map/pallas_call | solution.py:135
  131.7 1.6 %select_select_fusion = f32[1,256,128]{2,1,0:T(8,128)} fusion(f32[1,256,128]{2,1,0:T(8,128)} %get-tuple-element.26, f32[1,256,128]{2,1,0:T(8,128)S(1)} %copy-done.3, f32[1,256,128]{2,1,0:T(8,128)S(1)} %copy-done.2, f32[1,256,128]{2,1,0:T(8,128)S(1)} %copy-done.1, f32[2,256,128]{2,1,0:T(8,128)S(1)} %copy-done.4, s32[]{:T(128)S(6)} %select_n.129, ...), kind=kLoop, calls=%fused_computation.12 | loop fusion | flops 262144 | bytes 1179672 | tf_op jit(solution)/shard_map/jit(_where)/select_n | solution.py:167
  (40 shorter events, 6.4 us)
Async XLA Ops:
  0.6 1.0 copy-start
  3.1 3.8 %collective-permute-start = (f32[4,256,128]{2,1,0:T(8,128)S(1)}, f32[4,256,128]{2,1,0:T(8,128)S(1)}, u32[]{:S(2)}, u32[]{:S(2)}) collective-permute-start(f32[4,256,128]{2,1,0:T(8,128)S(1)} %bitcast.5), channel_id=1, source_target_pairs={{0,1},{1,0},{2,3},{3,2},{4,5},{5,4},{6,7},{7,6},{8,9},{9,8},{10,11... | collective-permute-start | bytes 1572872 | tf_op jit(solution)/shard_map/ppermute | solution.py:20
  20.3 10.0 %collective-permute-start.3 = (f32[1,128,128]{2,1,0:T(8,128)}, f32[1,128,128]{2,1,0:T(8,128)S(1)}, u32[]{:S(2)}, u32[]{:S(2)}) collective-permute-start(f32[1,128,128]{2,1,0:T(8,128)} %get-tuple-element.22), channel_id=1, source_target_pairs={{0,6},{2,4},{4,2},{6,0},{8,14},{10,12},{12,10},{14,8},{16,22},{18,... | collective-permute-start | bytes 196616 | tf_op jit(solution)/shard_map/ppermute | solution.py:20
  25.0 7.9 %collective-permute-start.2 = (f32[1,128,128]{2,1,0:T(8,128)}, f32[1,128,128]{2,1,0:T(8,128)S(1)}, u32[]{:S(2)}, u32[]{:S(2)}) collective-permute-start(f32[1,128,128]{2,1,0:T(8,128)} %get-tuple-element.22), channel_id=1, source_target_pairs={{0,4},{2,6},{4,0},{6,2},{8,12},{10,14},{12,8},{14,10},{16,20},{18,... | collective-permute-start | bytes 196616 | tf_op jit(solution)/shard_map/ppermute | solution.py:20
  27.7 6.4 %collective-permute-start.1 = (f32[1,128,128]{2,1,0:T(8,128)}, f32[1,128,128]{2,1,0:T(8,128)S(1)}, u32[]{:S(2)}, u32[]{:S(2)}) collective-permute-start(f32[1,128,128]{2,1,0:T(8,128)} %get-tuple-element.22), channel_id=1, source_target_pairs={{0,2},{2,0},{4,6},{6,4},{8,10},{10,8},{12,14},{14,12},{16,18},{18,... | collective-permute-start | bytes 196616 | tf_op jit(solution)/shard_map/ppermute | solution.py:20
  44.3 12.5 %collective-permute-start.6 = (f32[1,128,128]{2,1,0:T(8,128)}, f32[1,128,128]{2,1,0:T(8,128)S(1)}, u32[]{:S(2)}, u32[]{:S(2)}) collective-permute-start(f32[1,128,128]{2,1,0:T(8,128)} %get-tuple-element.23), channel_id=1, source_target_pairs={{0,24},{2,26},{4,28},{6,30},{8,16},{10,18},{12,20},{14,22},{16,8},... | collective-permute-start | bytes 196616 | tf_op jit(solution)/shard_map/ppermute | solution.py:20
  47.8 10.1 %collective-permute-start.5 = (f32[1,128,128]{2,1,0:T(8,128)}, f32[1,128,128]{2,1,0:T(8,128)S(1)}, u32[]{:S(2)}, u32[]{:S(2)}) collective-permute-start(f32[1,128,128]{2,1,0:T(8,128)} %get-tuple-element.23), channel_id=1, source_target_pairs={{0,16},{2,18},{4,20},{6,22},{8,24},{10,26},{12,28},{14,30},{16,0},... | collective-permute-start | bytes 196616 | tf_op jit(solution)/shard_map/ppermute | solution.py:20
  54.8 6.4 %collective-permute-start.4 = (f32[1,128,128]{2,1,0:T(8,128)}, f32[1,128,128]{2,1,0:T(8,128)S(1)}, u32[]{:S(2)}, u32[]{:S(2)}) collective-permute-start(f32[1,128,128]{2,1,0:T(8,128)} %get-tuple-element.23), channel_id=1, source_target_pairs={{0,8},{2,10},{4,12},{6,14},{8,0},{10,2},{12,4},{14,6},{16,24},{18,... | collective-permute-start | bytes 196616 | tf_op jit(solution)/shard_map/ppermute | solution.py:20
  71.4 13.4 %collective-permute-start.9 = (f32[1,128,128]{2,1,0:T(8,128)}, f32[1,128,128]{2,1,0:T(8,128)S(1)}, u32[]{:S(2)}, u32[]{:S(2)}) collective-permute-start(f32[1,128,128]{2,1,0:T(8,128)} %get-tuple-element.24), channel_id=1, source_target_pairs={{0,96},{2,98},{4,100},{6,102},{8,104},{10,106},{12,108},{14,110},{... | collective-permute-start | bytes 196616 | tf_op jit(solution)/shard_map/ppermute | solution.py:20
  77.0 7.7 %collective-permute-start.8 = (f32[1,128,128]{2,1,0:T(8,128)}, f32[1,128,128]{2,1,0:T(8,128)S(1)}, u32[]{:S(2)}, u32[]{:S(2)}) collective-permute-start(f32[1,128,128]{2,1,0:T(8,128)} %get-tuple-element.24), channel_id=1, source_target_pairs={{0,64},{2,66},{4,68},{6,70},{8,72},{10,74},{12,76},{14,78},{16,80}... | collective-permute-start | bytes 196616 | tf_op jit(solution)/shard_map/ppermute | solution.py:20
  79.0 10.7 %collective-permute-start.7 = (f32[1,128,128]{2,1,0:T(8,128)}, f32[1,128,128]{2,1,0:T(8,128)S(1)}, u32[]{:S(2)}, u32[]{:S(2)}) collective-permute-start(f32[1,128,128]{2,1,0:T(8,128)} %get-tuple-element.24), channel_id=1, source_target_pairs={{0,32},{2,34},{4,36},{6,38},{8,40},{10,42},{12,44},{14,46},{16,48}... | collective-permute-start | bytes 196616 | tf_op jit(solution)/shard_map/ppermute | solution.py:20
  99.8 16.9 %collective-permute-start.12 = (f32[1,128,128]{2,1,0:T(8,128)}, f32[1,128,128]{2,1,0:T(8,128)S(1)}, u32[]{:S(2)}, u32[]{:S(2)}) collective-permute-start(f32[1,128,128]{2,1,0:T(8,128)} %get-tuple-element.25), channel_id=1, source_target_pairs={{0,384},{2,386},{4,388},{6,390},{8,392},{10,394},{12,396},{14,398}... | collective-permute-start | bytes 196616 | tf_op jit(solution)/shard_map/ppermute | solution.py:20
  110.5 10.9 %collective-permute-start.11 = (f32[1,128,128]{2,1,0:T(8,128)}, f32[1,128,128]{2,1,0:T(8,128)S(1)}, u32[]{:S(2)}, u32[]{:S(2)}) collective-permute-start(f32[1,128,128]{2,1,0:T(8,128)} %get-tuple-element.25), channel_id=1, source_target_pairs={{0,256},{2,258},{4,260},{6,262},{8,264},{10,266},{12,268},{14,270}... | collective-permute-start | bytes 196616 | tf_op jit(solution)/shard_map/ppermute | solution.py:20
  112.5 8.9 %collective-permute-start.10 = (f32[1,128,128]{2,1,0:T(8,128)}, f32[1,128,128]{2,1,0:T(8,128)S(1)}, u32[]{:S(2)}, u32[]{:S(2)}) collective-permute-start(f32[1,128,128]{2,1,0:T(8,128)} %get-tuple-element.25), channel_id=1, source_target_pairs={{0,128},{2,130},{4,132},{6,134},{8,136},{10,138},{12,140},{14,142}... | collective-permute-start | bytes 196616 | tf_op jit(solution)/shard_map/ppermute | solution.py:20
  122.2 9.4 %copy-start.5 = (f32[2,256,128]{2,1,0:T(8,128)S(1)}, f32[2,256,128]{2,1,0:T(8,128)}, u32[]{:S(2)}) copy-start(f32[2,256,128]{2,1,0:T(8,128)} %get-tuple-element.31) | copy-start | bytes 786436
  122.3 9.4 %copy-start.6 = (f32[2,256,128]{2,1,0:T(8,128)S(1)}, f32[2,256,128]{2,1,0:T(8,128)}, u32[]{:S(2)}) copy-start(f32[2,256,128]{2,1,0:T(8,128)} %get-tuple-element.29) | copy-start | bytes 786436
  122.8 8.8 %copy-start.3 = (f32[1,256,128]{2,1,0:T(8,128)S(1)}, f32[1,256,128]{2,1,0:T(8,128)}, u32[]{:S(2)}) copy-start(f32[1,256,128]{2,1,0:T(8,128)} %get-tuple-element.28) | copy-start | bytes 393220
  122.8 8.8 %copy-start.4 = (f32[2,256,128]{2,1,0:T(8,128)S(1)}, f32[2,256,128]{2,1,0:T(8,128)}, u32[]{:S(2)}) copy-start(f32[2,256,128]{2,1,0:T(8,128)} %get-tuple-element.33) | copy-start | bytes 786436
  123.6 8.0 %copy-start.1 = (f32[1,256,128]{2,1,0:T(8,128)S(1)}, f32[1,256,128]{2,1,0:T(8,128)}, u32[]{:S(2)}) copy-start(f32[1,256,128]{2,1,0:T(8,128)} %get-tuple-element.32) | copy-start | bytes 393220
  123.6 8.0 %copy-start.2 = (f32[1,256,128]{2,1,0:T(8,128)S(1)}, f32[1,256,128]{2,1,0:T(8,128)}, u32[]{:S(2)}) copy-start(f32[1,256,128]{2,1,0:T(8,128)} %get-tuple-element.30) | copy-start | bytes 393220

commit v3 on v2

v3 whole, which is shorter than its diff:
```python
import functools

import jax
import jax.numpy as jnp
from jax import lax
from jax.experimental import pallas as pl
from jax.experimental.pallas import tpu as pltpu
from jax.sharding import PartitionSpec as P

NS_STEPS = 5
ROUND_BITS = 2


highest = lax.Precision.HIGHEST


def from_xor(block, axis, mask):
    count = lax.axis_size(axis)
    route = [(low, low ^ mask) for low in range(count) if low ^ mask < count]
    return lax.ppermute(block, axis, route)


def mm(a, b):
    return jnp.dot(a, b, precision=highest, preferred_element_type=jnp.float32)


def gram(a):
    return lax.dot_general(a, a, (((0,), (0,)), ((), ())), precision=highest, preferred_element_type=jnp.float32)


def factor_nodes(nodes, keep_inverse=False):
    width = nodes[0][0].shape[1]
    rows = lax.broadcasted_iota(jnp.int32, (width, width), 0)
    cols = lax.broadcasted_iota(jnp.int32, (width, width), 1)
    diag = rows == cols
    identity = jnp.where(diag, 1.0, 0.0).astype(jnp.float32)
    grams = []
    for parts in nodes:
        g = gram(parts[0])
        for part in parts[1:]:
            g = g + gram(part)
        grams.append(g)
    scales = [jnp.sum(jnp.where(diag, g, 0.0), keepdims=True) + 1e-06 for g in grams]
    roots = [g / c for g, c in zip(grams, scales)]
    inverses = [identity for _ in nodes]
    for _ in range(NS_STEPS):
        middles = [1.5 * identity - 0.5 * mm(w, y) for w, y in zip(inverses, roots)]
        roots, inverses = (
            [mm(y, m) for y, m in zip(roots, middles)],
            [mm(m, w) for m, w in zip(middles, inverses)],
        )
    results = []
    for parts, c, y, w in zip(nodes, scales, roots, inverses):
        s = jnp.sqrt(c)
        if keep_inverse:
            results.append((w, y * s, s))
        else:
            results.append(([mm(part, w) / s for part in parts], y * s))
    return results


def pair_levels(factors, levels, store):
    for level in range(levels):
        nodes = [[factors[2 * i], factors[2 * i + 1]] for i in range(len(factors) // 2)]
        results = factor_nodes(nodes)
        for i, (q_parts, _) in enumerate(results):
            store(level, i, q_parts)
        factors = [r for _, r in results]
    return factors


def local_kernel(slot_ref, z_ref, other_ref, basis_ref, transfer_ref, top_ref):
    leaf_count = z_ref.shape[0]
    width = z_ref.shape[2]
    results = factor_nodes([[z_ref[i] + other_ref[i]] for i in range(leaf_count)])
    for i, (q_parts, _) in enumerate(results):
        basis_ref[i] = q_parts[0]
    triangles = [r for _, r in results]
    factors = []
    for j in range(leaf_count):
        pick = slot_ref[0, j]
        chosen = triangles[0]
        for i in range(1, leaf_count):
            chosen = jnp.where(pick == i, triangles[i], chosen)
        factors.append(chosen)
    offsets = []
    count = leaf_count
    total = 0
    while count > 1:
        count //= 2
        offsets.append(total)
        total += count

    def store(level, i, q_parts):
        for p, part in enumerate(q_parts):
            transfer_ref[offsets[level] + i, p * width:(p + 1) * width, :] = part

    factors = pair_levels(factors, len(offsets), store)
    top_ref[0] = factors[0]


def round_kernel(low_bit, own_ref, *refs):
    received_refs, top_in_ref, top_ref, next_ref = refs[:-3], refs[-3], refs[-2], refs[-1]
    width = own_ref.shape[2]
    levels = len(received_refs)
    members = 1 << levels
    position = lax.axis_index("clus")
    member = (position >> low_bit) & (members - 1)
    arrived = [own_ref[0]]
    for received_ref in received_refs:
        arrived += [received_ref[t] for t in range(received_ref.shape[0])]
    group = []
    for p in range(members):
        chosen = arrived[p]
        for t in range(members):
            if t != p:
                chosen = jnp.where(member == p ^ t, arrived[t], chosen)
        group.append(chosen)
    top = top_in_ref[0]
    factors = group
    for level in range(levels):
        nodes = [[factors[2 * i], factors[2 * i + 1]] for i in range(len(factors) // 2)]
        results = factor_nodes(nodes, keep_inverse=True)
        node = member >> (level + 1)
        mine_low, mine_high, mine_inverse, mine_scale = nodes[0][0], nodes[0][1], results[0][0], results[0][2]
        for i in range(1, len(nodes)):
            pick = node == i
            mine_low = jnp.where(pick, nodes[i][0], mine_low)
            mine_high = jnp.where(pick, nodes[i][1], mine_high)
            mine_inverse = jnp.where(pick, results[i][0], mine_inverse)
            mine_scale = jnp.where(pick, results[i][2], mine_scale)
        level_bit = low_bit + level
        owned = position % (2 << level_bit) == 1 << level_bit
        transfer = jnp.concatenate([mm(mine_low, mine_inverse) / mine_scale, mm(mine_high, mine_inverse) / mine_scale], axis=0)
        top = jnp.where(owned, transfer, top)
        factors = [r for _, r, _ in results]
    top_ref[0] = top
    next_ref[0] = factors[0]


def local_call(leaf_slot, partial_value, other_value):
    leaf_count, rows, width = partial_value.shape
    vmem = pltpu.MemorySpace.VMEM
    return pl.pallas_call(
        local_kernel,
        out_shape=(
            jax.ShapeDtypeStruct((leaf_count, rows, width), jnp.float32),
            jax.ShapeDtypeStruct((leaf_count - 1, 2 * width, width), jnp.float32),
            jax.ShapeDtypeStruct((1, width, width), jnp.float32),
        ),
        in_specs=[pl.BlockSpec(memory_space=pltpu.MemorySpace.SMEM), pl.BlockSpec(memory_space=vmem), pl.BlockSpec(memory_space=vmem)],
        out_specs=tuple(pl.BlockSpec(memory_space=vmem) for _ in range(3)),
    )(leaf_slot, partial_value, other_value)


def round_call(low_bit, own, received, top_in):
    width = own.shape[2]
    vmem = pltpu.MemorySpace.VMEM
    return pl.pallas_call(
        functools.partial(round_kernel, low_bit),
        out_shape=(
            jax.ShapeDtypeStruct(top_in.shape, jnp.float32),
            jax.ShapeDtypeStruct((1, width, width), jnp.float32),
        ),
        in_specs=[pl.BlockSpec(memory_space=vmem) for _ in range(len(received) + 2)],
        out_specs=(pl.BlockSpec(memory_space=vmem), pl.BlockSpec(memory_space=vmem)),
    )(own, *received, top_in)


def body(samples, sketch, leaf_slot):
    columns = sketch.shape[1]
    leaf_count = leaf_slot.shape[1]
    partial_value = jnp.dot(samples, sketch, precision=highest).reshape(leaf_count, -1, columns)
    other_value = from_xor(partial_value, "samp", 1)
    leaf_basis, local_transfer, factors = local_call(leaf_slot, partial_value, other_value)
    tree_depth = lax.axis_size("clus").bit_length() - 1
    top_out = jnp.zeros((1, 2 * columns, columns), jnp.float32)
    low_bit = 0
    while low_bit < tree_depth:
        width = min(ROUND_BITS, tree_depth - low_bit)
        gathered = factors
        received = []
        for step in range(width):
            arrived = from_xor(gathered, "clus", 1 << (low_bit + step))
            received.append(arrived)
            if step + 1 < width:
                gathered = jnp.concatenate([gathered, arrived], axis=0)
        top_out, factors = round_call(low_bit, factors, received, top_out)
        low_bit += width
    return (leaf_basis.reshape(-1, columns), local_transfer, top_out, factors[0])


def solution(mesh):
    return jax.shard_map(
        body,
        mesh=mesh,
        in_specs=(P("clus", "samp"), P("samp", None), P("clus", None)),
        out_specs=(P("clus", None), P("clus", None, None), P("clus", None, None), P()),
        check_vma=False,
    )
```

time: 134 us -> 130 us (0.970)
  the two profiles are of different devices: /device:TPU:8 before, /device:TPU:34 now
where the time goes in v3:
time: 130 us; the launch traced here: 129 us
  Pallas kernels  45 us (35%)
  starting transfers between devices  40.3 us (31%)
  waiting for transfers between devices  34 us (26%)
  local copies, waits for them, and re-layouts  4.53 us (3%)
  other arithmetic  3.49 us (3%)
  matrix products  1.4 us (1%)
    ppermute x9, starting transfers between devices, from_xor(): return lax.ppermute(block, axis, route)  40.3 us
    ppermute x9, waiting for transfers between devices, from_xor(): return lax.ppermute(block, axis, route)  34 us
    pallas_call x4, Pallas kernels, round_call(): pl.pallas_call(functools.partial(round_kernel, low_bit), out_shape=(jax.S...  32.2 us
    pallas_call x1, Pallas kernels, local_call(): pl.pallas_call(local_kernel, out_shape=(jax.ShapeDtypeStruct((leaf_count,...  12.7 us
    unnamed x22, local copies, waits for them, and re-layouts  3.84 us
    concatenate x4, other arithmetic, body(): gathered = jnp.concatenate([gathered, arrived], axis=0)  3.49 us
  transfers between devices with their start and end apart: 9, of which 9 were waited for; matrix products, arithmetic and copies ran while one was open for 0% of the time, Pallas kernels for 0%

profile of v3, /device:TPU:34, one launch (start us, length us, event | category | flops | bytes accessed | tf_op | source)
XLA Modules:
  0.0 129.5 jit_solution(8950369199683900524)
XLA Ops:
  0.6 1.0 copy-done
  1.7 1.4 %fusion = f32[1024,128]{1,0:T(8,128)S(1)} fusion(f32[1024,128]{1,0:T(8,128)S(1)} %copy-done, f32[128,128]{1,0:T(8,128)} %param.4), kind=kOutput, calls=%fused_computation.4 | convolution fusion | flops 201326592 | bytes 1114112 | tf_op jit(solution)/shard_map/dot_general | solution.py:173
  3.1 1.9 %collective-permute-start = (f32[4,256,128]{2,1,0:T(8,128)S(1)}, f32[4,256,128]{2,1,0:T(8,128)S(1)}, u32[]{:S(2)}, u32[]{:S(2)}) collective-permute-start(f32[4,256,128]{2,1,0:T(8,128)S(1)} %bitcast.5), channel_id=1, source_target_pairs={{0,1},{1,0},{2,3},{3,2},{4,5},{5,4},{6,7},{7,6},{8,9},{9,8},{10,11... | collective-permute-start | bytes 1572872 | tf_op jit(solution)/shard_map/ppermute | solution.py:20
  5.0 1.9 %collective-permute-done.other_ref = f32[4,256,128]{2,1,0:T(8,128)S(1)} collective-permute-done((f32[4,256,128]{2,1,0:T(8,128)S(1)}, f32[4,256,128]{2,1,0:T(8,128)S(1)}, u32[]{:S(2)}, u32[]{:S(2)}) %collective-permute-start) | collective-permute-done | bytes 524320 | tf_op jit(solution)/shard_map/ppermute | solution.py:20
  6.9 0.8 copy-done.2
  7.7 12.7 %shard_map.66 = (f32[4,256,128]{2,1,0:T(8,128)}, f32[3,256,128]{2,1,0:T(8,128)}, f32[1,128,128]{2,1,0:T(8,128)}) custom-call(s32[1,4]{1,0:T(1,128)} %slot_ref.1, f32[4,256,128]{2,1,0:T(8,128)} %bitcast.6, f32[4,256,128]{2,1,0:T(8,128)} %copy-done.2), custom_call_target="tpu_custom_call" | custom-call | tf_op jit(solution)/shard_map/pallas_call | solution.py:144
  20.4 2.4 %collective-permute-start.1 = (f32[1,128,128]{2,1,0:T(8,128)}, f32[1,128,128]{2,1,0:T(8,128)S(1)}, u32[]{:S(2)}, u32[]{:S(2)}) collective-permute-start(f32[1,128,128]{2,1,0:T(8,128)} %get-tuple-element.17.own_ref), channel_id=1, source_target_pairs={{0,2},{2,0},{4,6},{6,4},{8,10},{10,8},{12,14},{14,12},{16,18},{18,... | collective-permute-start | bytes 196616 | tf_op jit(solution)/shard_map/ppermute | solution.py:20
  22.9 3.9 %collective-permute-done.1.refs_0_ = f32[1,128,128]{2,1,0:T(8,128)S(1)} collective-permute-done((f32[1,128,128]{2,1,0:T(8,128)}, f32[1,128,128]{2,1,0:T(8,128)S(1)}, u32[]{:S(2)}, u32[]{:S(2)}) %collective-permute-start.1) | collective-permute-done | bytes 65568 | tf_op jit(solution)/shard_map/ppermute | solution.py:20
  26.8 0.9 pad_maximum_fusion
  27.7 4.2 %collective-permute-start.2 = (f32[2,128,128]{2,1,0:T(8,128)S(1)}, f32[2,128,128]{2,1,0:T(8,128)S(1)}, u32[]{:S(2)}, u32[]{:S(2)}) collective-permute-start(f32[2,128,128]{2,1,0:T(8,128)S(1)} %pad_maximum_fusion), channel_id=1, source_target_pairs={{0,4},{2,6},{4,0},{6,2},{8,12},{10,14},{12,8},{14,10},{16,20},{18,... | collective-permute-start | bytes 393224 | tf_op jit(solution)/shard_map/ppermute | solution.py:20
  31.9 4.1 %collective-permute-done.2.refs_1_ = f32[2,128,128]{2,1,0:T(8,128)S(1)} collective-permute-done((f32[2,128,128]{2,1,0:T(8,128)S(1)}, f32[2,128,128]{2,1,0:T(8,128)S(1)}, u32[]{:S(2)}, u32[]{:S(2)}) %collective-permute-start.2) | collective-permute-done | bytes 131104 | tf_op jit(solution)/shard_map/ppermute | solution.py:20
  36.1 0.7 broadcast_in_dim.3.refs_2_
  36.8 8.0 %shard_map.67 = (f32[1,256,128]{2,1,0:T(8,128)}, f32[1,128,128]{2,1,0:T(8,128)}) custom-call(f32[1,128,128]{2,1,0:T(8,128)} %get-tuple-element.17.own_ref, f32[1,128,128]{2,1,0:T(8,128)} %copy-done.3, f32[2,128,128]{2,1,0:T(8,128)} %copy-done.7, f32[1,256,128]{2,1,0:T(8,128)} %broadcast_in_dim.3.refs_2_), custom_call_target="tpu_custom_call" | custom-call | tf_op jit(solution)/shard_map/pallas_call | solution.py:159
  44.8 2.6 %collective-permute-start.3 = (f32[1,128,128]{2,1,0:T(8,128)}, f32[1,128,128]{2,1,0:T(8,128)S(1)}, u32[]{:S(2)}, u32[]{:S(2)}) collective-permute-start(f32[1,128,128]{2,1,0:T(8,128)} %get-tuple-element.18.own_ref), channel_id=1, source_target_pairs={{0,8},{2,10},{4,12},{6,14},{8,0},{10,2},{12,4},{14,6},{16,24},{18,... | collective-permute-start | bytes 196616 | tf_op jit(solution)/shard_map/ppermute | solution.py:20
  47.4 3.8 %collective-permute-done.3.refs_0_ = f32[1,128,128]{2,1,0:T(8,128)S(1)} collective-permute-done((f32[1,128,128]{2,1,0:T(8,128)}, f32[1,128,128]{2,1,0:T(8,128)S(1)}, u32[]{:S(2)}, u32[]{:S(2)}) %collective-permute-start.3) | collective-permute-done | bytes 65568 | tf_op jit(solution)/shard_map/ppermute | solution.py:20
  51.2 0.9 pad_maximum_fusion.1
  52.1 2.7 %collective-permute-start.4 = (f32[2,128,128]{2,1,0:T(8,128)S(1)}, f32[2,128,128]{2,1,0:T(8,128)S(1)}, u32[]{:S(2)}, u32[]{:S(2)}) collective-permute-start(f32[2,128,128]{2,1,0:T(8,128)S(1)} %pad_maximum_fusion.1), channel_id=1, source_target_pairs={{0,16},{2,18},{4,20},{6,22},{8,24},{10,26},{12,28},{14,30},{16,0},... | collective-permute-start | bytes 393224 | tf_op jit(solution)/shard_map/ppermute | solution.py:20
  54.8 6.5 %collective-permute-done.4.refs_1_ = f32[2,128,128]{2,1,0:T(8,128)S(1)} collective-permute-done((f32[2,128,128]{2,1,0:T(8,128)S(1)}, f32[2,128,128]{2,1,0:T(8,128)S(1)}, u32[]{:S(2)}, u32[]{:S(2)}) %collective-permute-start.4) | collective-permute-done | bytes 131104 | tf_op jit(solution)/shard_map/ppermute | solution.py:20
  61.2 0.7 copy-done.8
  61.9 8.1 %shard_map.68 = (f32[1,256,128]{2,1,0:T(8,128)}, f32[1,128,128]{2,1,0:T(8,128)}) custom-call(f32[1,128,128]{2,1,0:T(8,128)} %get-tuple-element.18.own_ref, f32[1,128,128]{2,1,0:T(8,128)} %copy-done.4, f32[2,128,128]{2,1,0:T(8,128)} %copy-done.8, f32[1,256,128]{2,1,0:T(8,128)} %get-tuple-element.19.refs_2_), custom_call_target="tpu_custom_call" | custom-call | tf_op jit(solution)/shard_map/pallas_call | solution.py:159
  69.9 5.6 %collective-permute-start.5 = (f32[1,128,128]{2,1,0:T(8,128)}, f32[1,128,128]{2,1,0:T(8,128)S(1)}, u32[]{:S(2)}, u32[]{:S(2)}) collective-permute-start(f32[1,128,128]{2,1,0:T(8,128)} %get-tuple-element.20.own_ref), channel_id=1, source_target_pairs={{0,32},{2,34},{4,36},{6,38},{8,40},{10,42},{12,44},{14,46},{16,48}... | collective-permute-start | bytes 196616 | tf_op jit(solution)/shard_map/ppermute | solution.py:20
  75.5 5.4 %collective-permute-done.5.refs_0_ = f32[1,128,128]{2,1,0:T(8,128)S(1)} collective-permute-done((f32[1,128,128]{2,1,0:T(8,128)}, f32[1,128,128]{2,1,0:T(8,128)S(1)}, u32[]{:S(2)}, u32[]{:S(2)}) %collective-permute-start.5) | collective-permute-done | bytes 65568 | tf_op jit(solution)/shard_map/ppermute | solution.py:20
  80.9 0.9 pad_maximum_fusion.2
  81.8 3.8 %collective-permute-start.6 = (f32[2,128,128]{2,1,0:T(8,128)S(1)}, f32[2,128,128]{2,1,0:T(8,128)S(1)}, u32[]{:S(2)}, u32[]{:S(2)}) collective-permute-start(f32[2,128,128]{2,1,0:T(8,128)S(1)} %pad_maximum_fusion.2), channel_id=1, source_target_pairs={{0,64},{2,66},{4,68},{6,70},{8,72},{10,74},{12,76},{14,78},{16,80}... | collective-permute-start | bytes 393224 | tf_op jit(solution)/shard_map/ppermute | solution.py:20
  85.6 3.0 %collective-permute-done.6.refs_1_ = f32[2,128,128]{2,1,0:T(8,128)S(1)} collective-permute-done((f32[2,128,128]{2,1,0:T(8,128)S(1)}, f32[2,128,128]{2,1,0:T(8,128)S(1)}, u32[]{:S(2)}, u32[]{:S(2)}) %collective-permute-start.6) | collective-permute-done | bytes 131104 | tf_op jit(solution)/shard_map/ppermute | solution.py:20
  89.3 8.1 %shard_map.69 = (f32[1,256,128]{2,1,0:T(8,128)}, f32[1,128,128]{2,1,0:T(8,128)}) custom-call(f32[1,128,128]{2,1,0:T(8,128)} %get-tuple-element.20.own_ref, f32[1,128,128]{2,1,0:T(8,128)} %copy-done.5, f32[2,128,128]{2,1,0:T(8,128)} %copy-done.9, f32[1,256,128]{2,1,0:T(8,128)} %get-tuple-element.21.refs_2_), custom_call_target="tpu_custom_call" | custom-call | tf_op jit(solution)/shard_map/pallas_call | solution.py:159
  97.4 5.7 %collective-permute-start.7 = (f32[1,128,128]{2,1,0:T(8,128)}, f32[1,128,128]{2,1,0:T(8,128)S(1)}, u32[]{:S(2)}, u32[]{:S(2)}) collective-permute-start(f32[1,128,128]{2,1,0:T(8,128)} %get-tuple-element.22.own_ref), channel_id=1, source_target_pairs={{0,128},{2,130},{4,132},{6,134},{8,136},{10,138},{12,140},{14,142}... | collective-permute-start | bytes 196616 | tf_op jit(solution)/shard_map/ppermute | solution.py:20
  103.1 2.4 %collective-permute-done.7.refs_0_ = f32[1,128,128]{2,1,0:T(8,128)S(1)} collective-permute-done((f32[1,128,128]{2,1,0:T(8,128)}, f32[1,128,128]{2,1,0:T(8,128)S(1)}, u32[]{:S(2)}, u32[]{:S(2)}) %collective-permute-start.7) | collective-permute-done | bytes 65568 | tf_op jit(solution)/shard_map/ppermute | solution.py:20
  105.5 0.9 pad_maximum_fusion.3
  106.4 11.4 %collective-permute-start.8 = (f32[2,128,128]{2,1,0:T(8,128)S(1)}, f32[2,128,128]{2,1,0:T(8,128)S(1)}, u32[]{:S(2)}, u32[]{:S(2)}) collective-permute-start(f32[2,128,128]{2,1,0:T(8,128)S(1)} %pad_maximum_fusion.3), channel_id=1, source_target_pairs={{0,256},{2,258},{4,260},{6,262},{8,264},{10,266},{12,268},{14,270}... | collective-permute-start | bytes 393224 | tf_op jit(solution)/shard_map/ppermute | solution.py:20
  117.8 2.9 %collective-permute-done.8.refs_1_ = f32[2,128,128]{2,1,0:T(8,128)S(1)} collective-permute-done((f32[2,128,128]{2,1,0:T(8,128)S(1)}, f32[2,128,128]{2,1,0:T(8,128)S(1)}, u32[]{:S(2)}, u32[]{:S(2)}) %collective-permute-start.8) | collective-permute-done | bytes 131104 | tf_op jit(solution)/shard_map/ppermute | solution.py:20
  121.4 8.1 %shard_map.70 = (f32[1,256,128]{2,1,0:T(8,128)}, f32[1,128,128]{2,1,0:T(8,128)}) custom-call(f32[1,128,128]{2,1,0:T(8,128)} %get-tuple-element.22.own_ref, f32[1,128,128]{2,1,0:T(8,128)} %copy-done.6, f32[2,128,128]{2,1,0:T(8,128)} %copy-done.10, f32[1,256,128]{2,1,0:T(8,128)} %get-tuple-element.23.refs_2_), custom_call_target="tpu_custom_call" | custom-call | tf_op jit(solution)/shard_map/pallas_call | solution.py:159
  (19 shorter events, 1.3 us)
Async XLA Ops:
  0.6 1.0 copy-start
  3.1 3.8 %copy-start.1 = (f32[1024,128]{1,0:T(8,128)}, f32[1024,128]{1,0:T(8,128)S(1)}, u32[]{:S(2)}) copy-start(f32[1024,128]{1,0:T(8,128)S(1)} %fusion) | copy-start | bytes 1572868
  3.1 3.8 %collective-permute-start = (f32[4,256,128]{2,1,0:T(8,128)S(1)}, f32[4,256,128]{2,1,0:T(8,128)S(1)}, u32[]{:S(2)}, u32[]{:S(2)}) collective-permute-start(f32[4,256,128]{2,1,0:T(8,128)S(1)} %bitcast.5), channel_id=1, source_target_pairs={{0,1},{1,0},{2,3},{3,2},{4,5},{5,4},{6,7},{7,6},{8,9},{9,8},{10,11... | collective-permute-start | bytes 1572872 | tf_op jit(solution)/shard_map/ppermute | solution.py:20
  6.9 0.8 copy-start.2
  20.4 6.4 %collective-permute-start.1 = (f32[1,128,128]{2,1,0:T(8,128)}, f32[1,128,128]{2,1,0:T(8,128)S(1)}, u32[]{:S(2)}, u32[]{:S(2)}) collective-permute-start(f32[1,128,128]{2,1,0:T(8,128)} %get-tuple-element.17.own_ref), channel_id=1, source_target_pairs={{0,2},{2,0},{4,6},{6,4},{8,10},{10,8},{12,14},{14,12},{16,18},{18,... | collective-permute-start | bytes 196616 | tf_op jit(solution)/shard_map/ppermute | solution.py:20
  26.8 0.9 copy-start.3
  27.7 8.4 %collective-permute-start.2 = (f32[2,128,128]{2,1,0:T(8,128)S(1)}, f32[2,128,128]{2,1,0:T(8,128)S(1)}, u32[]{:S(2)}, u32[]{:S(2)}) collective-permute-start(f32[2,128,128]{2,1,0:T(8,128)S(1)} %pad_maximum_fusion), channel_id=1, source_target_pairs={{0,4},{2,6},{4,0},{6,2},{8,12},{10,14},{12,8},{14,10},{16,20},{18,... | collective-permute-start | bytes 393224 | tf_op jit(solution)/shard_map/ppermute | solution.py:20
  36.1 0.7 copy-start.7
  44.8 6.4 %collective-permute-start.3 = (f32[1,128,128]{2,1,0:T(8,128)}, f32[1,128,128]{2,1,0:T(8,128)S(1)}, u32[]{:S(2)}, u32[]{:S(2)}) collective-permute-start(f32[1,128,128]{2,1,0:T(8,128)} %get-tuple-element.18.own_ref), channel_id=1, source_target_pairs={{0,8},{2,10},{4,12},{6,14},{8,0},{10,2},{12,4},{14,6},{16,24},{18,... | collective-permute-start | bytes 196616 | tf_op jit(solution)/shard_map/ppermute | solution.py:20
  51.2 0.9 copy-start.4
  52.1 9.2 %collective-permute-start.4 = (f32[2,128,128]{2,1,0:T(8,128)S(1)}, f32[2,128,128]{2,1,0:T(8,128)S(1)}, u32[]{:S(2)}, u32[]{:S(2)}) collective-permute-start(f32[2,128,128]{2,1,0:T(8,128)S(1)} %pad_maximum_fusion.1), channel_id=1, source_target_pairs={{0,16},{2,18},{4,20},{6,22},{8,24},{10,26},{12,28},{14,30},{16,0},... | collective-permute-start | bytes 393224 | tf_op jit(solution)/shard_map/ppermute | solution.py:20
  61.2 0.7 copy-start.8
  69.9 11.0 %collective-permute-start.5 = (f32[1,128,128]{2,1,0:T(8,128)}, f32[1,128,128]{2,1,0:T(8,128)S(1)}, u32[]{:S(2)}, u32[]{:S(2)}) collective-permute-start(f32[1,128,128]{2,1,0:T(8,128)} %get-tuple-element.20.own_ref), channel_id=1, source_target_pairs={{0,32},{2,34},{4,36},{6,38},{8,40},{10,42},{12,44},{14,46},{16,48}... | collective-permute-start | bytes 196616 | tf_op jit(solution)/shard_map/ppermute | solution.py:20
  80.9 0.9 copy-start.5
  81.8 6.9 %collective-permute-start.6 = (f32[2,128,128]{2,1,0:T(8,128)S(1)}, f32[2,128,128]{2,1,0:T(8,128)S(1)}, u32[]{:S(2)}, u32[]{:S(2)}) collective-permute-start(f32[2,128,128]{2,1,0:T(8,128)S(1)} %pad_maximum_fusion.2), channel_id=1, source_target_pairs={{0,64},{2,66},{4,68},{6,70},{8,72},{10,74},{12,76},{14,78},{16,80}... | collective-permute-start | bytes 393224 | tf_op jit(solution)/shard_map/ppermute | solution.py:20
  88.7 0.7 copy-start.9
  97.4 8.2 %collective-permute-start.7 = (f32[1,128,128]{2,1,0:T(8,128)}, f32[1,128,128]{2,1,0:T(8,128)S(1)}, u32[]{:S(2)}, u32[]{:S(2)}) collective-permute-start(f32[1,128,128]{2,1,0:T(8,128)} %get-tuple-element.22.own_ref), channel_id=1, source_target_pairs={{0,128},{2,130},{4,132},{6,134},{8,136},{10,138},{12,140},{14,142}... | collective-permute-start | bytes 196616 | tf_op jit(solution)/shard_map/ppermute | solution.py:20
  105.5 0.9 copy-start.6
  106.4 14.3 %collective-permute-start.8 = (f32[2,128,128]{2,1,0:T(8,128)S(1)}, f32[2,128,128]{2,1,0:T(8,128)S(1)}, u32[]{:S(2)}, u32[]{:S(2)}) collective-permute-start(f32[2,128,128]{2,1,0:T(8,128)S(1)} %pad_maximum_fusion.3), channel_id=1, source_target_pairs={{0,256},{2,258},{4,260},{6,262},{8,264},{10,266},{12,268},{14,270}... | collective-permute-start | bytes 393224 | tf_op jit(solution)/shard_map/ppermute | solution.py:20
  120.8 0.7 copy-start.10

commit v4 on v3

--- a/solution.py
+++ b/solution.py
@@ -99,23 +99,19 @@
     top_ref[0] = factors[0]
 
 
-def round_kernel(low_bit, own_ref, *refs):
-    received_refs, top_in_ref, top_ref, next_ref = refs[:-3], refs[-3], refs[-2], refs[-1]
-    width = own_ref.shape[2]
-    levels = len(received_refs)
-    members = 1 << levels
-    position = lax.axis_index("clus")
+def clus_position(axes):
+    position = 0
+    for name in axes:
+        position = position * lax.axis_size(name) + lax.axis_index(name)
+    return position
+
+
+def round_kernel(low_bit, axes, group_ref, top_in_ref, top_ref, next_ref):
+    members = group_ref.shape[0]
+    levels = members.bit_length() - 1
+    position = clus_position(axes)
     member = (position >> low_bit) & (members - 1)
-    arrived = [own_ref[0]]
-    for received_ref in received_refs:
-        arrived += [received_ref[t] for t in range(received_ref.shape[0])]
-    group = []
-    for p in range(members):
-        chosen = arrived[p]
-        for t in range(members):
-            if t != p:
-                chosen = jnp.where(member == p ^ t, arrived[t], chosen)
-        group.append(chosen)
+    group = [group_ref[p] for p in range(members)]
     top = top_in_ref[0]
     factors = group
     for level in range(levels):
@@ -153,48 +149,53 @@
     )(leaf_slot, partial_value, other_value)
 
 
-def round_call(low_bit, own, received, top_in):
-    width = own.shape[2]
+def round_call(low_bit, axes, group, top_in):
+    width = group.shape[2]
     vmem = pltpu.MemorySpace.VMEM
     return pl.pallas_call(
-        functools.partial(round_kernel, low_bit),
+        functools.partial(round_kernel, low_bit, axes),
         out_shape=(
             jax.ShapeDtypeStruct(top_in.shape, jnp.float32),
             jax.ShapeDtypeStruct((1, width, width), jnp.float32),
         ),
-        in_specs=[pl.BlockSpec(memory_space=vmem) for _ in range(len(received) + 2)],
+        in_specs=[pl.BlockSpec(memory_space=vmem), pl.BlockSpec(memory_space=vmem)],
         out_specs=(pl.BlockSpec(memory_space=vmem), pl.BlockSpec(memory_space=vmem)),
-    )(own, *received, top_in)
-
-
-def body(samples, sketch, leaf_slot):
+    )(group, top_in)
+
+
+def round_widths(count):
+    depth = count.bit_length() - 1
+    return [ROUND_BITS] * (depth // ROUND_BITS) + ([depth % ROUND_BITS] if depth % ROUND_BITS else [])
+
+
+def body(axes, samples, sketch, leaf_slot):
     columns = sketch.shape[1]
     leaf_count = leaf_slot.shape[1]
     partial_value = jnp.dot(samples, sketch, precision=highest).reshape(leaf_count, -1, columns)
     other_value = from_xor(partial_value, "samp", 1)
     leaf_basis, local_transfer, factors = local_call(leaf_slot, partial_value, other_value)
-    tree_depth = lax.axis_size("clus").bit_length() - 1
     top_out = jnp.zeros((1, 2 * columns, columns), jnp.float32)
     low_bit = 0
-    while low_bit < tree_depth:
-        width = min(ROUND_BITS, tree_depth - low_bit)
-        gathered = factors
-        received = []
-        for step in range(width):
-            arrived = from_xor(gathered, "clus", 1 << (low_bit + step))
-            received.append(arrived)
-            if step + 1 < width:
-                gathered = jnp.concatenate([gathered, arrived], axis=0)
-        top_out, factors = round_call(low_bit, factors, received, top_out)
-        low_bit += width
+    for name in reversed(axes):
+        members = lax.axis_size(name)
+        spread = jnp.broadcast_to(factors, (members,) + factors.shape[1:])
+        group = lax.all_to_all(spread, name, 0, 0, tiled=True)
+        top_out, factors = round_call(low_bit, axes, group, top_out)
+        low_bit += members.bit_length() - 1
     return (leaf_basis.reshape(-1, columns), local_transfer, top_out, factors[0])
 
 
 def solution(mesh):
+    clus = mesh.shape["clus"]
+    widths = round_widths(clus)
+    axes = tuple(f"clus{i}" for i in range(len(widths)))
+    sizes = tuple(1 << w for w in reversed(widths))
+    devices = mesh.devices.reshape(sizes + (mesh.shape["samp"],))
+    split = jax.sharding.Mesh(devices, axes + ("samp",))
     return jax.shard_map(
-        body,
-        mesh=mesh,
-        in_specs=(P("clus", "samp"), P("samp", None), P("clus", None)),
-        out_specs=(P("clus", None), P("clus", None, None), P("clus", None, None), P()),
+        functools.partial(body, axes),
+        mesh=split,
+        in_specs=(P(axes, "samp"), P("samp", None), P(axes, None)),
+        out_specs=(P(axes, None), P(axes, None, None), P(axes, None, None), P()),
         check_vma=False,
     )

time: 130 us -> 117 us (0.900)
  the two profiles are of different devices: /device:TPU:34 before, /device:TPU:8 now
where the time goes in v4:
time: 117 us; the launch traced here: 116 us
  blocking collectives  59.3 us (51%)
  Pallas kernels  44.7 us (38%)
  local copies, waits for them, and re-layouts  5.93 us (5%)
  starting transfers between devices  1.92 us (2%)
  waiting for transfers between devices  1.88 us (2%)
  matrix products  1.4 us (1%)
    all_to_all x4, blocking collectives, body(): group = lax.all_to_all(spread, name, 0, 0, tiled=True)  59.3 us
    pallas_call x4, Pallas kernels, round_call(): pl.pallas_call(functools.partial(round_kernel, low_bit, axes), out_shape=...  32 us
    pallas_call x1, Pallas kernels, local_call(): pl.pallas_call(local_kernel, out_shape=(jax.ShapeDtypeStruct((leaf_count,...  12.7 us
    broadcast_in_dim x4, local copies, waits for them, and re-layouts, body(): spread = jnp.broadcast_to(factors, (members,) + factors.shape[1:])  3.43 us
  transfers between devices with their start and end apart: 1, of which 1 were waited for; matrix products, arithmetic and copies ran while one was open for 0% of the time, Pallas kernels for 0%

profile of v4, /device:TPU:8, one launch (start us, length us, event | category | flops | bytes accessed | tf_op | source)
XLA Modules:
  0.0 115.9 jit_solution(15821346252068097363)
XLA Ops:
  0.6 0.0 copy-start
  0.6 1.0 copy-done
  1.7 1.4 %fusion = f32[1024,128]{1,0:T(8,128)S(1)} fusion(f32[1024,128]{1,0:T(8,128)S(1)} %copy-done, f32[128,128]{1,0:T(8,128)} %param.4), kind=kOutput, calls=%fused_computation | convolution fusion | flops 201326592 | bytes 1114112 | tf_op jit(solution)/shard_map/dot_general | solution.py:174
  3.1 0.0 copy-start.1
  3.1 1.9 %collective-permute-start = (f32[4,256,128]{2,1,0:T(8,128)S(1)}, f32[4,256,128]{2,1,0:T(8,128)S(1)}, u32[]{:S(2)}, u32[]{:S(2)}) collective-permute-start(f32[4,256,128]{2,1,0:T(8,128)S(1)} %bitcast.9), channel_id=1, source_target_pairs={{0,1},{1,0},{2,3},{3,2},{4,5},{5,4},{6,7},{7,6},{8,9},{9,8},{10,11... | collective-permute-start | bytes 1572872 | tf_op jit(solution)/shard_map/ppermute | solution.py:20
  5.0 1.9 %collective-permute-done.other_ref = f32[4,256,128]{2,1,0:T(8,128)S(1)} collective-permute-done((f32[4,256,128]{2,1,0:T(8,128)S(1)}, f32[4,256,128]{2,1,0:T(8,128)S(1)}, u32[]{:S(2)}, u32[]{:S(2)}) %collective-permute-start) | collective-permute-done | bytes 524320 | tf_op jit(solution)/shard_map/ppermute | solution.py:20
  6.9 0.0 copy-done.1
  6.9 0.0 copy-start.2
  6.9 0.8 copy-done.2
  7.7 12.7 %shard_map.66 = (f32[4,256,128]{2,1,0:T(8,128)}, f32[3,256,128]{2,1,0:T(8,128)}, f32[1,128,128]{2,1,0:T(8,128)}) custom-call(s32[1,4]{1,0:T(1,128)} %slot_ref.1, f32[4,256,128]{2,1,0:T(8,128)} %bitcast.10, f32[4,256,128]{2,1,0:T(8,128)} %copy-done.2), custom_call_target="tpu_custom_call" | custom-call | tf_op jit(solution)/shard_map/pallas_call | solution.py:140
  20.4 0.9 broadcast_in_dim.32
  21.3 11.2 %all_to_all.20.group_ref = f32[4,128,128]{2,1,0:T(8,128)} all-to-all(f32[4,128,128]{2,1,0:T(8,128)S(1)} %broadcast_in_dim.32), channel_id=1, replica_groups=mesh['clus0'=4,'clus1'=4,'clus2'=4,'clus3'=4,'samp'=2] {'clus3'}, dimensions={0} | all-to-all | bytes 524288 | tf_op jit(solution)/shard_map/all_to_all | solution.py:182
  32.5 0.7 broadcast_in_dim.33.top_in_ref
  33.1 8.0 %shard_map.67 = (f32[1,256,128]{2,1,0:T(8,128)}, f32[1,128,128]{2,1,0:T(8,128)}) custom-call(f32[4,128,128]{2,1,0:T(8,128)} %all_to_all.20.group_ref, f32[1,256,128]{2,1,0:T(8,128)} %broadcast_in_dim.33.top_in_ref), custom_call_target="tpu_custom_call" | custom-call | tf_op jit(solution)/shard_map/pallas_call | solution.py:155
  41.1 0.9 broadcast_in_dim.35
  42.0 14.8 %all_to_all.21.group_ref = f32[4,128,128]{2,1,0:T(8,128)} all-to-all(f32[4,128,128]{2,1,0:T(8,128)S(1)} %broadcast_in_dim.35), channel_id=1, replica_groups=mesh['clus0'=4,'clus1'=4,'clus2'=4,'clus3'=4,'samp'=2] {'clus2'}, dimensions={0} | all-to-all | bytes 524288 | tf_op jit(solution)/shard_map/all_to_all | solution.py:182
  56.8 8.0 %shard_map.68 = (f32[1,256,128]{2,1,0:T(8,128)}, f32[1,128,128]{2,1,0:T(8,128)}) custom-call(f32[4,128,128]{2,1,0:T(8,128)} %all_to_all.21.group_ref, f32[1,256,128]{2,1,0:T(8,128)} %get-tuple-element.19.top_in_ref), custom_call_target="tpu_custom_call" | custom-call | tf_op jit(solution)/shard_map/pallas_call | solution.py:155
  64.8 0.9 broadcast_in_dim.37
  65.7 14.0 %all_to_all.22.group_ref = f32[4,128,128]{2,1,0:T(8,128)} all-to-all(f32[4,128,128]{2,1,0:T(8,128)S(1)} %broadcast_in_dim.37), channel_id=1, replica_groups=mesh['clus0'=4,'clus1'=4,'clus2'=4,'clus3'=4,'samp'=2] {'clus1'}, dimensions={0} | all-to-all | bytes 524288 | tf_op jit(solution)/shard_map/all_to_all | solution.py:182
  79.7 8.0 %shard_map.69 = (f32[1,256,128]{2,1,0:T(8,128)}, f32[1,128,128]{2,1,0:T(8,128)}) custom-call(f32[4,128,128]{2,1,0:T(8,128)} %all_to_all.22.group_ref, f32[1,256,128]{2,1,0:T(8,128)} %get-tuple-element.21.top_in_ref), custom_call_target="tpu_custom_call" | custom-call | tf_op jit(solution)/shard_map/pallas_call | solution.py:155
  87.7 0.9 broadcast_in_dim.39
  88.5 19.3 %all_to_all.23.group_ref = f32[4,128,128]{2,1,0:T(8,128)} all-to-all(f32[4,128,128]{2,1,0:T(8,128)S(1)} %broadcast_in_dim.39), channel_id=1, replica_groups=mesh['clus0'=4,'clus1'=4,'clus2'=4,'clus3'=4,'samp'=2] {'clus0'}, dimensions={0} | all-to-all | bytes 524288 | tf_op jit(solution)/shard_map/all_to_all | solution.py:182
  107.9 8.0 %shard_map.70 = (f32[1,256,128]{2,1,0:T(8,128)}, f32[1,128,128]{2,1,0:T(8,128)}) custom-call(f32[4,128,128]{2,1,0:T(8,128)} %all_to_all.23.group_ref, f32[1,256,128]{2,1,0:T(8,128)} %get-tuple-element.23.top_in_ref), custom_call_target="tpu_custom_call" | custom-call | tf_op jit(solution)/shard_map/pallas_call | solution.py:155
Async XLA Ops:
  0.6 1.0 copy-start
  3.1 3.8 %copy-start.1 = (f32[1024,128]{1,0:T(8,128)}, f32[1024,128]{1,0:T(8,128)S(1)}, u32[]{:S(2)}) copy-start(f32[1024,128]{1,0:T(8,128)S(1)} %fusion) | copy-start | bytes 1572868
  3.1 3.8 %collective-permute-start = (f32[4,256,128]{2,1,0:T(8,128)S(1)}, f32[4,256,128]{2,1,0:T(8,128)S(1)}, u32[]{:S(2)}, u32[]{:S(2)}) collective-permute-start(f32[4,256,128]{2,1,0:T(8,128)S(1)} %bitcast.9), channel_id=1, source_target_pairs={{0,1},{1,0},{2,3},{3,2},{4,5},{5,4},{6,7},{7,6},{8,9},{9,8},{10,11... | collective-permute-start | bytes 1572872 | tf_op jit(solution)/shard_map/ppermute | solution.py:20
  6.9 0.8 copy-start.2

commit v5 on v4

--- a/solution.py
+++ b/solution.py
@@ -96,7 +96,8 @@
             transfer_ref[offsets[level] + i, p * width:(p + 1) * width, :] = part
 
     factors = pair_levels(factors, len(offsets), store)
-    top_ref[0] = factors[0]
+    for p in range(top_ref.shape[0]):
+        top_ref[p] = factors[0]
 
 
 def clus_position(axes):
@@ -106,13 +107,17 @@
     return position
 
 
-def round_kernel(low_bit, axes, group_ref, top_in_ref, top_ref, next_ref):
+def round_kernel(low_bit, axes, group_ref, *refs):
+    top_in_ref, top_ref, next_ref = refs if len(refs) == 3 else (None,) + refs
     members = group_ref.shape[0]
     levels = members.bit_length() - 1
     position = clus_position(axes)
     member = (position >> low_bit) & (members - 1)
     group = [group_ref[p] for p in range(members)]
-    top = top_in_ref[0]
+    if top_in_ref is None:
+        top = jnp.zeros(top_ref.shape[1:], jnp.float32)
+    else:
+        top = top_in_ref[0]
     factors = group
     for level in range(levels):
         nodes = [[factors[2 * i], factors[2 * i + 1]] for i in range(len(factors) // 2)]
@@ -131,10 +136,11 @@
         top = jnp.where(owned, transfer, top)
         factors = [r for _, r, _ in results]
     top_ref[0] = top
-    next_ref[0] = factors[0]
-
-
-def local_call(leaf_slot, partial_value, other_value):
+    for p in range(next_ref.shape[0]):
+        next_ref[p] = factors[0]
+
+
+def local_call(leaf_slot, partial_value, other_value, spread):
     leaf_count, rows, width = partial_value.shape
     vmem = pltpu.MemorySpace.VMEM
     return pl.pallas_call(
@@ -142,25 +148,26 @@
         out_shape=(
             jax.ShapeDtypeStruct((leaf_count, rows, width), jnp.float32),
             jax.ShapeDtypeStruct((leaf_count - 1, 2 * width, width), jnp.float32),
-            jax.ShapeDtypeStruct((1, width, width), jnp.float32),
+            jax.ShapeDtypeStruct((spread, width, width), jnp.float32),
         ),
         in_specs=[pl.BlockSpec(memory_space=pltpu.MemorySpace.SMEM), pl.BlockSpec(memory_space=vmem), pl.BlockSpec(memory_space=vmem)],
         out_specs=tuple(pl.BlockSpec(memory_space=vmem) for _ in range(3)),
     )(leaf_slot, partial_value, other_value)
 
 
-def round_call(low_bit, axes, group, top_in):
+def round_call(low_bit, axes, group, top_in, spread):
     width = group.shape[2]
     vmem = pltpu.MemorySpace.VMEM
+    operands = [group] if top_in is None else [group, top_in]
     return pl.pallas_call(
         functools.partial(round_kernel, low_bit, axes),
         out_shape=(
-            jax.ShapeDtypeStruct(top_in.shape, jnp.float32),
-            jax.ShapeDtypeStruct((1, width, width), jnp.float32),
+            jax.ShapeDtypeStruct((1, 2 * width, width), jnp.float32),
+            jax.ShapeDtypeStruct((spread, width, width), jnp.float32),
         ),
-        in_specs=[pl.BlockSpec(memory_space=vmem), pl.BlockSpec(memory_space=vmem)],
+        in_specs=[pl.BlockSpec(memory_space=vmem) for _ in operands],
         out_specs=(pl.BlockSpec(memory_space=vmem), pl.BlockSpec(memory_space=vmem)),
-    )(group, top_in)
+    )(*operands)
 
 
 def round_widths(count):
@@ -173,15 +180,15 @@
     leaf_count = leaf_slot.shape[1]
     partial_value = jnp.dot(samples, sketch, precision=highest).reshape(leaf_count, -1, columns)
     other_value = from_xor(partial_value, "samp", 1)
-    leaf_basis, local_transfer, factors = local_call(leaf_slot, partial_value, other_value)
-    top_out = jnp.zeros((1, 2 * columns, columns), jnp.float32)
+    order = list(reversed(axes))
+    sizes = [lax.axis_size(name) for name in order] + [1]
+    leaf_basis, local_transfer, factors = local_call(leaf_slot, partial_value, other_value, sizes[0])
+    top_out = None
     low_bit = 0
-    for name in reversed(axes):
-        members = lax.axis_size(name)
-        spread = jnp.broadcast_to(factors, (members,) + factors.shape[1:])
-        group = lax.all_to_all(spread, name, 0, 0, tiled=True)
-        top_out, factors = round_call(low_bit, axes, group, top_out)
-        low_bit += members.bit_length() - 1
+    for index, name in enumerate(order):
+        group = lax.all_to_all(factors, name, 0, 0, tiled=True)
+        top_out, factors = round_call(low_bit, axes, group, top_out, sizes[index + 1])
+        low_bit += sizes[index].bit_length() - 1
     return (leaf_basis.reshape(-1, columns), local_transfer, top_out, factors[0])
 
 

time: 117 us -> 114 us (0.974)
  local copies, waits for them, and re-layouts: 5.93 us -> 1.84 us
  blocking collectives: 59.3 us -> 61 us
    broadcast_in_dim x5 -> x0, local copies, waits for them, and re-layouts: 4.09 us -> none  [the longest x4 3.43 us: body(): spread = jnp.broadcast_to(factors, (members,) + factors.shape[1:])]
    all_to_all x4, blocking collectives: 59.3 us -> 61 us  [body(): group = lax.all_to_all(factors, name, 0, 0, tiled=True)]
where the time goes in v5:
time: 114 us; the launch traced here: 113 us
  blocking collectives  61 us (54%)
  Pallas kernels  44.8 us (39%)
  starting transfers between devices  1.92 us (2%)
  waiting for transfers between devices  1.88 us (2%)
  local copies, waits for them, and re-layouts  1.84 us (2%)
  matrix products  1.4 us (1%)
    all_to_all x4, blocking collectives, body(): group = lax.all_to_all(factors, name, 0, 0, tiled=True)  61 us
    pallas_call x4, Pallas kernels, round_call(): pl.pallas_call(functools.partial(round_kernel, low_bit, axes), out_shape=...  32 us
    pallas_call x1, Pallas kernels, local_call(): pl.pallas_call(local_kernel, out_shape=(jax.ShapeDtypeStruct((leaf_count,...  12.8 us
  transfers between devices with their start and end apart: 1, of which 1 were waited for; matrix products, arithmetic and copies ran while one was open for 0% of the time, Pallas kernels for 0%

profile of v5, /device:TPU:8, one launch (start us, length us, event | category | flops | bytes accessed | tf_op | source)
XLA Modules:
  0.0 113.5 jit_solution(8420656396361452678)
XLA Ops:
  0.6 0.0 copy-start
  0.6 1.0 copy-done
  1.7 1.4 %fusion = f32[1024,128]{1,0:T(8,128)S(1)} fusion(f32[1024,128]{1,0:T(8,128)S(1)} %copy-done, f32[128,128]{1,0:T(8,128)} %param.4), kind=kOutput, calls=%fused_computation | convolution fusion | flops 201326592 | bytes 1114112 | tf_op jit(solution)/shard_map/dot_general | solution.py:181
  3.1 0.0 copy-start.1
  3.1 1.9 %collective-permute-start = (f32[4,256,128]{2,1,0:T(8,128)S(1)}, f32[4,256,128]{2,1,0:T(8,128)S(1)}, u32[]{:S(2)}, u32[]{:S(2)}) collective-permute-start(f32[4,256,128]{2,1,0:T(8,128)S(1)} %bitcast.5), channel_id=1, source_target_pairs={{0,1},{1,0},{2,3},{3,2},{4,5},{5,4},{6,7},{7,6},{8,9},{9,8},{10,11... | collective-permute-start | bytes 1572872 | tf_op jit(solution)/shard_map/ppermute | solution.py:20
  5.0 1.9 %collective-permute-done.other_ref = f32[4,256,128]{2,1,0:T(8,128)S(1)} collective-permute-done((f32[4,256,128]{2,1,0:T(8,128)S(1)}, f32[4,256,128]{2,1,0:T(8,128)S(1)}, u32[]{:S(2)}, u32[]{:S(2)}) %collective-permute-start) | collective-permute-done | bytes 524320 | tf_op jit(solution)/shard_map/ppermute | solution.py:20
  6.9 0.0 copy-done.1
  6.9 0.0 copy-start.2
  6.9 0.8 copy-done.2
  7.7 12.8 %shard_map.66 = (f32[4,256,128]{2,1,0:T(8,128)}, f32[3,256,128]{2,1,0:T(8,128)}, f32[4,128,128]{2,1,0:T(8,128)}) custom-call(s32[1,4]{1,0:T(1,128)} %slot_ref.1, f32[4,256,128]{2,1,0:T(8,128)} %bitcast.6, f32[4,256,128]{2,1,0:T(8,128)} %copy-done.2), custom_call_target="tpu_custom_call" | custom-call | tf_op jit(solution)/shard_map/pallas_call | solution.py:146
  20.5 11.4 %all_to_all.20.group_ref = f32[4,128,128]{2,1,0:T(8,128)} all-to-all(f32[4,128,128]{2,1,0:T(8,128)} %get-tuple-element.17), channel_id=1, replica_groups=mesh['clus0'=4,'clus1'=4,'clus2'=4,'clus3'=4,'samp'=2] {'clus3'}, dimensions={0} | all-to-all | bytes 524288 | tf_op jit(solution)/shard_map/all_to_all | solution.py:189
  31.9 8.0 %shard_map.67 = (f32[1,256,128]{2,1,0:T(8,128)}, f32[4,128,128]{2,1,0:T(8,128)}) custom-call(f32[4,128,128]{2,1,0:T(8,128)} %all_to_all.20.group_ref), custom_call_target="tpu_custom_call" | custom-call | tf_op jit(solution)/shard_map/pallas_call | solution.py:162
  39.9 16.7 %all_to_all.21.group_ref = f32[4,128,128]{2,1,0:T(8,128)} all-to-all(f32[4,128,128]{2,1,0:T(8,128)} %get-tuple-element.18), channel_id=1, replica_groups=mesh['clus0'=4,'clus1'=4,'clus2'=4,'clus3'=4,'samp'=2] {'clus2'}, dimensions={0} | all-to-all | bytes 524288 | tf_op jit(solution)/shard_map/all_to_all | solution.py:189
  56.6 8.0 %shard_map.68 = (f32[1,256,128]{2,1,0:T(8,128)}, f32[4,128,128]{2,1,0:T(8,128)}) custom-call(f32[4,128,128]{2,1,0:T(8,128)} %all_to_all.21.group_ref, f32[1,256,128]{2,1,0:T(8,128)} %get-tuple-element.19.refs_0_), custom_call_target="tpu_custom_call" | custom-call | tf_op jit(solution)/shard_map/pallas_call | solution.py:162
  64.6 15.4 %all_to_all.22.group_ref = f32[4,128,128]{2,1,0:T(8,128)} all-to-all(f32[4,128,128]{2,1,0:T(8,128)} %get-tuple-element.20), channel_id=1, replica_groups=mesh['clus0'=4,'clus1'=4,'clus2'=4,'clus3'=4,'samp'=2] {'clus1'}, dimensions={0} | all-to-all | bytes 524288 | tf_op jit(solution)/shard_map/all_to_all | solution.py:189
  80.0 8.0 %shard_map.69 = (f32[1,256,128]{2,1,0:T(8,128)}, f32[4,128,128]{2,1,0:T(8,128)}) custom-call(f32[4,128,128]{2,1,0:T(8,128)} %all_to_all.22.group_ref, f32[1,256,128]{2,1,0:T(8,128)} %get-tuple-element.21.refs_0_), custom_call_target="tpu_custom_call" | custom-call | tf_op jit(solution)/shard_map/pallas_call | solution.py:162
  88.0 17.4 %all_to_all.23.group_ref = f32[4,128,128]{2,1,0:T(8,128)} all-to-all(f32[4,128,128]{2,1,0:T(8,128)} %get-tuple-element.22), channel_id=1, replica_groups=mesh['clus0'=4,'clus1'=4,'clus2'=4,'clus3'=4,'samp'=2] {'clus0'}, dimensions={0} | all-to-all | bytes 524288 | tf_op jit(solution)/shard_map/all_to_all | solution.py:189
  105.5 8.0 %shard_map.70 = (f32[1,256,128]{2,1,0:T(8,128)}, f32[1,128,128]{2,1,0:T(8,128)}) custom-call(f32[4,128,128]{2,1,0:T(8,128)} %all_to_all.23.group_ref, f32[1,256,128]{2,1,0:T(8,128)} %get-tuple-element.23.refs_0_), custom_call_target="tpu_custom_call" | custom-call | tf_op jit(solution)/shard_map/pallas_call | solution.py:162
Async XLA Ops:
  0.6 1.0 copy-start
  3.1 3.8 %copy-start.1 = (f32[1024,128]{1,0:T(8,128)}, f32[1024,128]{1,0:T(8,128)S(1)}, u32[]{:S(2)}) copy-start(f32[1024,128]{1,0:T(8,128)S(1)} %fusion) | copy-start | bytes 1572868
  3.1 3.8 %collective-permute-start = (f32[4,256,128]{2,1,0:T(8,128)S(1)}, f32[4,256,128]{2,1,0:T(8,128)S(1)}, u32[]{:S(2)}, u32[]{:S(2)}) collective-permute-start(f32[4,256,128]{2,1,0:T(8,128)S(1)} %bitcast.5), channel_id=1, source_target_pairs={{0,1},{1,0},{2,3},{3,2},{4,5},{5,4},{6,7},{7,6},{8,9},{9,8},{10,11... | collective-permute-start | bytes 1572872 | tf_op jit(solution)/shard_map/ppermute | solution.py:20
  6.9 0.8 copy-start.2

commit v6 on v5

--- a/solution.py
+++ b/solution.py
@@ -40,10 +40,17 @@
         for part in parts[1:]:
             g = g + gram(part)
         grams.append(g)
-    scales = [jnp.sum(jnp.where(diag, g, 0.0), keepdims=True) + 1e-06 for g in grams]
-    roots = [g / c for g, c in zip(grams, scales)]
-    inverses = [identity for _ in nodes]
-    for _ in range(NS_STEPS):
+    scales = []
+    for parts in nodes:
+        c = jnp.sum(parts[0] * parts[0], keepdims=True)
+        for part in parts[1:]:
+            c = c + jnp.sum(part * part, keepdims=True)
+        scales.append(c + 1e-06)
+    roots = [g * (1.0 / c) for g, c in zip(grams, scales)]
+    middles = [1.5 * identity - 0.5 * y for y in roots]
+    roots = [mm(y, m) for y, m in zip(roots, middles)]
+    inverses = middles
+    for _ in range(NS_STEPS - 1):
         middles = [1.5 * identity - 0.5 * mm(w, y) for w, y in zip(inverses, roots)]
         roots, inverses = (
             [mm(y, m) for y, m in zip(roots, middles)],

time: 114 us -> 109 us (0.956)
  Pallas kernels: 44.8 us -> 40.1 us
    pallas_call x4, Pallas kernels: 32 us -> 28.6 us  [round_call(): pl.pallas_call(functools.partial(round_kernel, low_bit, axes), out_shape=...]
    pallas_call x1, Pallas kernels: 12.8 us -> 11.5 us  [local_call(): pl.pallas_call(local_kernel, out_shape=(jax.ShapeDtypeStruct((leaf_count,...]
where the time goes in v6:
time: 109 us
  blocking collectives  61 us (56%)
  Pallas kernels  40.1 us (37%)
  starting transfers between devices  1.92 us (2%)
  waiting for transfers between devices  1.88 us (2%)
  local copies, waits for them, and re-layouts  1.84 us (2%)
  matrix products  1.4 us (1%)
    all_to_all x4, blocking collectives, body(): group = lax.all_to_all(factors, name, 0, 0, tiled=True)  61 us
    pallas_call x4, Pallas kernels, round_call(): pl.pallas_call(functools.partial(round_kernel, low_bit, axes), out_shape=...  28.6 us
    pallas_call x1, Pallas kernels, local_call(): pl.pallas_call(local_kernel, out_shape=(jax.ShapeDtypeStruct((leaf_count,...  11.5 us
  transfers between devices with their start and end apart: 1, of which 1 were waited for; matrix products, arithmetic and copies ran while one was open for 0% of the time, Pallas kernels for 0%

profile of v6, /device:TPU:8, one launch (start us, length us, event | category | flops | bytes accessed | tf_op | source)
XLA Modules:
  0.0 108.8 jit_solution(6433755523708389562)
XLA Ops:
  0.6 0.0 copy-start
  0.6 1.0 copy-done
  1.7 1.4 %fusion = f32[1024,128]{1,0:T(8,128)S(1)} fusion(f32[1024,128]{1,0:T(8,128)S(1)} %copy-done, f32[128,128]{1,0:T(8,128)} %param.4), kind=kOutput, calls=%fused_computation | convolution fusion | flops 201326592 | bytes 1114112 | tf_op jit(solution)/shard_map/dot_general | solution.py:188
  3.1 0.0 copy-start.1
  3.1 1.9 %collective-permute-start = (f32[4,256,128]{2,1,0:T(8,128)S(1)}, f32[4,256,128]{2,1,0:T(8,128)S(1)}, u32[]{:S(2)}, u32[]{:S(2)}) collective-permute-start(f32[4,256,128]{2,1,0:T(8,128)S(1)} %bitcast.5), channel_id=1, source_target_pairs={{0,1},{1,0},{2,3},{3,2},{4,5},{5,4},{6,7},{7,6},{8,9},{9,8},{10,11... | collective-permute-start | bytes 1572872 | tf_op jit(solution)/shard_map/ppermute | solution.py:20
  5.0 1.9 %collective-permute-done.other_ref = f32[4,256,128]{2,1,0:T(8,128)S(1)} collective-permute-done((f32[4,256,128]{2,1,0:T(8,128)S(1)}, f32[4,256,128]{2,1,0:T(8,128)S(1)}, u32[]{:S(2)}, u32[]{:S(2)}) %collective-permute-start) | collective-permute-done | bytes 524320 | tf_op jit(solution)/shard_map/ppermute | solution.py:20
  6.9 0.0 copy-done.1
  6.9 0.0 copy-start.2
  6.9 0.8 copy-done.2
  7.7 11.5 %shard_map.66 = (f32[4,256,128]{2,1,0:T(8,128)}, f32[3,256,128]{2,1,0:T(8,128)}, f32[4,128,128]{2,1,0:T(8,128)}) custom-call(s32[1,4]{1,0:T(1,128)} %slot_ref.1, f32[4,256,128]{2,1,0:T(8,128)} %bitcast.6, f32[4,256,128]{2,1,0:T(8,128)} %copy-done.2), custom_call_target="tpu_custom_call" | custom-call | tf_op jit(solution)/shard_map/pallas_call | solution.py:153
  19.2 11.4 %all_to_all.20.group_ref = f32[4,128,128]{2,1,0:T(8,128)} all-to-all(f32[4,128,128]{2,1,0:T(8,128)} %get-tuple-element.17), channel_id=1, replica_groups=mesh['clus0'=4,'clus1'=4,'clus2'=4,'clus3'=4,'samp'=2] {'clus3'}, dimensions={0} | all-to-all | bytes 524288 | tf_op jit(solution)/shard_map/all_to_all | solution.py:196
  30.6 7.1 %shard_map.67 = (f32[1,256,128]{2,1,0:T(8,128)}, f32[4,128,128]{2,1,0:T(8,128)}) custom-call(f32[4,128,128]{2,1,0:T(8,128)} %all_to_all.20.group_ref), custom_call_target="tpu_custom_call" | custom-call | tf_op jit(solution)/shard_map/pallas_call | solution.py:169
  37.7 16.7 %all_to_all.21.group_ref = f32[4,128,128]{2,1,0:T(8,128)} all-to-all(f32[4,128,128]{2,1,0:T(8,128)} %get-tuple-element.18), channel_id=1, replica_groups=mesh['clus0'=4,'clus1'=4,'clus2'=4,'clus3'=4,'samp'=2] {'clus2'}, dimensions={0} | all-to-all | bytes 524288 | tf_op jit(solution)/shard_map/all_to_all | solution.py:196
  54.4 7.2 %shard_map.68 = (f32[1,256,128]{2,1,0:T(8,128)}, f32[4,128,128]{2,1,0:T(8,128)}) custom-call(f32[4,128,128]{2,1,0:T(8,128)} %all_to_all.21.group_ref, f32[1,256,128]{2,1,0:T(8,128)} %get-tuple-element.19.refs_0_), custom_call_target="tpu_custom_call" | custom-call | tf_op jit(solution)/shard_map/pallas_call | solution.py:169
  61.6 15.4 %all_to_all.22.group_ref = f32[4,128,128]{2,1,0:T(8,128)} all-to-all(f32[4,128,128]{2,1,0:T(8,128)} %get-tuple-element.20), channel_id=1, replica_groups=mesh['clus0'=4,'clus1'=4,'clus2'=4,'clus3'=4,'samp'=2] {'clus1'}, dimensions={0} | all-to-all | bytes 524288 | tf_op jit(solution)/shard_map/all_to_all | solution.py:196
  77.0 7.2 %shard_map.69 = (f32[1,256,128]{2,1,0:T(8,128)}, f32[4,128,128]{2,1,0:T(8,128)}) custom-call(f32[4,128,128]{2,1,0:T(8,128)} %all_to_all.22.group_ref, f32[1,256,128]{2,1,0:T(8,128)} %get-tuple-element.21.refs_0_), custom_call_target="tpu_custom_call" | custom-call | tf_op jit(solution)/shard_map/pallas_call | solution.py:169
  84.2 17.5 %all_to_all.23.group_ref = f32[4,128,128]{2,1,0:T(8,128)} all-to-all(f32[4,128,128]{2,1,0:T(8,128)} %get-tuple-element.22), channel_id=1, replica_groups=mesh['clus0'=4,'clus1'=4,'clus2'=4,'clus3'=4,'samp'=2] {'clus0'}, dimensions={0} | all-to-all | bytes 524288 | tf_op jit(solution)/shard_map/all_to_all | solution.py:196
  101.7 7.2 %shard_map.70 = (f32[1,256,128]{2,1,0:T(8,128)}, f32[1,128,128]{2,1,0:T(8,128)}) custom-call(f32[4,128,128]{2,1,0:T(8,128)} %all_to_all.23.group_ref, f32[1,256,128]{2,1,0:T(8,128)} %get-tuple-element.23.refs_0_), custom_call_target="tpu_custom_call" | custom-call | tf_op jit(solution)/shard_map/pallas_call | solution.py:169
Async XLA Ops:
  0.6 1.0 copy-start
  3.1 3.8 %copy-start.1 = (f32[1024,128]{1,0:T(8,128)}, f32[1024,128]{1,0:T(8,128)S(1)}, u32[]{:S(2)}) copy-start(f32[1024,128]{1,0:T(8,128)S(1)} %fusion) | copy-start | bytes 1572868
  3.1 3.8 %collective-permute-start = (f32[4,256,128]{2,1,0:T(8,128)S(1)}, f32[4,256,128]{2,1,0:T(8,128)S(1)}, u32[]{:S(2)}, u32[]{:S(2)}) collective-permute-start(f32[4,256,128]{2,1,0:T(8,128)S(1)} %bitcast.5), channel_id=1, source_target_pairs={{0,1},{1,0},{2,3},{3,2},{4,5},{5,4},{6,7},{7,6},{8,9},{9,8},{10,11... | collective-permute-start | bytes 1572872 | tf_op jit(solution)/shard_map/ppermute | solution.py:20
  6.9 0.8 copy-start.2

commit v7 on v6

--- a/solution.py
+++ b/solution.py
@@ -21,7 +21,12 @@
 
 
 def mm(a, b):
-    return jnp.dot(a, b, precision=highest, preferred_element_type=jnp.float32)
+    a_high = a.astype(jnp.bfloat16)
+    a_low = (a - a_high.astype(jnp.float32)).astype(jnp.bfloat16)
+    b_high = b.astype(jnp.bfloat16)
+    b_low = (b - b_high.astype(jnp.float32)).astype(jnp.bfloat16)
+    dot = functools.partial(jnp.dot, preferred_element_type=jnp.float32)
+    return dot(a_high, b_high) + (dot(a_high, b_low) + dot(a_low, b_high))
 
 
 def gram(a):

time: 109 us -> 102 us (0.936)
  Pallas kernels: 40.1 us -> 33.1 us
    pallas_call x4, Pallas kernels: 28.6 us -> 24 us  [round_call(): pl.pallas_call(functools.partial(round_kernel, low_bit, axes), out_shape=...]
    pallas_call x1, Pallas kernels: 11.5 us -> 9.15 us  [local_call(): pl.pallas_call(local_kernel, out_shape=(jax.ShapeDtypeStruct((leaf_count,...]
where the time goes in v7:
time: 102 us
  blocking collectives  61 us (60%)
  Pallas kernels  33.1 us (32%)
  starting transfers between devices  1.92 us (2%)
  waiting for transfers between devices  1.88 us (2%)
  local copies, waits for them, and re-layouts  1.84 us (2%)
  matrix products  1.4 us (1%)
    all_to_all x4, blocking collectives, body(): group = lax.all_to_all(factors, name, 0, 0, tiled=True)  61 us
    pallas_call x4, Pallas kernels, round_call(): pl.pallas_call(functools.partial(round_kernel, low_bit, axes), out_shape=...  24 us
    pallas_call x1, Pallas kernels, local_call(): pl.pallas_call(local_kernel, out_shape=(jax.ShapeDtypeStruct((leaf_count,...  9.15 us
  transfers between devices with their start and end apart: 1, of which 1 were waited for; matrix products, arithmetic and copies ran while one was open for 0% of the time, Pallas kernels for 0%

profile of v7, /device:TPU:8, one launch (start us, length us, event | category | flops | bytes accessed | tf_op | source)
XLA Modules:
  0.0 101.8 jit_solution(15020854347633473451)
XLA Ops:
  0.6 0.0 copy-start
  0.6 1.0 %copy-done = f32[1024,128]{1,0:T(8,128)S(1)} copy-done((f32[1024,128]{1,0:T(8,128)S(1)}, f32[1024,128]{1,0:T(8,128)}, u32[]{:S(2)}) %copy-start) | copy-done | bytes 524312
  1.7 1.4 %fusion = f32[1024,128]{1,0:T(8,128)S(1)} fusion(f32[1024,128]{1,0:T(8,128)S(1)} %copy-done, f32[128,128]{1,0:T(8,128)} %param.4), kind=kOutput, calls=%fused_computation | convolution fusion | flops 201326592 | bytes 1114112 | tf_op jit(solution)/shard_map/dot_general | solution.py:193
  3.1 0.0 copy-start.1
  3.1 1.9 %collective-permute-start = (f32[4,256,128]{2,1,0:T(8,128)S(1)}, f32[4,256,128]{2,1,0:T(8,128)S(1)}, u32[]{:S(2)}, u32[]{:S(2)}) collective-permute-start(f32[4,256,128]{2,1,0:T(8,128)S(1)} %bitcast.5), channel_id=1, source_target_pairs={{0,1},{1,0},{2,3},{3,2},{4,5},{5,4},{6,7},{7,6},{8,9},{9,8},{10,11... | collective-permute-start | bytes 1572872 | tf_op jit(solution)/shard_map/ppermute | solution.py:20
  5.0 1.9 %collective-permute-done.other_ref = f32[4,256,128]{2,1,0:T(8,128)S(1)} collective-permute-done((f32[4,256,128]{2,1,0:T(8,128)S(1)}, f32[4,256,128]{2,1,0:T(8,128)S(1)}, u32[]{:S(2)}, u32[]{:S(2)}) %collective-permute-start) | collective-permute-done | bytes 524320 | tf_op jit(solution)/shard_map/ppermute | solution.py:20
  6.9 0.0 copy-done.1
  6.9 0.0 copy-start.2
  6.9 0.8 copy-done.2
  7.7 9.2 %shard_map.66 = (f32[4,256,128]{2,1,0:T(8,128)}, f32[3,256,128]{2,1,0:T(8,128)}, f32[4,128,128]{2,1,0:T(8,128)}) custom-call(s32[1,4]{1,0:T(1,128)} %slot_ref.1, f32[4,256,128]{2,1,0:T(8,128)} %bitcast.6, f32[4,256,128]{2,1,0:T(8,128)} %copy-done.2), custom_call_target="tpu_custom_call" | custom-call | tf_op jit(solution)/shard_map/pallas_call | solution.py:158
  16.9 11.4 %all_to_all.20.group_ref = f32[4,128,128]{2,1,0:T(8,128)} all-to-all(f32[4,128,128]{2,1,0:T(8,128)} %get-tuple-element.17), channel_id=1, replica_groups=mesh['clus0'=4,'clus1'=4,'clus2'=4,'clus3'=4,'samp'=2] {'clus3'}, dimensions={0} | all-to-all | bytes 524288 | tf_op jit(solution)/shard_map/all_to_all | solution.py:201
  28.2 6.0 %shard_map.67 = (f32[1,256,128]{2,1,0:T(8,128)}, f32[4,128,128]{2,1,0:T(8,128)}) custom-call(f32[4,128,128]{2,1,0:T(8,128)} %all_to_all.20.group_ref), custom_call_target="tpu_custom_call" | custom-call | tf_op jit(solution)/shard_map/pallas_call | solution.py:174
  34.2 16.7 %all_to_all.21.group_ref = f32[4,128,128]{2,1,0:T(8,128)} all-to-all(f32[4,128,128]{2,1,0:T(8,128)} %get-tuple-element.18), channel_id=1, replica_groups=mesh['clus0'=4,'clus1'=4,'clus2'=4,'clus3'=4,'samp'=2] {'clus2'}, dimensions={0} | all-to-all | bytes 524288 | tf_op jit(solution)/shard_map/all_to_all | solution.py:201
  50.9 6.0 %shard_map.68 = (f32[1,256,128]{2,1,0:T(8,128)}, f32[4,128,128]{2,1,0:T(8,128)}) custom-call(f32[4,128,128]{2,1,0:T(8,128)} %all_to_all.21.group_ref, f32[1,256,128]{2,1,0:T(8,128)} %get-tuple-element.19.refs_0_), custom_call_target="tpu_custom_call" | custom-call | tf_op jit(solution)/shard_map/pallas_call | solution.py:174
  56.9 15.4 %all_to_all.22.group_ref = f32[4,128,128]{2,1,0:T(8,128)} all-to-all(f32[4,128,128]{2,1,0:T(8,128)} %get-tuple-element.20), channel_id=1, replica_groups=mesh['clus0'=4,'clus1'=4,'clus2'=4,'clus3'=4,'samp'=2] {'clus1'}, dimensions={0} | all-to-all | bytes 524288 | tf_op jit(solution)/shard_map/all_to_all | solution.py:201
  72.4 6.0 %shard_map.69 = (f32[1,256,128]{2,1,0:T(8,128)}, f32[4,128,128]{2,1,0:T(8,128)}) custom-call(f32[4,128,128]{2,1,0:T(8,128)} %all_to_all.22.group_ref, f32[1,256,128]{2,1,0:T(8,128)} %get-tuple-element.21.refs_0_), custom_call_target="tpu_custom_call" | custom-call | tf_op jit(solution)/shard_map/pallas_call | solution.py:174
  78.4 17.4 %all_to_all.23.group_ref = f32[4,128,128]{2,1,0:T(8,128)} all-to-all(f32[4,128,128]{2,1,0:T(8,128)} %get-tuple-element.22), channel_id=1, replica_groups=mesh['clus0'=4,'clus1'=4,'clus2'=4,'clus3'=4,'samp'=2] {'clus0'}, dimensions={0} | all-to-all | bytes 524288 | tf_op jit(solution)/shard_map/all_to_all | solution.py:201
  95.8 6.0 %shard_map.70 = (f32[1,256,128]{2,1,0:T(8,128)}, f32[1,128,128]{2,1,0:T(8,128)}) custom-call(f32[4,128,128]{2,1,0:T(8,128)} %all_to_all.23.group_ref, f32[1,256,128]{2,1,0:T(8,128)} %get-tuple-element.23.refs_0_), custom_call_target="tpu_custom_call" | custom-call | tf_op jit(solution)/shard_map/pallas_call | solution.py:174
Async XLA Ops:
  0.6 1.0 %copy-start = (f32[1024,128]{1,0:T(8,128)S(1)}, f32[1024,128]{1,0:T(8,128)}, u32[]{:S(2)}) copy-start(f32[1024,128]{1,0:T(8,128)} %param.3) | copy-start | bytes 1572868
  3.1 3.8 %copy-start.1 = (f32[1024,128]{1,0:T(8,128)}, f32[1024,128]{1,0:T(8,128)S(1)}, u32[]{:S(2)}) copy-start(f32[1024,128]{1,0:T(8,128)S(1)} %fusion) | copy-start | bytes 1572868
  3.1 3.8 %collective-permute-start = (f32[4,256,128]{2,1,0:T(8,128)S(1)}, f32[4,256,128]{2,1,0:T(8,128)S(1)}, u32[]{:S(2)}, u32[]{:S(2)}) collective-permute-start(f32[4,256,128]{2,1,0:T(8,128)S(1)} %bitcast.5), channel_id=1, source_target_pairs={{0,1},{1,0},{2,3},{3,2},{4,5},{5,4},{6,7},{7,6},{8,9},{9,8},{10,11... | collective-permute-start | bytes 1572872 | tf_op jit(solution)/shard_map/ppermute | solution.py:20
  6.9 0.8 copy-start.2

commit v8 on v7

--- a/solution.py
+++ b/solution.py
@@ -8,7 +8,7 @@
 from jax.sharding import PartitionSpec as P
 
 NS_STEPS = 5
-ROUND_BITS = 2
+ROUND_BITS = 3
 
 
 highest = lax.Precision.HIGHEST

time: 102 us -> 99.6 us (0.976)
  blocking collectives: 61 us -> 58.3 us
    all_to_all x4 -> x3, blocking collectives: 61 us -> 58.3 us  [body(): group = lax.all_to_all(factors, name, 0, 0, tiled=True)]
    pallas_call x4 -> x3, Pallas kernels: 24 us -> 23.8 us  [round_call(): pl.pallas_call(functools.partial(round_kernel, low_bit, axes), out_shape=...]
where the time goes in v8:
time: 99.6 us; the launch traced here: 99 us
  blocking collectives  58.3 us (59%)
  Pallas kernels  33 us (33%)
  starting transfers between devices  1.92 us (2%)
  waiting for transfers between devices  1.88 us (2%)
  local copies, waits for them, and re-layouts  1.86 us (2%)
  matrix products  1.4 us (1%)
    all_to_all x3, blocking collectives, body(): group = lax.all_to_all(factors, name, 0, 0, tiled=True)  58.3 us
    pallas_call x3, Pallas kernels, round_call(): pl.pallas_call(functools.partial(round_kernel, low_bit, axes), out_shape=...  23.8 us
    pallas_call x1, Pallas kernels, local_call(): pl.pallas_call(local_kernel, out_shape=(jax.ShapeDtypeStruct((leaf_count,...  9.24 us
  transfers between devices with their start and end apart: 1, of which 1 were waited for; matrix products, arithmetic and copies ran while one was open for 0% of the time, Pallas kernels for 0%

profile of v8, /device:TPU:8, one launch (start us, length us, event | category | flops | bytes accessed | tf_op | source)
XLA Modules:
  0.0 99.0 jit_solution(10687766033503720052)
XLA Ops:
  0.6 0.0 copy-start
  0.6 1.0 %copy-done = f32[1024,128]{1,0:T(8,128)S(1)} copy-done((f32[1024,128]{1,0:T(8,128)S(1)}, f32[1024,128]{1,0:T(8,128)}, u32[]{:S(2)}) %copy-start) | copy-done | bytes 524312
  1.7 1.4 %fusion = f32[1024,128]{1,0:T(8,128)S(1)} fusion(f32[1024,128]{1,0:T(8,128)S(1)} %copy-done, f32[128,128]{1,0:T(8,128)} %param.4), kind=kOutput, calls=%fused_computation | convolution fusion | flops 201326592 | bytes 1114112 | tf_op jit(solution)/shard_map/dot_general | solution.py:193
  3.1 0.0 copy-start.1
  3.1 1.9 %collective-permute-start = (f32[4,256,128]{2,1,0:T(8,128)S(1)}, f32[4,256,128]{2,1,0:T(8,128)S(1)}, u32[]{:S(2)}, u32[]{:S(2)}) collective-permute-start(f32[4,256,128]{2,1,0:T(8,128)S(1)} %bitcast.5), channel_id=1, source_target_pairs={{0,1},{1,0},{2,3},{3,2},{4,5},{5,4},{6,7},{7,6},{8,9},{9,8},{10,11... | collective-permute-start | bytes 1572872 | tf_op jit(solution)/shard_map/ppermute | solution.py:20
  5.0 1.9 %collective-permute-done.other_ref = f32[4,256,128]{2,1,0:T(8,128)S(1)} collective-permute-done((f32[4,256,128]{2,1,0:T(8,128)S(1)}, f32[4,256,128]{2,1,0:T(8,128)S(1)}, u32[]{:S(2)}, u32[]{:S(2)}) %collective-permute-start) | collective-permute-done | bytes 524320 | tf_op jit(solution)/shard_map/ppermute | solution.py:20
  6.9 0.0 copy-done.1
  6.9 0.0 copy-start.2
  6.9 0.8 copy-done.2
  7.7 9.2 %shard_map.66 = (f32[4,256,128]{2,1,0:T(8,128)}, f32[3,256,128]{2,1,0:T(8,128)}, f32[8,128,128]{2,1,0:T(8,128)}) custom-call(s32[1,4]{1,0:T(1,128)} %slot_ref.1, f32[4,256,128]{2,1,0:T(8,128)} %bitcast.6, f32[4,256,128]{2,1,0:T(8,128)} %copy-done.2), custom_call_target="tpu_custom_call" | custom-call | tf_op jit(solution)/shard_map/pallas_call | solution.py:158
  17.0 19.2 %all_to_all.15.group_ref = f32[8,128,128]{2,1,0:T(8,128)} all-to-all(f32[8,128,128]{2,1,0:T(8,128)} %get-tuple-element.15), channel_id=1, replica_groups=mesh['clus0'=4,'clus1'=8,'clus2'=8,'samp'=2] {'clus2'}, dimensions={0} | all-to-all | bytes 1048576 | tf_op jit(solution)/shard_map/all_to_all | solution.py:201
  36.1 8.9 %shard_map.67 = (f32[1,256,128]{2,1,0:T(8,128)}, f32[8,128,128]{2,1,0:T(8,128)}) custom-call(f32[8,128,128]{2,1,0:T(8,128)} %all_to_all.15.group_ref), custom_call_target="tpu_custom_call" | custom-call | tf_op jit(solution)/shard_map/pallas_call | solution.py:174
  45.0 21.3 %all_to_all.16.group_ref = f32[8,128,128]{2,1,0:T(8,128)} all-to-all(f32[8,128,128]{2,1,0:T(8,128)} %get-tuple-element.16), channel_id=1, replica_groups=mesh['clus0'=4,'clus1'=8,'clus2'=8,'samp'=2] {'clus1'}, dimensions={0} | all-to-all | bytes 1048576 | tf_op jit(solution)/shard_map/all_to_all | solution.py:201
  66.3 8.9 %shard_map.68 = (f32[1,256,128]{2,1,0:T(8,128)}, f32[4,128,128]{2,1,0:T(8,128)}) custom-call(f32[8,128,128]{2,1,0:T(8,128)} %all_to_all.16.group_ref, f32[1,256,128]{2,1,0:T(8,128)} %get-tuple-element.17.refs_0_), custom_call_target="tpu_custom_call" | custom-call | tf_op jit(solution)/shard_map/pallas_call | solution.py:174
  75.2 17.8 %all_to_all.17.group_ref = f32[4,128,128]{2,1,0:T(8,128)} all-to-all(f32[4,128,128]{2,1,0:T(8,128)} %get-tuple-element.18), channel_id=1, replica_groups=mesh['clus0'=4,'clus1'=8,'clus2'=8,'samp'=2] {'clus0'}, dimensions={0} | all-to-all | bytes 524288 | tf_op jit(solution)/shard_map/all_to_all | solution.py:201
  93.0 6.0 %shard_map.69 = (f32[1,256,128]{2,1,0:T(8,128)}, f32[1,128,128]{2,1,0:T(8,128)}) custom-call(f32[4,128,128]{2,1,0:T(8,128)} %all_to_all.17.group_ref, f32[1,256,128]{2,1,0:T(8,128)} %get-tuple-element.19.refs_0_), custom_call_target="tpu_custom_call" | custom-call | tf_op jit(solution)/shard_map/pallas_call | solution.py:174
Async XLA Ops:
  0.6 1.0 %copy-start = (f32[1024,128]{1,0:T(8,128)S(1)}, f32[1024,128]{1,0:T(8,128)}, u32[]{:S(2)}) copy-start(f32[1024,128]{1,0:T(8,128)} %param.3) | copy-start | bytes 1572868
  3.1 3.8 %copy-start.1 = (f32[1024,128]{1,0:T(8,128)}, f32[1024,128]{1,0:T(8,128)S(1)}, u32[]{:S(2)}) copy-start(f32[1024,128]{1,0:T(8,128)S(1)} %fusion) | copy-start | bytes 1572868
  3.1 3.8 %collective-permute-start = (f32[4,256,128]{2,1,0:T(8,128)S(1)}, f32[4,256,128]{2,1,0:T(8,128)S(1)}, u32[]{:S(2)}, u32[]{:S(2)}) collective-permute-start(f32[4,256,128]{2,1,0:T(8,128)S(1)} %bitcast.5), channel_id=1, source_target_pairs={{0,1},{1,0},{2,3},{3,2},{4,5},{5,4},{6,7},{7,6},{8,9},{9,8},{10,11... | collective-permute-start | bytes 1572872 | tf_op jit(solution)/shard_map/ppermute | solution.py:20
  6.9 0.8 copy-start.2

commit v9 on v8

--- a/solution.py
+++ b/solution.py
@@ -30,7 +30,11 @@
 
 
 def gram(a):
-    return lax.dot_general(a, a, (((0,), (0,)), ((), ())), precision=highest, preferred_element_type=jnp.float32)
+    high = a.astype(jnp.bfloat16)
+    low = (a - high.astype(jnp.float32)).astype(jnp.bfloat16)
+    dims = (((0,), (0,)), ((), ()))
+    dot = functools.partial(lax.dot_general, dimension_numbers=dims, preferred_element_type=jnp.float32)
+    return dot(high, high) + (dot(high, low) + dot(low, high))
 
 
 def factor_nodes(nodes, keep_inverse=False):

time: 99.6 us -> 97.9 us (0.983)
  Pallas kernels: 33 us -> 31.4 us
    pallas_call x3, Pallas kernels: 23.8 us -> 22.6 us  [round_call(): pl.pallas_call(functools.partial(round_kernel, low_bit, axes), out_shape=...]
where the time goes in v9:
time: 97.9 us; the launch traced here: 97.3 us
  blocking collectives  58.2 us (59%)
  Pallas kernels  31.4 us (32%)
  starting transfers between devices  1.92 us (2%)
  waiting for transfers between devices  1.88 us (2%)
  local copies, waits for them, and re-layouts  1.86 us (2%)
  matrix products  1.4 us (1%)
    all_to_all x3, blocking collectives, body(): group = lax.all_to_all(factors, name, 0, 0, tiled=True)  58.2 us
    pallas_call x3, Pallas kernels, round_call(): pl.pallas_call(functools.partial(round_kernel, low_bit, axes), out_shape=...  22.6 us
    pallas_call x1, Pallas kernels, local_call(): pl.pallas_call(local_kernel, out_shape=(jax.ShapeDtypeStruct((leaf_count,...  8.7 us
  transfers between devices with their start and end apart: 1, of which 1 were waited for; matrix products, arithmetic and copies ran while one was open for 0% of the time, Pallas kernels for 0%

profile of v9, /device:TPU:8, one launch (start us, length us, event | category | flops | bytes accessed | tf_op | source)
XLA Modules:
  0.0 97.3 jit_solution(806128245951094322)
XLA Ops:
  0.6 0.0 copy-start
  0.6 1.0 %copy-done = f32[1024,128]{1,0:T(8,128)S(1)} copy-done((f32[1024,128]{1,0:T(8,128)S(1)}, f32[1024,128]{1,0:T(8,128)}, u32[]{:S(2)}) %copy-start) | copy-done | bytes 524312
  1.7 1.4 %fusion = f32[1024,128]{1,0:T(8,128)S(1)} fusion(f32[1024,128]{1,0:T(8,128)S(1)} %copy-done, f32[128,128]{1,0:T(8,128)} %param.4), kind=kOutput, calls=%fused_computation | convolution fusion | flops 201326592 | bytes 1114112 | tf_op jit(solution)/shard_map/dot_general | solution.py:197
  3.1 0.0 copy-start.1
  3.1 1.9 %collective-permute-start = (f32[4,256,128]{2,1,0:T(8,128)S(1)}, f32[4,256,128]{2,1,0:T(8,128)S(1)}, u32[]{:S(2)}, u32[]{:S(2)}) collective-permute-start(f32[4,256,128]{2,1,0:T(8,128)S(1)} %bitcast.5), channel_id=1, source_target_pairs={{0,1},{1,0},{2,3},{3,2},{4,5},{5,4},{6,7},{7,6},{8,9},{9,8},{10,11... | collective-permute-start | bytes 1572872 | tf_op jit(solution)/shard_map/ppermute | solution.py:20
  5.0 1.9 %collective-permute-done.other_ref = f32[4,256,128]{2,1,0:T(8,128)S(1)} collective-permute-done((f32[4,256,128]{2,1,0:T(8,128)S(1)}, f32[4,256,128]{2,1,0:T(8,128)S(1)}, u32[]{:S(2)}, u32[]{:S(2)}) %collective-permute-start) | collective-permute-done | bytes 524320 | tf_op jit(solution)/shard_map/ppermute | solution.py:20
  6.9 0.0 copy-done.1
  6.9 0.0 copy-start.2
  6.9 0.8 copy-done.2
  7.7 8.7 %shard_map.66 = (f32[4,256,128]{2,1,0:T(8,128)}, f32[3,256,128]{2,1,0:T(8,128)}, f32[8,128,128]{2,1,0:T(8,128)}) custom-call(s32[1,4]{1,0:T(1,128)} %slot_ref.1, f32[4,256,128]{2,1,0:T(8,128)} %bitcast.6, f32[4,256,128]{2,1,0:T(8,128)} %copy-done.2), custom_call_target="tpu_custom_call" | custom-call | tf_op jit(solution)/shard_map/pallas_call | solution.py:162
  16.4 19.2 %all_to_all.15.group_ref = f32[8,128,128]{2,1,0:T(8,128)} all-to-all(f32[8,128,128]{2,1,0:T(8,128)} %get-tuple-element.15), channel_id=1, replica_groups=mesh['clus0'=4,'clus1'=8,'clus2'=8,'samp'=2] {'clus2'}, dimensions={0} | all-to-all | bytes 1048576 | tf_op jit(solution)/shard_map/all_to_all | solution.py:205
  35.6 8.4 %shard_map.67 = (f32[1,256,128]{2,1,0:T(8,128)}, f32[8,128,128]{2,1,0:T(8,128)}) custom-call(f32[8,128,128]{2,1,0:T(8,128)} %all_to_all.15.group_ref), custom_call_target="tpu_custom_call" | custom-call | tf_op jit(solution)/shard_map/pallas_call | solution.py:178
  44.0 21.3 %all_to_all.16.group_ref = f32[8,128,128]{2,1,0:T(8,128)} all-to-all(f32[8,128,128]{2,1,0:T(8,128)} %get-tuple-element.16), channel_id=1, replica_groups=mesh['clus0'=4,'clus1'=8,'clus2'=8,'samp'=2] {'clus1'}, dimensions={0} | all-to-all | bytes 1048576 | tf_op jit(solution)/shard_map/all_to_all | solution.py:205
  65.3 8.4 %shard_map.68 = (f32[1,256,128]{2,1,0:T(8,128)}, f32[4,128,128]{2,1,0:T(8,128)}) custom-call(f32[8,128,128]{2,1,0:T(8,128)} %all_to_all.16.group_ref, f32[1,256,128]{2,1,0:T(8,128)} %get-tuple-element.17.refs_0_), custom_call_target="tpu_custom_call" | custom-call | tf_op jit(solution)/shard_map/pallas_call | solution.py:178
  73.7 17.8 %all_to_all.17.group_ref = f32[4,128,128]{2,1,0:T(8,128)} all-to-all(f32[4,128,128]{2,1,0:T(8,128)} %get-tuple-element.18), channel_id=1, replica_groups=mesh['clus0'=4,'clus1'=8,'clus2'=8,'samp'=2] {'clus0'}, dimensions={0} | all-to-all | bytes 524288 | tf_op jit(solution)/shard_map/all_to_all | solution.py:205
  91.5 5.8 %shard_map.69 = (f32[1,256,128]{2,1,0:T(8,128)}, f32[1,128,128]{2,1,0:T(8,128)}) custom-call(f32[4,128,128]{2,1,0:T(8,128)} %all_to_all.17.group_ref, f32[1,256,128]{2,1,0:T(8,128)} %get-tuple-element.19.refs_0_), custom_call_target="tpu_custom_call" | custom-call | tf_op jit(solution)/shard_map/pallas_call | solution.py:178
Async XLA Ops:
  0.6 1.0 %copy-start = (f32[1024,128]{1,0:T(8,128)S(1)}, f32[1024,128]{1,0:T(8,128)}, u32[]{:S(2)}) copy-start(f32[1024,128]{1,0:T(8,128)} %param.3) | copy-start | bytes 1572868
  3.1 3.8 %copy-start.1 = (f32[1024,128]{1,0:T(8,128)}, f32[1024,128]{1,0:T(8,128)S(1)}, u32[]{:S(2)}) copy-start(f32[1024,128]{1,0:T(8,128)S(1)} %fusion) | copy-start | bytes 1572868
  3.1 3.8 %collective-permute-start = (f32[4,256,128]{2,1,0:T(8,128)S(1)}, f32[4,256,128]{2,1,0:T(8,128)S(1)}, u32[]{:S(2)}, u32[]{:S(2)}) collective-permute-start(f32[4,256,128]{2,1,0:T(8,128)S(1)} %bitcast.5), channel_id=1, source_target_pairs={{0,1},{1,0},{2,3},{3,2},{4,5},{5,4},{6,7},{7,6},{8,9},{9,8},{10,11... | collective-permute-start | bytes 1572872 | tf_op jit(solution)/shard_map/ppermute | solution.py:20
  6.9 0.8 copy-start.2

commit v10 on v9

--- a/solution.py
+++ b/solution.py
@@ -194,7 +194,7 @@
 def body(axes, samples, sketch, leaf_slot):
     columns = sketch.shape[1]
     leaf_count = leaf_slot.shape[1]
-    partial_value = jnp.dot(samples, sketch, precision=highest).reshape(leaf_count, -1, columns)
+    partial_value = jnp.dot(samples, sketch, precision=lax.Precision.HIGH).reshape(leaf_count, -1, columns)
     other_value = from_xor(partial_value, "samp", 1)
     order = list(reversed(axes))
     sizes = [lax.axis_size(name) for name in order] + [1]

time: 97.9 us -> 97.8 us (level)
  no operation moved by 1% of the time
where the time goes in v10:
time: 97.8 us; the launch traced here: 97.2 us
  blocking collectives  58.3 us (60%)
  Pallas kernels  31.3 us (32%)
  starting transfers between devices  1.92 us (2%)
  waiting for transfers between devices  1.88 us (2%)
  local copies, waits for them, and re-layouts  1.86 us (2%)
  matrix products  1.2 us (1%)
    all_to_all x3, blocking collectives, body(): group = lax.all_to_all(factors, name, 0, 0, tiled=True)  58.3 us
    pallas_call x3, Pallas kernels, round_call(): pl.pallas_call(functools.partial(round_kernel, low_bit, axes), out_shape=...  22.6 us
    pallas_call x1, Pallas kernels, local_call(): pl.pallas_call(local_kernel, out_shape=(jax.ShapeDtypeStruct((leaf_count,...  8.7 us
  transfers between devices with their start and end apart: 1, of which 1 were waited for; matrix products, arithmetic and copies ran while one was open for 0% of the time, Pallas kernels for 0%

profile of v10, /device:TPU:8, one launch (start us, length us, event | category | flops | bytes accessed | tf_op | source)
XLA Modules:
  0.0 97.2 jit_solution(7648647862510558822)
XLA Ops:
  0.6 0.0 copy-start
  0.6 1.0 %copy-done = f32[1024,128]{1,0:T(8,128)S(1)} copy-done((f32[1024,128]{1,0:T(8,128)S(1)}, f32[1024,128]{1,0:T(8,128)}, u32[]{:S(2)}) %copy-start) | copy-done | bytes 524312
  1.7 1.2 %fusion = f32[1024,128]{1,0:T(8,128)S(1)} fusion(f32[1024,128]{1,0:T(8,128)S(1)} %copy-done, f32[128,128]{1,0:T(8,128)} %param.4), kind=kOutput, calls=%fused_computation | convolution fusion | flops 100663296 | bytes 1114112 | tf_op jit(solution)/shard_map/dot_general | solution.py:197
  2.9 0.0 copy-start.1
  2.9 1.9 %collective-permute-start = (f32[4,256,128]{2,1,0:T(8,128)S(1)}, f32[4,256,128]{2,1,0:T(8,128)S(1)}, u32[]{:S(2)}, u32[]{:S(2)}) collective-permute-start(f32[4,256,128]{2,1,0:T(8,128)S(1)} %bitcast.5), channel_id=1, source_target_pairs={{0,1},{1,0},{2,3},{3,2},{4,5},{5,4},{6,7},{7,6},{8,9},{9,8},{10,11... | collective-permute-start | bytes 1572872 | tf_op jit(solution)/shard_map/ppermute | solution.py:20
  4.8 1.9 %collective-permute-done.other_ref = f32[4,256,128]{2,1,0:T(8,128)S(1)} collective-permute-done((f32[4,256,128]{2,1,0:T(8,128)S(1)}, f32[4,256,128]{2,1,0:T(8,128)S(1)}, u32[]{:S(2)}, u32[]{:S(2)}) %collective-permute-start) | collective-permute-done | bytes 524320 | tf_op jit(solution)/shard_map/ppermute | solution.py:20
  6.7 0.0 copy-done.1
  6.7 0.0 copy-start.2
  6.7 0.8 copy-done.2
  7.5 8.7 %shard_map.66 = (f32[4,256,128]{2,1,0:T(8,128)}, f32[3,256,128]{2,1,0:T(8,128)}, f32[8,128,128]{2,1,0:T(8,128)}) custom-call(s32[1,4]{1,0:T(1,128)} %slot_ref.1, f32[4,256,128]{2,1,0:T(8,128)} %bitcast.6, f32[4,256,128]{2,1,0:T(8,128)} %copy-done.2), custom_call_target="tpu_custom_call" | custom-call | tf_op jit(solution)/shard_map/pallas_call | solution.py:162
  16.2 19.2 %all_to_all.15.group_ref = f32[8,128,128]{2,1,0:T(8,128)} all-to-all(f32[8,128,128]{2,1,0:T(8,128)} %get-tuple-element.15), channel_id=1, replica_groups=mesh['clus0'=4,'clus1'=8,'clus2'=8,'samp'=2] {'clus2'}, dimensions={0} | all-to-all | bytes 1048576 | tf_op jit(solution)/shard_map/all_to_all | solution.py:205
  35.4 8.4 %shard_map.67 = (f32[1,256,128]{2,1,0:T(8,128)}, f32[8,128,128]{2,1,0:T(8,128)}) custom-call(f32[8,128,128]{2,1,0:T(8,128)} %all_to_all.15.group_ref), custom_call_target="tpu_custom_call" | custom-call | tf_op jit(solution)/shard_map/pallas_call | solution.py:178
  43.8 21.3 %all_to_all.16.group_ref = f32[8,128,128]{2,1,0:T(8,128)} all-to-all(f32[8,128,128]{2,1,0:T(8,128)} %get-tuple-element.16), channel_id=1, replica_groups=mesh['clus0'=4,'clus1'=8,'clus2'=8,'samp'=2] {'clus1'}, dimensions={0} | all-to-all | bytes 1048576 | tf_op jit(solution)/shard_map/all_to_all | solution.py:205
  65.1 8.4 %shard_map.68 = (f32[1,256,128]{2,1,0:T(8,128)}, f32[4,128,128]{2,1,0:T(8,128)}) custom-call(f32[8,128,128]{2,1,0:T(8,128)} %all_to_all.16.group_ref, f32[1,256,128]{2,1,0:T(8,128)} %get-tuple-element.17.refs_0_), custom_call_target="tpu_custom_call" | custom-call | tf_op jit(solution)/shard_map/pallas_call | solution.py:178
  73.5 17.9 %all_to_all.17.group_ref = f32[4,128,128]{2,1,0:T(8,128)} all-to-all(f32[4,128,128]{2,1,0:T(8,128)} %get-tuple-element.18), channel_id=1, replica_groups=mesh['clus0'=4,'clus1'=8,'clus2'=8,'samp'=2] {'clus0'}, dimensions={0} | all-to-all | bytes 524288 | tf_op jit(solution)/shard_map/all_to_all | solution.py:205
  91.4 5.8 %shard_map.69 = (f32[1,256,128]{2,1,0:T(8,128)}, f32[1,128,128]{2,1,0:T(8,128)}) custom-call(f32[4,128,128]{2,1,0:T(8,128)} %all_to_all.17.group_ref, f32[1,256,128]{2,1,0:T(8,128)} %get-tuple-element.19.refs_0_), custom_call_target="tpu_custom_call" | custom-call | tf_op jit(solution)/shard_map/pallas_call | solution.py:178
Async XLA Ops:
  0.6 1.0 %copy-start = (f32[1024,128]{1,0:T(8,128)S(1)}, f32[1024,128]{1,0:T(8,128)}, u32[]{:S(2)}) copy-start(f32[1024,128]{1,0:T(8,128)} %param.3) | copy-start | bytes 1572868
  2.9 3.8 %copy-start.1 = (f32[1024,128]{1,0:T(8,128)}, f32[1024,128]{1,0:T(8,128)S(1)}, u32[]{:S(2)}) copy-start(f32[1024,128]{1,0:T(8,128)S(1)} %fusion) | copy-start | bytes 1572868
  2.9 3.8 %collective-permute-start = (f32[4,256,128]{2,1,0:T(8,128)S(1)}, f32[4,256,128]{2,1,0:T(8,128)S(1)}, u32[]{:S(2)}, u32[]{:S(2)}) collective-permute-start(f32[4,256,128]{2,1,0:T(8,128)S(1)} %bitcast.5), channel_id=1, source_target_pairs={{0,1},{1,0},{2,3},{3,2},{4,5},{5,4},{6,7},{7,6},{8,9},{9,8},{10,11... | collective-permute-start | bytes 1572872 | tf_op jit(solution)/shard_map/ppermute | solution.py:20
  6.7 0.8 copy-start.2

commit v11 on v10

--- a/solution.py
+++ b/solution.py
@@ -59,20 +59,27 @@
     middles = [1.5 * identity - 0.5 * y for y in roots]
     roots = [mm(y, m) for y, m in zip(roots, middles)]
     inverses = middles
-    for _ in range(NS_STEPS - 1):
+    finals = [None for _ in nodes]
+    for step in range(NS_STEPS - 1):
         middles = [1.5 * identity - 0.5 * mm(w, y) for w, y in zip(inverses, roots)]
-        roots, inverses = (
-            [mm(y, m) for y, m in zip(roots, middles)],
-            [mm(m, w) for m, w in zip(middles, inverses)],
-        )
+        roots = [mm(y, m) for y, m in zip(roots, middles)]
+        if step < NS_STEPS - 2:
+            inverses = [mm(m, w) for m, w in zip(middles, inverses)]
+        else:
+            finals = middles
     results = []
-    for parts, c, y, w in zip(nodes, scales, roots, inverses):
+    for parts, c, y, w, last in zip(nodes, scales, roots, inverses, finals):
         s = jnp.sqrt(c)
         if keep_inverse:
-            results.append((w, y * s, s))
+            results.append((w, y * s, s, last))
         else:
-            results.append(([mm(part, w) / s for part in parts], y * s))
+            results.append(([apply_inverse(part, w, last) / s for part in parts], y * s))
     return results
+
+
+def apply_inverse(part, inverse, last):
+    product = mm(part, inverse)
+    return product if last is None else mm(product, last)
 
 
 def pair_levels(factors, levels, store):
@@ -139,18 +146,23 @@
         nodes = [[factors[2 * i], factors[2 * i + 1]] for i in range(len(factors) // 2)]
         results = factor_nodes(nodes, keep_inverse=True)
         node = member >> (level + 1)
-        mine_low, mine_high, mine_inverse, mine_scale = nodes[0][0], nodes[0][1], results[0][0], results[0][2]
+        mine_low, mine_high, mine_inverse, mine_scale, mine_last = nodes[0][0], nodes[0][1], results[0][0], results[0][2], results[0][3]
         for i in range(1, len(nodes)):
             pick = node == i
             mine_low = jnp.where(pick, nodes[i][0], mine_low)
             mine_high = jnp.where(pick, nodes[i][1], mine_high)
             mine_inverse = jnp.where(pick, results[i][0], mine_inverse)
             mine_scale = jnp.where(pick, results[i][2], mine_scale)
+            if mine_last is not None:
+                mine_last = jnp.where(pick, results[i][3], mine_last)
         level_bit = low_bit + level
         owned = position % (2 << level_bit) == 1 << level_bit
-        transfer = jnp.concatenate([mm(mine_low, mine_inverse) / mine_scale, mm(mine_high, mine_inverse) / mine_scale], axis=0)
+        transfer = jnp.concatenate(
+            [apply_inverse(mine_low, mine_inverse, mine_last) / mine_scale, apply_inverse(mine_high, mine_inverse, mine_last) / mine_scale],
+            axis=0,
+        )
         top = jnp.where(owned, transfer, top)
-        factors = [r for _, r, _ in results]
+        factors = [r for _, r, _, _ in results]
     top_ref[0] = top
     for p in range(next_ref.shape[0]):
         next_ref[p] = factors[0]

time: 97.8 us -> 96.7 us (0.989)
  Pallas kernels: 31.3 us -> 30.3 us
    pallas_call x3, Pallas kernels: 22.6 us -> 21.6 us  [round_call(): pl.pallas_call(functools.partial(round_kernel, low_bit, axes), out_shape=...]
where the time goes in v11:
time: 96.7 us; the launch traced here: 96.1 us
  blocking collectives  58.3 us (60%)
  Pallas kernels  30.3 us (31%)
  starting transfers between devices  1.92 us (2%)
  waiting for transfers between devices  1.88 us (2%)
  local copies, waits for them, and re-layouts  1.86 us (2%)
  matrix products  1.2 us (1%)
    all_to_all x3, blocking collectives, body(): group = lax.all_to_all(factors, name, 0, 0, tiled=True)  58.3 us
    pallas_call x3, Pallas kernels, round_call(): pl.pallas_call(functools.partial(round_kernel, low_bit, axes), out_shape=...  21.6 us
    pallas_call x1, Pallas kernels, local_call(): pl.pallas_call(local_kernel, out_shape=(jax.ShapeDtypeStruct((leaf_count,...  8.68 us
  transfers between devices with their start and end apart: 1, of which 1 were waited for; matrix products, arithmetic and copies ran while one was open for 0% of the time, Pallas kernels for 0%

profile of v11, /device:TPU:8, one launch (start us, length us, event | category | flops | bytes accessed | tf_op | source)
XLA Modules:
  0.0 96.1 jit_solution(6306857560787991659)
XLA Ops:
  0.6 0.0 copy-start
  0.6 1.0 %copy-done = f32[1024,128]{1,0:T(8,128)S(1)} copy-done((f32[1024,128]{1,0:T(8,128)S(1)}, f32[1024,128]{1,0:T(8,128)}, u32[]{:S(2)}) %copy-start) | copy-done | bytes 524312
  1.7 1.2 %fusion = f32[1024,128]{1,0:T(8,128)S(1)} fusion(f32[1024,128]{1,0:T(8,128)S(1)} %copy-done, f32[128,128]{1,0:T(8,128)} %param.4), kind=kOutput, calls=%fused_computation | convolution fusion | flops 100663296 | bytes 1114112 | tf_op jit(solution)/shard_map/dot_general | solution.py:209
  2.9 0.0 copy-start.1
  2.9 1.9 %collective-permute-start = (f32[4,256,128]{2,1,0:T(8,128)S(1)}, f32[4,256,128]{2,1,0:T(8,128)S(1)}, u32[]{:S(2)}, u32[]{:S(2)}) collective-permute-start(f32[4,256,128]{2,1,0:T(8,128)S(1)} %bitcast.5), channel_id=1, source_target_pairs={{0,1},{1,0},{2,3},{3,2},{4,5},{5,4},{6,7},{7,6},{8,9},{9,8},{10,11... | collective-permute-start | bytes 1572872 | tf_op jit(solution)/shard_map/ppermute | solution.py:20
  4.8 1.9 %collective-permute-done.other_ref = f32[4,256,128]{2,1,0:T(8,128)S(1)} collective-permute-done((f32[4,256,128]{2,1,0:T(8,128)S(1)}, f32[4,256,128]{2,1,0:T(8,128)S(1)}, u32[]{:S(2)}, u32[]{:S(2)}) %collective-permute-start) | collective-permute-done | bytes 524320 | tf_op jit(solution)/shard_map/ppermute | solution.py:20
  6.7 0.0 copy-done.1
  6.7 0.0 copy-start.2
  6.7 0.8 copy-done.2
  7.5 8.7 %shard_map.66 = (f32[4,256,128]{2,1,0:T(8,128)}, f32[3,256,128]{2,1,0:T(8,128)}, f32[8,128,128]{2,1,0:T(8,128)}) custom-call(s32[1,4]{1,0:T(1,128)} %slot_ref.1, f32[4,256,128]{2,1,0:T(8,128)} %bitcast.6, f32[4,256,128]{2,1,0:T(8,128)} %copy-done.2), custom_call_target="tpu_custom_call" | custom-call | tf_op jit(solution)/shard_map/pallas_call | solution.py:174
  16.2 19.2 %all_to_all.15.group_ref = f32[8,128,128]{2,1,0:T(8,128)} all-to-all(f32[8,128,128]{2,1,0:T(8,128)} %get-tuple-element.15), channel_id=1, replica_groups=mesh['clus0'=4,'clus1'=8,'clus2'=8,'samp'=2] {'clus2'}, dimensions={0} | all-to-all | bytes 1048576 | tf_op jit(solution)/shard_map/all_to_all | solution.py:217
  35.3 8.0 %shard_map.67 = (f32[1,256,128]{2,1,0:T(8,128)}, f32[8,128,128]{2,1,0:T(8,128)}) custom-call(f32[8,128,128]{2,1,0:T(8,128)} %all_to_all.15.group_ref), custom_call_target="tpu_custom_call" | custom-call | tf_op jit(solution)/shard_map/pallas_call | solution.py:190
  43.4 21.3 %all_to_all.16.group_ref = f32[8,128,128]{2,1,0:T(8,128)} all-to-all(f32[8,128,128]{2,1,0:T(8,128)} %get-tuple-element.16), channel_id=1, replica_groups=mesh['clus0'=4,'clus1'=8,'clus2'=8,'samp'=2] {'clus1'}, dimensions={0} | all-to-all | bytes 1048576 | tf_op jit(solution)/shard_map/all_to_all | solution.py:217
  64.6 8.0 %shard_map.68 = (f32[1,256,128]{2,1,0:T(8,128)}, f32[4,128,128]{2,1,0:T(8,128)}) custom-call(f32[8,128,128]{2,1,0:T(8,128)} %all_to_all.16.group_ref, f32[1,256,128]{2,1,0:T(8,128)} %get-tuple-element.17.refs_0_), custom_call_target="tpu_custom_call" | custom-call | tf_op jit(solution)/shard_map/pallas_call | solution.py:190
  72.6 17.9 %all_to_all.17.group_ref = f32[4,128,128]{2,1,0:T(8,128)} all-to-all(f32[4,128,128]{2,1,0:T(8,128)} %get-tuple-element.18), channel_id=1, replica_groups=mesh['clus0'=4,'clus1'=8,'clus2'=8,'samp'=2] {'clus0'}, dimensions={0} | all-to-all | bytes 524288 | tf_op jit(solution)/shard_map/all_to_all | solution.py:217
  90.5 5.6 %shard_map.69 = (f32[1,256,128]{2,1,0:T(8,128)}, f32[1,128,128]{2,1,0:T(8,128)}) custom-call(f32[4,128,128]{2,1,0:T(8,128)} %all_to_all.17.group_ref, f32[1,256,128]{2,1,0:T(8,128)} %get-tuple-element.19.refs_0_), custom_call_target="tpu_custom_call" | custom-call | tf_op jit(solution)/shard_map/pallas_call | solution.py:190
Async XLA Ops:
  0.6 1.0 %copy-start = (f32[1024,128]{1,0:T(8,128)S(1)}, f32[1024,128]{1,0:T(8,128)}, u32[]{:S(2)}) copy-start(f32[1024,128]{1,0:T(8,128)} %param.3) | copy-start | bytes 1572868
  2.9 3.8 %copy-start.1 = (f32[1024,128]{1,0:T(8,128)}, f32[1024,128]{1,0:T(8,128)S(1)}, u32[]{:S(2)}) copy-start(f32[1024,128]{1,0:T(8,128)S(1)} %fusion) | copy-start | bytes 1572868
  2.9 3.8 %collective-permute-start = (f32[4,256,128]{2,1,0:T(8,128)S(1)}, f32[4,256,128]{2,1,0:T(8,128)S(1)}, u32[]{:S(2)}, u32[]{:S(2)}) collective-permute-start(f32[4,256,128]{2,1,0:T(8,128)S(1)} %bitcast.5), channel_id=1, source_target_pairs={{0,1},{1,0},{2,3},{3,2},{4,5},{5,4},{6,7},{7,6},{8,9},{9,8},{10,11... | collective-permute-start | bytes 1572872 | tf_op jit(solution)/shard_map/ppermute | solution.py:20
  6.7 0.8 copy-start.2

commit v12 on v11

--- a/solution.py
+++ b/solution.py
@@ -131,6 +131,7 @@
 
 
 def round_kernel(low_bit, axes, group_ref, *refs):
+    refs, (spread_ref, sem) = refs[:-2], refs[-2:]
     top_in_ref, top_ref, next_ref = refs if len(refs) == 3 else (None,) + refs
     members = group_ref.shape[0]
     levels = members.bit_length() - 1
@@ -145,6 +146,12 @@
     for level in range(levels):
         nodes = [[factors[2 * i], factors[2 * i + 1]] for i in range(len(factors) // 2)]
         results = factor_nodes(nodes, keep_inverse=True)
+        factors = [r for _, r, _, _ in results]
+        if level == levels - 1:
+            for p in range(spread_ref.shape[0]):
+                spread_ref[p] = factors[0]
+            send = pltpu.make_async_copy(spread_ref, next_ref, sem)
+            send.start()
         node = member >> (level + 1)
         mine_low, mine_high, mine_inverse, mine_scale, mine_last = nodes[0][0], nodes[0][1], results[0][0], results[0][2], results[0][3]
         for i in range(1, len(nodes)):
@@ -162,10 +169,8 @@
             axis=0,
         )
         top = jnp.where(owned, transfer, top)
-        factors = [r for _, r, _, _ in results]
     top_ref[0] = top
-    for p in range(next_ref.shape[0]):
-        next_ref[p] = factors[0]
+    send.wait()
 
 
 def local_call(leaf_slot, partial_value, other_value, spread):
@@ -194,7 +199,8 @@
             jax.ShapeDtypeStruct((spread, width, width), jnp.float32),
         ),
         in_specs=[pl.BlockSpec(memory_space=vmem) for _ in operands],
-        out_specs=(pl.BlockSpec(memory_space=vmem), pl.BlockSpec(memory_space=vmem)),
+        out_specs=(pl.BlockSpec(memory_space=vmem), pl.BlockSpec(memory_space=pl.ANY)),
+        scratch_shapes=[pltpu.VMEM((spread, width, width), jnp.float32), pltpu.SemaphoreType.DMA(())],
     )(*operands)
 
 

time: 96.7 us -> 98.7 us (1.021)
  Pallas kernels: 30.3 us -> 32.1 us
    pallas_call x3, Pallas kernels: 21.6 us -> 23.4 us  [round_call(): pl.pallas_call(functools.partial(round_kernel, low_bit, axes), out_shape=...]
where the time goes in v12:
time: 98.7 us; the launch traced here: 98.1 us
  blocking collectives  58.3 us (59%)
  Pallas kernels  32.1 us (33%)
  starting transfers between devices  1.92 us (2%)
  waiting for transfers between devices  1.88 us (2%)
  local copies, waits for them, and re-layouts  1.86 us (2%)
  matrix products  1.2 us (1%)
    all_to_all x3, blocking collectives, body(): group = lax.all_to_all(factors, name, 0, 0, tiled=True)  58.3 us
    pallas_call x3, Pallas kernels, round_call(): pl.pallas_call(functools.partial(round_kernel, low_bit, axes), out_shape=...  23.4 us
    pallas_call x1, Pallas kernels, local_call(): pl.pallas_call(local_kernel, out_shape=(jax.ShapeDtypeStruct((leaf_count,...  8.68 us
  transfers between devices with their start and end apart: 1, of which 1 were waited for; matrix products, arithmetic and copies ran while one was open for 0% of the time, Pallas kernels for 0%

profile of v12, /device:TPU:8, one launch (start us, length us, event | category | flops | bytes accessed | tf_op | source)
XLA Modules:
  0.0 98.1 jit_solution(6314913972421945064)
XLA Ops:
  0.6 0.0 copy-start
  0.6 1.0 %copy-done = f32[1024,128]{1,0:T(8,128)S(1)} copy-done((f32[1024,128]{1,0:T(8,128)S(1)}, f32[1024,128]{1,0:T(8,128)}, u32[]{:S(2)}) %copy-start) | copy-done | bytes 524312
  1.7 1.2 %fusion = f32[1024,128]{1,0:T(8,128)S(1)} fusion(f32[1024,128]{1,0:T(8,128)S(1)} %copy-done, f32[128,128]{1,0:T(8,128)} %param.4), kind=kOutput, calls=%fused_computation | convolution fusion | flops 100663296 | bytes 1114112 | tf_op jit(solution)/shard_map/dot_general | solution.py:215
  2.9 0.0 copy-start.1
  2.9 1.9 %collective-permute-start = (f32[4,256,128]{2,1,0:T(8,128)S(1)}, f32[4,256,128]{2,1,0:T(8,128)S(1)}, u32[]{:S(2)}, u32[]{:S(2)}) collective-permute-start(f32[4,256,128]{2,1,0:T(8,128)S(1)} %bitcast.5), channel_id=1, source_target_pairs={{0,1},{1,0},{2,3},{3,2},{4,5},{5,4},{6,7},{7,6},{8,9},{9,8},{10,11... | collective-permute-start | bytes 1572872 | tf_op jit(solution)/shard_map/ppermute | solution.py:20
  4.8 1.9 %collective-permute-done.other_ref = f32[4,256,128]{2,1,0:T(8,128)S(1)} collective-permute-done((f32[4,256,128]{2,1,0:T(8,128)S(1)}, f32[4,256,128]{2,1,0:T(8,128)S(1)}, u32[]{:S(2)}, u32[]{:S(2)}) %collective-permute-start) | collective-permute-done | bytes 524320 | tf_op jit(solution)/shard_map/ppermute | solution.py:20
  6.7 0.0 copy-done.1
  6.7 0.0 copy-start.2
  6.7 0.8 copy-done.2
  7.5 8.7 %shard_map.66 = (f32[4,256,128]{2,1,0:T(8,128)}, f32[3,256,128]{2,1,0:T(8,128)}, f32[8,128,128]{2,1,0:T(8,128)}) custom-call(s32[1,4]{1,0:T(1,128)} %slot_ref.1, f32[4,256,128]{2,1,0:T(8,128)} %bitcast.6, f32[4,256,128]{2,1,0:T(8,128)} %copy-done.2), custom_call_target="tpu_custom_call" | custom-call | tf_op jit(solution)/shard_map/pallas_call | solution.py:179
  16.2 19.2 %all_to_all.15.group_ref = f32[8,128,128]{2,1,0:T(8,128)} all-to-all(f32[8,128,128]{2,1,0:T(8,128)} %get-tuple-element.15), channel_id=1, replica_groups=mesh['clus0'=4,'clus1'=8,'clus2'=8,'samp'=2] {'clus2'}, dimensions={0} | all-to-all | bytes 1048576 | tf_op jit(solution)/shard_map/all_to_all | solution.py:223
  35.3 8.7 %shard_map.67 = (f32[1,256,128]{2,1,0:T(8,128)}, f32[8,128,128]{2,1,0:T(8,128)}) custom-call(f32[8,128,128]{2,1,0:T(8,128)} %all_to_all.15.group_ref), custom_call_target="tpu_custom_call" | custom-call | tf_op jit(solution)/shard_map/pallas_call | solution.py:195
  44.0 21.3 %all_to_all.16.group_ref = f32[8,128,128]{2,1,0:T(8,128)} all-to-all(f32[8,128,128]{2,1,0:T(8,128)} %get-tuple-element.16), channel_id=1, replica_groups=mesh['clus0'=4,'clus1'=8,'clus2'=8,'samp'=2] {'clus1'}, dimensions={0} | all-to-all | bytes 1048576 | tf_op jit(solution)/shard_map/all_to_all | solution.py:223
  65.3 8.6 %shard_map.68 = (f32[1,256,128]{2,1,0:T(8,128)}, f32[4,128,128]{2,1,0:T(8,128)}) custom-call(f32[8,128,128]{2,1,0:T(8,128)} %all_to_all.16.group_ref, f32[1,256,128]{2,1,0:T(8,128)} %get-tuple-element.17.refs_0_), custom_call_target="tpu_custom_call" | custom-call | tf_op jit(solution)/shard_map/pallas_call | solution.py:195
  73.9 17.9 %all_to_all.17.group_ref = f32[4,128,128]{2,1,0:T(8,128)} all-to-all(f32[4,128,128]{2,1,0:T(8,128)} %get-tuple-element.18), channel_id=1, replica_groups=mesh['clus0'=4,'clus1'=8,'clus2'=8,'samp'=2] {'clus0'}, dimensions={0} | all-to-all | bytes 524288 | tf_op jit(solution)/shard_map/all_to_all | solution.py:223
  91.8 6.2 %shard_map.69 = (f32[1,256,128]{2,1,0:T(8,128)}, f32[1,128,128]{2,1,0:T(8,128)}) custom-call(f32[4,128,128]{2,1,0:T(8,128)} %all_to_all.17.group_ref, f32[1,256,128]{2,1,0:T(8,128)} %get-tuple-element.19.refs_0_), custom_call_target="tpu_custom_call" | custom-call | tf_op jit(solution)/shard_map/pallas_call | solution.py:195
Async XLA Ops:
  0.6 1.0 %copy-start = (f32[1024,128]{1,0:T(8,128)S(1)}, f32[1024,128]{1,0:T(8,128)}, u32[]{:S(2)}) copy-start(f32[1024,128]{1,0:T(8,128)} %param.3) | copy-start | bytes 1572868
  2.9 3.8 %copy-start.1 = (f32[1024,128]{1,0:T(8,128)}, f32[1024,128]{1,0:T(8,128)S(1)}, u32[]{:S(2)}) copy-start(f32[1024,128]{1,0:T(8,128)S(1)} %fusion) | copy-start | bytes 1572868
  2.9 3.8 %collective-permute-start = (f32[4,256,128]{2,1,0:T(8,128)S(1)}, f32[4,256,128]{2,1,0:T(8,128)S(1)}, u32[]{:S(2)}, u32[]{:S(2)}) collective-permute-start(f32[4,256,128]{2,1,0:T(8,128)S(1)} %bitcast.5), channel_id=1, source_target_pairs={{0,1},{1,0},{2,3},{3,2},{4,5},{5,4},{6,7},{7,6},{8,9},{9,8},{10,11... | collective-permute-start | bytes 1572872 | tf_op jit(solution)/shard_map/ppermute | solution.py:20
  6.7 0.8 copy-start.2
